TPU v7x, 32 devices: a whole 2x2x4 slice. The times are simulated.
32 devices in a mesh: seq: 8 (over y, x, core), fsdp: 4 (over z).
Axes of the slice: x: 2, y: 2, z: 4, core: 2. Of those that a mesh axis runs over, the one named last changes fastest.
Arguments:
- tokens: bfloat16 [4, 4096, 3072], P('fsdp', 'seq'), may hold values from -6 to 6
- doc_ids: int32 [4, 4096], P('fsdp', 'seq'), may hold values from 0 to 15, never falling along the last dimension, each value on 1 to 1024 neighbouring positions
- norm_gain: float32 [3072], replicated, may hold values from 0.5 to 2
- query_weight: bfloat16 [3072, 1536], P(('seq', 'fsdp')), may hold values from -0.109375 to 0.109375
- key_weight: bfloat16 [3072, 1536], P(('seq', 'fsdp')), may hold values from -0.109375 to 0.109375
- value_weight: bfloat16 [3072, 1536], P(('seq', 'fsdp')), may hold values from -0.109375 to 0.109375
- out_gain: float32 [1536], replicated, may hold values from 0.5 to 2
Outputs:
- attended: bfloat16 [4, 4096, 1536], P('fsdp', 'seq')
Inputs may be any that keep to these rules, and one draw needn't show every extreme that they name: `doc_ids`: document numbers never fall along a stream, so every document is one run of consecutive tokens; every number below 16 is used in each stream, every run holds at most 1024 tokens, and one run holds exactly 1024.
All inputs are finite; a program needn't handle non-finite values.
Results may differ from a plain program's by a relative error of at most 0.0044.
Values may be sent and summed in bfloat16 or wider, within the bound.
No kernel may reach another device: no remote copies, remote signals or barrier semaphores. Data moves between devices by JAX's collectives and lax.ppermute only.
A program may use at most 128 MiB of HBM per device.

v0:
```python
import jax
import jax.numpy as jnp
from jax import lax
from jax.sharding import PartitionSpec as P

HEADS = 12
HEAD_DIM = 128
ATTN_WIDTH = 1536


EPS = 1e-06
BIG_DOC = 1073741824


def entering(value, axis, combine, identity):
    length, here = (lax.axis_size(axis), lax.axis_index(axis))
    everything = jax.tree.map(
        lambda part, kind: lax.all_gather(part.astype(kind), axis),
        value,
        jax.tree.map(lambda a: jnp.bfloat16 if a.dtype == jnp.float32 else a.dtype, value),
    )
    start = jax.tree.map(
        lambda part, zero: jnp.broadcast_to(jnp.asarray(zero, part.dtype), part.shape),
        value,
        identity,
    )

    def turn(k, before):
        reached = k < here
        new = combine(
            before, jax.tree.map(lambda part, own: part[k].astype(own.dtype), everything, value)
        )
        return jax.tree.map(lambda a, b: jnp.where(reached, a, b), new, before)

    return lax.fori_loop(0, length, turn, start)


def norm_rows(values, gain):
    mean_sq = jnp.mean(values * values, axis=-1, keepdims=True)
    return values * lax.rsqrt(mean_sq + EPS) * gain


def join_states(earlier, later):
    state_early, first_early, last_early = earlier
    state_late, first_late, last_late = later
    keep_state = (last_late < 0) | (last_early == first_late) & (first_late == last_late)
    merged = state_late + jnp.where(keep_state[:, None, None, None], state_early, 0.0)
    return (merged, jnp.minimum(first_early, first_late), jnp.maximum(last_early, last_late))


def start_summary(streams, heads):
    return (
        jnp.zeros((streams, heads, HEAD_DIM, HEAD_DIM), jnp.float32),
        jnp.full((streams,), BIG_DOC, jnp.int32),
        jnp.full((streams,), -1, jnp.int32),
    )


def block_summary(key_rows, value_rows, doc_rows):
    last_doc = doc_rows[:, -1]
    tail_keys = jnp.where(
        (doc_rows == last_doc[:, None])[:, :, None, None], key_rows, jnp.zeros_like(key_rows)
    )
    tail_state = jnp.einsum(
        "sjhe,sjhf->shef", tail_keys, value_rows, preferred_element_type=jnp.float32
    )
    return (tail_state, doc_rows[:, 0], last_doc)


def mix_block(query_rows, key_rows, value_rows, doc_rows, past_state, past_doc):
    count = doc_rows.shape[1]
    scores = jnp.einsum("sihe,sjhe->shij", query_rows, key_rows, preferred_element_type=jnp.float32)
    row_pos = lax.broadcasted_iota(jnp.int32, (count, count), 0)
    col_pos = lax.broadcasted_iota(jnp.int32, (count, count), 1)
    visible = (row_pos >= col_pos)[None] & (doc_rows[:, :, None] == doc_rows[:, None, :])
    weights = jnp.where(visible[:, None], scores, 0.0).astype(jnp.bfloat16)
    local_part = jnp.einsum(
        "shij,sjhe->sihe", weights, value_rows, preferred_element_type=jnp.float32
    )
    from_past = jnp.einsum(
        "sihe,shef->sihf",
        query_rows,
        past_state.astype(jnp.bfloat16),
        preferred_element_type=jnp.float32,
    )
    joined = (doc_rows == past_doc[:, None])[:, :, None, None]
    return local_part + jnp.where(joined, from_past, 0.0)


def row_adder(normed, matrices):
    return tuple(
        (
            jnp.dot(normed, matrix_rows, preferred_element_type=jnp.float32)
            for matrix_rows in matrices
        )
    )


def shards(tokens, doc_ids, norm_gain, query_weight, key_weight, value_weight, out_gain):
    count = tokens.shape[1]
    normed = norm_rows(tokens[0].astype(jnp.float32), norm_gain).astype(jnp.bfloat16)
    projected = row_adder(
        normed,
        (
            lax.all_gather(query_weight, ("seq", "fsdp"), axis=0, tiled=True),
            lax.all_gather(key_weight, ("seq", "fsdp"), axis=0, tiled=True),
            lax.all_gather(value_weight, ("seq", "fsdp"), axis=0, tiled=True),
        ),
    )
    query_rows, key_rows, value_rows = [
        jax.nn.silu(summed).astype(jnp.bfloat16).reshape(1, count, HEADS, HEAD_DIM)
        for summed in projected
    ]
    own_summary = block_summary(key_rows, value_rows, doc_ids)
    past = entering(own_summary, "seq", join_states, start_summary(1, HEADS))
    mixed = mix_block(query_rows, key_rows, value_rows, doc_ids, past[0], past[2])
    attended = norm_rows(mixed.reshape(1, count, ATTN_WIDTH), out_gain).astype(jnp.bfloat16)
    return attended


def solution(mesh):
    in_specs = (
        P("fsdp", "seq", None),
        P("fsdp", "seq"),
        P(),
        P(("seq", "fsdp"), None),
        P(("seq", "fsdp"), None),
        P(("seq", "fsdp"), None),
        P(),
    )
    out_specs = P("fsdp", "seq", None)
    return jax.shard_map(shards, mesh=mesh, in_specs=in_specs, out_specs=out_specs, check_vma=False)
```

profile of v0, /device:TPU:0, one launch (start us, length us, event | category | flops | bytes accessed | tf_op | source)
XLA Modules:
  0.0 360.0 jit_solution(146407506452272884)
XLA Ops:
  6.5 0.7 all-gather.6.cloned.1.call-update
  7.3 0.0 all-gather.10.cloned.1.call-start
  7.3 0.7 all-gather.10.cloned.1.call-update
  8.0 0.0 all-gather.8.cloned.1.call-start
  8.1 0.7 all-gather.8.cloned.1.call-update
  8.7 0.0 all-gather.12.cloned.1.call-start
  8.8 1.2 fusion.36
  10.0 1.3 compare_reduce_fusion.1
  11.3 2.6 fusion.1
  13.9 81.0 %all-gather.6.cloned.1.call-done = bf16[3072,1536]{1,0:T(8,128)(2,1)} async-done(((bf16[96,1536]{1,0:T(8,128)(2,1)}), bf16[3072,1536]{1,0:T(8,128)(2,1)}) %all-gather.6.cloned.1.call-update) | async-done | bytes 9437200 | tf_op jit(solution)/shard_map/all_gather | solution.py:107
  94.9 10.2 %multiply_convert_fusion.3 = bf16[512,1536]{1,0:T(8,128)(2,1)} fusion(bf16[3072,1536]{1,0:T(8,128)(2,1)} %all-gather.6.cloned.1.call-done, bf16[1,512,3072]{2,1,0:T(8,128)(2,1)S(1)} %copy-done, f32[3072]{0:T(1024)S(1)} %copy-done.5, f32[512]{0:T(512)S(1)} %add_rsqrt_fusion.1), kind=kOutput, calls=%fused_computation.21 | convolution fusion | flops 4842061824 | bytes 14170112 | tf_op jit(solution)/shard_map/dot_general | solution.py:93
  105.1 2.6 copy.23
  107.7 70.7 %all-gather.10.cloned.1.call-done = bf16[3072,1536]{1,0:T(8,128)(2,1)} async-done(((bf16[96,1536]{1,0:T(8,128)(2,1)}), bf16[3072,1536]{1,0:T(8,128)(2,1)}) %all-gather.10.cloned.1.call-update) | async-done | bytes 9437200 | tf_op jit(solution)/shard_map/all_gather | solution.py:106
  178.4 10.1 %multiply_convert_fusion.1 = bf16[512,1536]{1,0:T(8,128)(2,1)} fusion(bf16[3072,1536]{1,0:T(8,128)(2,1)} %all-gather.10.cloned.1.call-done, bf16[1,512,3072]{2,1,0:T(8,128)(2,1)S(1)} %copy-done, f32[3072]{0:T(1024)S(1)} %copy-done.5, f32[512]{0:T(512)S(1)} %add_rsqrt_fusion.1), kind=kOutput, calls=%fused_computation.19 | convolution fusion | flops 4842061824 | bytes 14170112 | tf_op jit(solution)/shard_map/dot_general | solution.py:93
  188.5 1.9 copy.25
  190.4 0.0 copy-done.1
  190.5 1.3 fusion.14
  191.8 0.0 all-gather.12.cloned.1.call-update
  191.8 0.6 dynamic-slice
  192.4 1.2 bitcast_dynamic-update-slice_fusion.1
  193.7 1.3 bitcast_dynamic-update-slice_fusion
  195.0 7.4 %all-reduce.2 = (s32[8]{0:T(128)S(1)}, s32[8]{0:T(128)S(1)}) all-reduce(s32[8]{0:T(128)S(1)} %bitcast_dynamic-update-slice_fusion.1, s32[8]{0:T(128)S(1)} %bitcast_dynamic-update-slice_fusion), channel_id=1, replica_groups=mesh['seq'=8,'fsdp'=4] {'seq'}, use_global_device_ids=true, to_apply=%add | all-reduce | flops 16 | bytes 128
  202.4 0.2 fusion.17
  202.6 59.3 %all-gather.8.cloned.1.call-done = bf16[3072,1536]{1,0:T(8,128)(2,1)} async-done(((bf16[96,1536]{1,0:T(8,128)(2,1)}), bf16[3072,1536]{1,0:T(8,128)(2,1)}) %all-gather.8.cloned.1.call-update) | async-done | bytes 9437200 | tf_op jit(solution)/shard_map/all_gather | solution.py:105
  261.9 10.6 %multiply_convert_fusion.2 = bf16[512,1536]{1,0:T(8,128)(2,1)} fusion(bf16[3072,1536]{1,0:T(8,128)(2,1)} %all-gather.8.cloned.1.call-done, bf16[1,512,3072]{2,1,0:T(8,128)(2,1)} %param.9, f32[3072]{0:T(1024)S(1)} %copy-done.5, f32[512]{0:T(512)S(1)} %add_rsqrt_fusion.1), kind=kOutput, calls=%fused_computation.20 | convolution fusion | flops 4842061824 | bytes 14170112 | tf_op jit(solution)/shard_map/dot_general | solution.py:93
  272.5 1.7 copy.24
  274.2 20.4 %all-gather.12.cloned.1.call-done = bf16[96,128,128]{2,1,0:T(8,128)(2,1)} async-done(((bf16[12,128,128]{2,1,0:T(8,128)(2,1)}), bf16[96,128,128]{2,1,0:T(8,128)(2,1)}) %all-gather.12.cloned.1.call-update) | async-done | bytes 3145744 | tf_op jit(solution)/shard_map/all_gather | solution.py:18
  294.6 44.3 %while.16 = (s32[]{:T(128)}, f32[1,12,128,128]{3,2,1,0:T(8,128)S(1)}, s32[1]{0:T(128)}, s32[]{:T(128)}, bf16[8,1,12,128,128]{4,3,2,1,0:T(8,128)(2,1)}, /*index=5...) while((s32[]{:T(128)}, f32[1,12,128,128]{3,2,1,0:T(8,128)S(1)}, ...), condition=%wide.region_2.3_spmd.clone, body=%wide.region_1.2_spmd.clone.sunk | while | flops 983051 | bytes 1966284 | solution.py:35
  294.6 0.7 constant_dynamic-slice_fusion.3
  297.9 1.5 fusion.46
  300.1 0.7 constant_dynamic-slice_fusion.3
  303.5 1.5 fusion.46
  305.7 0.7 constant_dynamic-slice_fusion.3
  309.0 1.5 fusion.46
  311.2 0.7 constant_dynamic-slice_fusion.3
  314.6 1.5 fusion.46
  316.7 0.7 constant_dynamic-slice_fusion.3
  320.1 1.5 fusion.46
  322.3 0.7 constant_dynamic-slice_fusion.3
  325.6 1.5 fusion.46
  327.8 0.7 constant_dynamic-slice_fusion.3
  331.2 1.5 fusion.46
  333.4 0.7 constant_dynamic-slice_fusion.3
  336.7 1.5 fusion.46
  338.9 2.3 fusion.19
  341.2 8.4 %fusion.9 = (f32[512]{0:T(512)S(1)}, f32[1,12,128,512]{3,2,1,0:T(8,128)}) fusion(f32[12,128,512]{2,1,0:T(8,128)} %fusion.19, pred[512]{0:T(512)(128)(4,1)S(1)} %compare_reduce_fusion, bf16[512,12,128]{0,2,1:T(8,128)(2,1)} %bitcast.72, pred[512,512]{1,0:T(8,128)(4,1)S(1)} %fusion.17, bf16[512,12,128]{0,2,1:T(8,128)(2,1)S(1)} %bitcast.70, ...), kind=kOutput, calls=%fused_computation.15 | convolution fusion | flops 1620049408 | bytes 11274752 | tf_op jit(solution)/shard_map/shij,sjhe->sihe/dot_general | solution.py:77
  349.6 2.4 copy.32
  352.0 1.5 multiply_convert_fusion
  (20 shorter events, 0.1 us)
Async XLA Ops:
  6.5 88.4 %copy-start = (bf16[1,512,3072]{2,1,0:T(8,128)(2,1)S(1)}, bf16[1,512,3072]{2,1,0:T(8,128)(2,1)}, u32[]{:S(2)}) copy-start(bf16[1,512,3072]{2,1,0:T(8,128)(2,1)} %param.9) | copy-start | bytes 9437188
  6.5 88.4 %copy-start.5 = (f32[3072]{0:T(1024)S(1)}, f32[3072]{0:T(1024)}, u32[]{:S(2)}) copy-start(f32[3072]{0:T(1024)} %param.11) | copy-start | bytes 36868
  6.5 88.4 %all-gather.6.cloned.1.call-start = ((), (), s32[]{:S(2)}) async-start(), calls=%async_computation | async-start | bytes 9732096 | tf_op jit(solution)/shard_map/all_gather | solution.py:107
  7.3 171.1 %all-gather.10.cloned.1.call-start = ((), (), s32[]{:S(2)}) async-start(), calls=%async_computation.2 | async-start | bytes 9732096 | tf_op jit(solution)/shard_map/all_gather | solution.py:106
  8.0 253.9 %all-gather.8.cloned.1.call-start = ((), (), s32[]{:S(2)}) async-start(), calls=%async_computation.1 | async-start | bytes 9732096 | tf_op jit(solution)/shard_map/all_gather | solution.py:105
  8.7 285.8 %all-gather.12.cloned.1.call-start = ((), (), s32[]{:S(2)}) async-start(), calls=%async_computation.3 | async-start | bytes 3538944 | tf_op jit(solution)/shard_map/all_gather | solution.py:18
  188.5 2.0 copy-start.1
  190.4 71.5 %copy-start.2 = (bf16[512,1536]{0,1:T(8,128)(2,1)}, bf16[512,1536]{0,1:T(8,128)(2,1)S(1)}, u32[]{:S(2)}) copy-start(bf16[512,1536]{0,1:T(8,128)(2,1)S(1)} %copy.25) | copy-start | bytes 4718596
  190.4 1.4 copy-start.6
  190.4 12.0 %copy-start.3 = (s32[1,512]{1,0:T(1,128)S(1)}, s32[1,512]{1,0:T(1,128)}, u32[]{:S(2)}) copy-start(s32[1,512]{1,0:T(1,128)} %param.10) | copy-start | bytes 6148
  349.6 2.4 copy-start.4
Sparse Core Ops, SparseCore 0:
  10.2 84.7 all-gather.5
  97.7 80.6 all-gather.9
  181.2 80.6 all-gather.7
  263.6 30.9 all-gather.11
where the time goes:
time: 361 us; the launch traced here: 360 us
  waiting for transfers between devices  233 us (65%)
  matrix products  42.9 us (12%)
  loops' own time  27.2 us (8%)
  local copies, waits for them, and re-layouts  18.4 us (5%)
  other arithmetic  17.3 us (5%)
  between operations  13.3 us (4%)
  blocking collectives  7.39 us (2%)
    all_gather x1, waiting for transfers between devices, shards(): lax.all_gather(value_weight, ('seq', 'fsdp'), axis=0, tiled=True)  81 us
    all_gather x1, waiting for transfers between devices, shards(): lax.all_gather(key_weight, ('seq', 'fsdp'), axis=0, tiled=True)  70.7 us
    all_gather x1, waiting for transfers between devices, shards(): lax.all_gather(query_weight, ('seq', 'fsdp'), axis=0, tiled=True)  59.3 us
    dot_general x3, matrix products, row_adder(): jnp.dot(normed, matrix_rows, preferred_element_type=jnp.float32)  30.9 us
    another operation x1, loops' own time, entering(): return lax.fori_loop(0, length, turn, start)  27.2 us
    all_gather x1, waiting for transfers between devices, entering(): lax.all_gather(part.astype(kind), axis)  20.4 us
    select_n x8, other arithmetic, turn(): return jax.tree.map(lambda a, b: jnp.where(reached, a, b), new, before)  11.7 us
    dot_general x1, matrix products, mix_block(): jnp.einsum('shij,sjhe->sihe', weights, value_rows, preferred_element_type...  8.45 us
  transfers between devices with their start and end apart: 4, of which 4 were waited for; matrix products, arithmetic and copies ran while one was open for 13% of the time, Pallas kernels for 0%

commit v1 on v0

v1 whole, which is shorter than its diff:
```python
import jax
import jax.numpy as jnp
from jax import lax
from jax.sharding import Mesh, PartitionSpec as P

HEADS = 12
HEAD_DIM = 128
ATTN_WIDTH = 1536


EPS = 1e-06


def norm_rows(values, gain):
    mean_sq = jnp.mean(values * values, axis=-1, keepdims=True)
    return values * lax.rsqrt(mean_sq + EPS) * gain


def swap_core(value):
    return lax.ppermute(value, "core", [(0, 1), (1, 0)])


def in_core_order(core, mine, theirs):
    return jnp.where(core == 0, jnp.stack([mine, theirs]), jnp.stack([theirs, mine]))


def mix_block(query_rows, key_rows, value_rows, doc_rows, past_state, past_doc):
    count = doc_rows.shape[1]
    scores = jnp.einsum("sihe,sjhe->shij", query_rows, key_rows, preferred_element_type=jnp.float32)
    row_pos = lax.broadcasted_iota(jnp.int32, (count, count), 0)
    col_pos = lax.broadcasted_iota(jnp.int32, (count, count), 1)
    visible = (row_pos >= col_pos)[None] & (doc_rows[:, :, None] == doc_rows[:, None, :])
    weights = jnp.where(visible[:, None], scores, 0.0).astype(jnp.bfloat16)
    local_part = jnp.einsum(
        "shij,sjhe->sihe", weights, value_rows, preferred_element_type=jnp.float32
    )
    from_past = jnp.einsum(
        "sihe,shef->sihf",
        query_rows,
        past_state.astype(jnp.bfloat16),
        preferred_element_type=jnp.float32,
    )
    joined = (doc_rows == past_doc[:, None])[:, :, None, None]
    return local_part + jnp.where(joined, from_past, 0.0)


def make_shards(n_sq, n_fsdp):
    def shards(tokens, doc_ids, norm_gain, query_weight, key_weight, value_weight, out_gain):
        core = lax.axis_index("core")
        sq = lax.axis_index("sq")
        count, width = tokens.shape[1], tokens.shape[2]
        rows = query_weight.shape[0]
        half = ATTN_WIDTH // 2
        heads = HEADS // 2

        normed = norm_rows(tokens[0].astype(jnp.float32), norm_gain).astype(jnp.bfloat16)
        normed = normed.reshape(count, n_sq, 2, n_fsdp, rows).transpose(0, 1, 3, 2, 4)
        normed = normed.reshape(count, width)
        pair = jnp.concatenate([normed, swap_core(normed)], axis=0)

        def gather_half(weight):
            mine = lax.dynamic_slice_in_dim(weight, core * half, half, axis=1)
            other = lax.dynamic_slice_in_dim(weight, (1 - core) * half, half, axis=1)
            both = in_core_order(core, mine, swap_core(other))
            full = lax.all_gather(both, ("sq", "fsdp"), axis=0, tiled=False)
            return full.reshape(width, half)

        def project(weight):
            summed = jnp.dot(pair, gather_half(weight), preferred_element_type=jnp.float32)
            return jax.nn.silu(summed).astype(jnp.bfloat16).reshape(2, count, heads, HEAD_DIM)

        query_rows = project(query_weight)
        key_rows = project(key_weight)
        value_rows = project(value_weight)

        own_docs = doc_ids[0]
        docs = jnp.stack([own_docs, swap_core(own_docs)])
        first, last = docs[:, 0], docs[:, -1]
        slot_core = jnp.stack([core, 1 - core])
        block = 2 * sq + slot_core

        tail_keys = jnp.where((docs == last[:, None])[:, :, None, None], key_rows, jnp.zeros_like(key_rows))
        tail = jnp.einsum("bjhe,bjhf->bhef", tail_keys, value_rows, preferred_element_type=jnp.float32)
        all_tail = lax.all_gather(tail.astype(jnp.bfloat16), "sq")
        all_last = lax.all_gather(last, "sq")
        all_block = 2 * jnp.arange(n_sq, dtype=jnp.int32)[:, None] + slot_core[None, :]
        counted = (all_block[None] < block[:, None, None]) & (all_last[None] == first[:, None, None])
        carried = jnp.einsum(
            "bsk,skhef->bhef",
            counted.astype(jnp.bfloat16),
            all_tail,
            preferred_element_type=jnp.float32,
        )

        mixed = mix_block(query_rows, key_rows, value_rows, docs, carried, first)
        mixed = mixed.reshape(2, count, half)
        squares = jnp.sum(mixed * mixed, axis=-1)
        total = squares + swap_core(squares)[::-1]
        scale = lax.rsqrt(total / ATTN_WIDTH + EPS)
        gain = lax.dynamic_slice_in_dim(out_gain, core * half, half)
        attended = (mixed * scale[:, :, None] * gain).astype(jnp.bfloat16)
        theirs = swap_core(attended[1])
        out = jnp.where(
            core == 0,
            jnp.concatenate([attended[0], theirs], axis=-1),
            jnp.concatenate([theirs, attended[0]], axis=-1),
        )
        return out[None]

    return shards


def solution(mesh):
    n_seq, n_fsdp = mesh.shape["seq"], mesh.shape["fsdp"]
    chips = Mesh(mesh.devices.reshape(n_seq // 2, 2, n_fsdp), ("sq", "core", "fsdp"))
    seq = ("sq", "core")
    in_specs = (
        P("fsdp", seq, None),
        P("fsdp", seq),
        P(),
        P(("sq", "core", "fsdp"), None),
        P(("sq", "core", "fsdp"), None),
        P(("sq", "core", "fsdp"), None),
        P(),
    )
    out_specs = P("fsdp", seq, None)
    return jax.shard_map(
        make_shards(n_seq // 2, n_fsdp), mesh=chips, in_specs=in_specs, out_specs=out_specs, check_vma=False
    )
```

time: 361 us -> 317 us (0.88)
  loops' own time: 27.2 us -> 0 us
  waiting for transfers between devices: 233 us -> 221 us
  other arithmetic: 17.3 us -> 8.72 us
    another operation x1 -> x0, loops' own time: 27.2 us -> none  [entering(): return lax.fori_loop(0, length, turn, start)]
    all_gather x4, waiting for transfers between devices: 231 us -> 213 us  [the longest x3 194 us: gather_half(): full = lax.all_gather(both, ('sq', 'fsdp'), axis=0, tiled=False)]
    ppermute x0 -> x7, waiting for transfers between devices: none -> 8.11 us  [swap_core(): return lax.ppermute(value, 'core', [(0, 1), (1, 0)])]
    reshape x1 -> x4, local copies, waits for them, and re-layouts: 2.39 us -> 9.73 us  [the longest x3 7.36 us: project(): jax.nn.silu(summed).astype(jnp.bfloat16).reshape(2, count, heads, HEAD_DIM)]
    select_n x8 -> x5, other arithmetic: 11.7 us -> 4.98 us  [the longest x3 2.21 us: in_core_order(): jnp.where(core == 0, jnp.stack([mine, theirs]), jnp.stack([theirs, mine]))]
    dynamic_slice x8 -> x1, local copies, waits for them, and re-layouts: 5.36 us -> 0.08 us  [shards(): gain = lax.dynamic_slice_in_dim(out_gain, core * half, half)]
    convert_element_type x3 -> x1, local copies, waits for them, and re-layouts: 6.21 us -> 1.75 us  [project(): jax.nn.silu(summed).astype(jnp.bfloat16).reshape(2, count, heads, HEAD_DIM)]
    dot_general x4 -> x5, matrix products: 32.2 us -> 32.4 us  [the longest x3 27.7 us: project(): jnp.dot(pair, gather_half(weight), preferred_element_type=jnp.float32)]
  transfers between devices with their start and end apart: 4 -> 11, of which waited for: 4 -> 10; matrix products, arithmetic and copies ran while one was open for 13% -> 17% of each run, Pallas kernels for 0% -> 0%
where the time goes in v1:
time: 317 us; the launch traced here: 316 us
  waiting for transfers between devices  221 us (70%)
  matrix products  43.4 us (14%)
  local copies, waits for them, and re-layouts  18.8 us (6%)
  between operations  14 us (4%)
  other arithmetic  8.72 us (3%)
  blocking collectives  7.36 us (2%)
    all_gather x3, waiting for transfers between devices, gather_half(): full = lax.all_gather(both, ('sq', 'fsdp'), axis=0, tiled=False)  194 us
    dot_general x3, matrix products, project(): jnp.dot(pair, gather_half(weight), preferred_element_type=jnp.float32)  27.7 us
    all_gather x1, waiting for transfers between devices, shards(): all_tail = lax.all_gather(tail.astype(jnp.bfloat16), 'sq')  18.9 us
    dot_general x1, matrix products, mix_block(): jnp.einsum('shij,sjhe->sihe', weights, value_rows, preferred_element_type...  8.7 us
    ppermute x7, waiting for transfers between devices, swap_core(): return lax.ppermute(value, 'core', [(0, 1), (1, 0)])  8.11 us
    reshape x3, local copies, waits for them, and re-layouts, project(): jax.nn.silu(summed).astype(jnp.bfloat16).reshape(2, count, heads, HEAD_DIM)  7.36 us
    unnamed x1, blocking collectives  7.36 us
  transfers between devices with their start and end apart: 11, of which 10 were waited for; matrix products, arithmetic and copies ran while one was open for 17% of the time, Pallas kernels for 0%

profile of v1, /device:TPU:0, one launch (start us, length us, event | category | flops | bytes accessed | tf_op | source)
XLA Modules:
  0.0 316.3 jit_solution(2478674754047236494)
XLA Ops:
  6.5 1.0 dynamic-slice_bitcast_fusion
  7.6 0.5 collective-permute-start.4
  8.1 1.0 collective-permute-done.4
  9.1 0.7 maximum_select_fusion.3
  9.9 1.0 dynamic-slice_bitcast_fusion.2
  10.9 0.4 collective-permute-start.1
  11.4 1.0 collective-permute-done.1
  12.4 0.7 maximum_select_fusion.1
  13.2 0.4 collective-permute-start.3
  13.7 1.0 collective-permute-done.3
  14.7 0.7 maximum_select_fusion.2
  15.5 3.2 %copy.37 = bf16[1,512,3072]{1,2,0:T(8,128)(2,1)S(1)} copy(bf16[1,512,3072]{2,1,0:T(8,128)(2,1)} %param.7) | data formatting | bytes 6291456 | tf_op args[0]
  18.8 0.7 multiply_reduce_fusion
  19.5 0.9 fusion.5
  20.4 0.3 copy.38
  20.7 0.4 collective-permute-start
  21.1 0.3 collective-permute-start.2
  21.6 0.6 dynamic-slice
  22.9 2.7 collective-permute-done.2
  25.6 0.2 fusion.45
  25.8 0.2 dynamic-update-slice
  26.1 0.5 collective-permute-done
  26.5 66.8 %all-gather.11.cloned.1.call-done = bf16[16,2,96,768]{3,2,1,0:T(8,128)(2,1)} async-done(((bf16[1,2,96,768]{3,2,1,0:T(8,128)(2,1)}), bf16[16,2,96,768]{3,2,1,0:T(8,128)(2,1)}) %all-gather.11.cloned.1.call-update) | async-done | bytes 4718608 | tf_op jit(solution)/shard_map/all_gather | solution.py:65
  93.3 9.0 %multiply_convert_fusion.2 = bf16[1024,768]{1,0:T(8,128)(2,1)} fusion(bf16[3072,768]{1,0:T(8,128)(2,1)} %bitcast.61, bf16[512,3072]{0,1:T(8,128)(2,1)} %collective-permute-done, bf16[512,3072]{0,1:T(8,128)(2,1)S(1)} %bitcast.49), kind=kOutput, calls=%fused_computation.13 | convolution fusion | flops 4848353280 | bytes 12582912 | tf_op jit(solution)/shard_map/dot_general | solution.py:69
  102.3 1.8 copy.41
  104.1 1.2 reshape.412
  105.3 69.9 %all-gather.7.cloned.1.call-done = bf16[16,2,96,768]{3,2,1,0:T(8,128)(2,1)} async-done(((bf16[1,2,96,768]{3,2,1,0:T(8,128)(2,1)}), bf16[16,2,96,768]{3,2,1,0:T(8,128)(2,1)}) %all-gather.7.cloned.1.call-update) | async-done | bytes 4718608 | tf_op jit(solution)/shard_map/all_gather | solution.py:65
  175.2 9.6 %multiply_convert_fusion.4 = bf16[1024,768]{1,0:T(8,128)(2,1)S(1)} fusion(bf16[3072,768]{1,0:T(8,128)(2,1)} %bitcast.63, bf16[512,3072]{0,1:T(8,128)(2,1)} %collective-permute-done, bf16[512,3072]{0,1:T(8,128)(2,1)} %bitcast.50), kind=kOutput, calls=%fused_computation.15 | convolution fusion | flops 4848353280 | bytes 12582912 | tf_op jit(solution)/shard_map/dot_general | solution.py:69
  184.8 2.8 reshape.428
  187.6 1.3 broadcast_select_fusion
  188.9 0.3 copy-done.3
  189.2 1.4 fusion.22
  190.8 7.4 %all-reduce = s32[8]{0:T(128)S(1)} all-reduce(s32[8]{0:T(128)S(1)} %dynamic-update-slice), channel_id=2, replica_groups=mesh['sq'=4,'core'=2,'fsdp'=4] {'sq'}, use_global_device_ids=true, to_apply=%add | all-reduce | flops 8 | bytes 64
  198.3 1.3 compare_and_fusion
  199.6 57.4 %all-gather.9.cloned.1.call-done = bf16[16,2,96,768]{3,2,1,0:T(8,128)(2,1)} async-done(((bf16[1,2,96,768]{3,2,1,0:T(8,128)(2,1)}), bf16[16,2,96,768]{3,2,1,0:T(8,128)(2,1)}) %all-gather.9.cloned.1.call-update) | async-done | bytes 4718608 | tf_op jit(solution)/shard_map/all_gather | solution.py:65
  257.0 9.0 %multiply_convert_fusion.3 = bf16[1024,768]{1,0:T(8,128)(2,1)} fusion(bf16[3072,768]{1,0:T(8,128)(2,1)} %bitcast.62, bf16[512,3072]{0,1:T(8,128)(2,1)} %collective-permute-done, bf16[512,3072]{0,1:T(8,128)(2,1)S(1)} %bitcast.51), kind=kOutput, calls=%fused_computation.14 | convolution fusion | flops 4848353280 | bytes 12582912 | tf_op jit(solution)/shard_map/dot_general | solution.py:69
  266.1 3.4 %reshape.425 = bf16[2,512,6,128]{3,2,1,0:T(8,128)(2,1)S(1)} reshape(bf16[1024,768]{1,0:T(8,128)(2,1)} %multiply_convert_fusion.3) | data formatting | bytes 3145728 | tf_op jit(solution)/shard_map/reshape | solution.py:70
  269.4 18.9 %all-gather.13.cloned.1.call-done = bf16[8,6,128,128]{3,2,1,0:T(8,128)(2,1)} async-done(((bf16[2,6,128,128]{3,2,1,0:T(8,128)(2,1)}), bf16[8,6,128,128]{3,2,1,0:T(8,128)(2,1)}) %all-gather.13.cloned.1.call-update) | async-done | bytes 1572880 | tf_op jit(solution)/shard_map/all_gather | solution.py:84
  288.4 3.3 %fusion.19 = bf16[2,6,128,128]{3,0,2,1:T(2,128)(2,1)S(1)} fusion(bf16[4,2,6,128,128]{4,3,2,1,0:T(8,128)(2,1)} %bitcast.64, s32[4,2]{0,1:T(2,128)S(1)} %copy.45, s32[4,2]{0,1:T(2,128)S(1)} %broadcast_add_fusion, s32[2]{0:T(128)S(1)} %get-tuple-element.5, s32[2]{0:T(128)S(1)} %get-tuple-element.7), kind=kOutput, calls=%fused_computation.28 | convolution fusion | flops 3342384 | bytes 1966160 | tf_op jit(solution)/shard_map/bsk,skhef->bhef/dot_general | solution.py:88
  291.7 2.3 fusion.31
  294.0 8.7 %fusion.6 = (f32[2,512]{1,0:T(2,128)S(1)}, f32[2,6,128,512]{3,2,1,0:T(8,128)}) fusion(f32[2,6,128,512]{3,2,1,0:T(8,128)} %fusion.31, pred[2,512]{1,0:T(4,128)(4,1)S(1)} %get-tuple-element.17, pred[2,512,512]{2,1,0:T(8,128)(4,1)S(1)} %copy-done.4, bf16[2,512,6,128]{1,0,3,2:T(2,128)(2,1)} %copy-done, bf16[2,512,6,128]{3,2,1,0:T(8,128)(2,1)S(1)} %reshape.425, ...), kind=kOutput, calls=%fused_computation.10 | convolution fusion | flops 1620048896 | bytes 11539456 | tf_op jit(solution)/shard_map/shij,sjhe->sihe/dot_general | solution.py:34
  302.8 2.4 copy.51
  305.2 0.1 rev.3
  305.3 0.3 multiply_convert_fusion.1
  305.7 0.1 fusion.52
  305.8 0.6 collective-permute-start.6
  306.4 1.9 collective-permute-done.6
  308.3 1.5 maximum_select_fusion
  (43 shorter events, 1.0 us)
Async XLA Ops:
  6.5 6.7 %copy-start.5 = (bf16[96,1536]{1,0:T(8,128)(2,1)S(1)}, bf16[96,1536]{1,0:T(8,128)(2,1)}, u32[]{:S(2)}) copy-start(bf16[96,1536]{1,0:T(8,128)(2,1)} %param.10) | copy-start | bytes 884740
  6.5 86.8 %all-gather.11.cloned.1.call-start = ((), (), s32[]{:S(2)}) async-start(), calls=%async_computation.2 | async-start | bytes 5013504 | tf_op jit(solution)/shard_map/all_gather | solution.py:65
  7.6 1.5 collective-permute-start.4
  9.9 165.3 %all-gather.7.cloned.1.call-start = ((), (), s32[]{:S(2)}) async-start(), calls=%async_computation | async-start | bytes 5013504 | tf_op jit(solution)/shard_map/all_gather | solution.py:65
  10.9 1.4 collective-permute-start.1
  13.1 243.9 %all-gather.9.cloned.1.call-start = ((), (), s32[]{:S(2)}) async-start(), calls=%async_computation.1 | async-start | bytes 5013504 | tf_op jit(solution)/shard_map/all_gather | solution.py:65
  13.2 1.4 collective-permute-start.3
  15.4 3.3 %copy-start.7 = (f32[3072]{0:T(1024)S(1)}, f32[3072]{0:T(1024)}, u32[]{:S(2)}) copy-start(f32[3072]{0:T(1024)} %param.9) | copy-start | bytes 36868
  15.4 272.9 %all-gather.13.cloned.1.call-start = ((), (), s32[]{:S(2)}) async-start(), calls=%async_computation.3 | async-start | bytes 1966080 | tf_op jit(solution)/shard_map/all_gather | solution.py:84
  20.4 0.7 copy-start.6
  20.4 1.2 copy-start.9
  20.7 72.6 %copy-start.1 = (bf16[512,4,4,2,96]{0,4,3,2,1:T(8,128)(2,1)}, bf16[512,4,4,2,96]{0,4,3,2,1:T(8,128)(2,1)S(1)}, u32[]{:S(2)}) copy-start(bf16[512,4,4,2,96]{0,4,3,2,1:T(8,128)(2,1)S(1)} %copy.38) | copy-start | bytes 9437188
  20.7 5.9 %collective-permute-start = (bf16[512,3072]{0,1:T(8,128)(2,1)S(1)}, bf16[512,3072]{0,1:T(8,128)(2,1)}, u32[]{:S(2)}, u32[]{:S(2)}) collective-permute-start(bf16[512,3072]{0,1:T(8,128)(2,1)S(1)} %bitcast.48), channel_id=1, source_target_pairs={{0,4},{4,0},{1,5},{5,1},{2,6},{6,2},{3,7},{7,3},{8,12},{12,8},{9,1... | collective-permute-start | bytes 9437192 | tf_op jit(solution)/shard_map/ppermute | solution.py:20
  21.1 4.5 %collective-permute-start.2 = (s32[512]{0:T(512)S(1)}, s32[512]{0:T(512)S(1)}, u32[]{:S(2)}, u32[]{:S(2)}) collective-permute-start(s32[512]{0:T(512)S(1)} %bitcast.57), channel_id=1, source_target_pairs={{0,4},{4,0},{1,5},{5,1},{2,6},{6,2},{3,7},{7,3},{8,12},{12,8},{9,1... | collective-permute-start | bytes 6152 | tf_op jit(solution)/shard_map/ppermute | solution.py:20
  105.3 82.3 %copy-start = (bf16[2,512,6,128]{1,0,3,2:T(2,128)(2,1)}, bf16[2,512,6,128]{1,0,3,2:T(2,128)(2,1)S(1)}, u32[]{:S(2)}) copy-start(bf16[2,512,6,128]{1,0,3,2:T(2,128)(2,1)S(1)} %reshape.412) | copy-start | bytes 4718596
  187.6 1.6 copy-start.3
  189.2 67.8 %copy-start.2 = (bf16[512,4,4,2,96]{0,4,3,2,1:T(8,128)(2,1)S(1)}, bf16[512,4,4,2,96]{0,4,3,2,1:T(8,128)(2,1)}, u32[]{:S(2)}) copy-start(bf16[512,4,4,2,96]{0,4,3,2,1:T(8,128)(2,1)} %copy-done.1) | copy-start | bytes 9437188
  291.7 2.3 copy-start.4
  294.0 8.7 %copy-start.8 = (f32[1536]{0:T(1024)S(1)}, f32[1536]{0:T(1024)}, u32[]{:S(2)}) copy-start(f32[1536]{0:T(1024)} %param.13) | copy-start | bytes 18436
  302.7 2.5 collective-permute-start.5
  305.8 2.5 collective-permute-start.6
Sparse Core Ops, SparseCore 0:
  10.1 83.1 all-gather.10
  96.1 79.0 all-gather.6
  177.9 79.0 all-gather.8
  258.7 29.5 all-gather.12

commit v2 on v1

--- a/solution.py
+++ b/solution.py
@@ -58,20 +58,25 @@
         normed = normed.reshape(count, width)
         pair = jnp.concatenate([normed, swap_core(normed)], axis=0)
 
-        def gather_half(weight):
-            mine = lax.dynamic_slice_in_dim(weight, core * half, half, axis=1)
-            other = lax.dynamic_slice_in_dim(weight, (1 - core) * half, half, axis=1)
-            both = in_core_order(core, mine, swap_core(other))
-            full = lax.all_gather(both, ("sq", "fsdp"), axis=0, tiled=False)
-            return full.reshape(width, half)
+        def halves(start):
+            return jnp.concatenate(
+                [
+                    lax.dynamic_slice_in_dim(weight, start, half, axis=1)
+                    for weight in (query_weight, key_weight, value_weight)
+                ],
+                axis=1,
+            )
 
-        def project(weight):
-            summed = jnp.dot(pair, gather_half(weight), preferred_element_type=jnp.float32)
-            return jax.nn.silu(summed).astype(jnp.bfloat16).reshape(2, count, heads, HEAD_DIM)
-
-        query_rows = project(query_weight)
-        key_rows = project(key_weight)
-        value_rows = project(value_weight)
+        mine, other = halves(core * half), halves((1 - core) * half)
+        both = in_core_order(core, mine, swap_core(other))
+        gathered = lax.all_gather(both, ("sq", "fsdp"), axis=0, tiled=False)
+        summed = jnp.dot(pair, gathered.reshape(width, 3 * half), preferred_element_type=jnp.float32)
+        query_rows, key_rows, value_rows = [
+            jax.nn.silu(summed[:, part * half:(part + 1) * half])
+            .astype(jnp.bfloat16)
+            .reshape(2, count, heads, HEAD_DIM)
+            for part in range(3)
+        ]
 
         own_docs = doc_ids[0]
         docs = jnp.stack([own_docs, swap_core(own_docs)])

time: 317 us -> 273 us (0.86)
  waiting for transfers between devices: 221 us -> 183 us
  matrix products: 43.4 us -> 35.4 us
    all_gather x3 -> x1, waiting for transfers between devices: 194 us -> 159 us  [shards(): gathered = lax.all_gather(both, ('sq', 'fsdp'), axis=0, tiled=False)]
    dot_general x3 -> x1, matrix products: 27.7 us -> 19.8 us  [shards(): jnp.dot(pair, gathered.reshape(width, 3 * half), preferred_element_type=j...]
    convert_element_type x0 -> x1, other arithmetic: none -> 3.57 us  [shards(): query_rows, key_rows, value_rows = [jax.nn.silu(summed[:, part * half:(pa...]
    ppermute x7 -> x5, waiting for transfers between devices: 8.11 us -> 8.11 us  [swap_core(): return lax.ppermute(value, 'core', [(0, 1), (1, 0)])]
  transfers between devices with their start and end apart: 11 -> 7, of which waited for: 10 -> 6; matrix products, arithmetic and copies ran while one was open for 17% -> 5% of each run, Pallas kernels for 0% -> 0%
where the time goes in v2:
time: 273 us
  waiting for transfers between devices  183 us (67%)
  matrix products  35.4 us (13%)
  local copies, waits for them, and re-layouts  20.3 us (7%)
  between operations  14.2 us (5%)
  other arithmetic  10.3 us (4%)
  blocking collectives  7.37 us (3%)
    all_gather x1, waiting for transfers between devices, shards(): gathered = lax.all_gather(both, ('sq', 'fsdp'), axis=0, tiled=False)  159 us
    dot_general x1, matrix products, shards(): jnp.dot(pair, gathered.reshape(width, 3 * half), preferred_element_type=j...  19.8 us
    all_gather x1, waiting for transfers between devices, shards(): all_tail = lax.all_gather(tail.astype(jnp.bfloat16), 'sq')  16.4 us
    reshape x3, local copies, waits for them, and re-layouts, shards(): query_rows, key_rows, value_rows = [jax.nn.silu(summed[:, part * half:(pa...  9.01 us
    dot_general x1, matrix products, mix_block(): jnp.einsum('shij,sjhe->sihe', weights, value_rows, preferred_element_type...  8.68 us
    ppermute x5, waiting for transfers between devices, swap_core(): return lax.ppermute(value, 'core', [(0, 1), (1, 0)])  8.11 us
    unnamed x1, blocking collectives  7.37 us
  transfers between devices with their start and end apart: 7, of which 6 were waited for; matrix products, arithmetic and copies ran while one was open for 5% of the time, Pallas kernels for 0%

profile of v2, /device:TPU:0, one launch (start us, length us, event | category | flops | bytes accessed | tf_op | source)
XLA Modules:
  0.0 272.7 jit_solution(795459140453705805)
XLA Ops:
  6.5 1.0 constant_dynamic-slice_fusion.5
  7.5 1.2 constant_dynamic-slice_fusion.3
  8.8 0.5 collective-permute-start.1
  9.3 1.4 collective-permute-done.1
  10.7 1.0 maximum_select_fusion.1
  11.8 0.0 all-gather.7.cloned.1.call-start
  11.8 3.2 %copy.37 = bf16[1,512,3072]{1,2,0:T(8,128)(2,1)S(1)} copy(bf16[1,512,3072]{2,1,0:T(8,128)(2,1)} %param.7) | data formatting | bytes 6291456 | tf_op args[0]
  15.0 0.1 mul.75
  15.1 0.7 multiply_reduce_fusion
  15.9 0.9 fusion.9
  16.7 0.3 copy.38
  17.0 0.4 collective-permute-start
  17.4 0.3 collective-permute-start.2
  17.8 4.2 %collective-permute-done.2 = s32[512]{0:T(512)S(1)} collective-permute-done((s32[512]{0:T(512)S(1)}, s32[512]{0:T(512)S(1)}, u32[]{:S(2)}, u32[]{:S(2)}) %collective-permute-start.2) | collective-permute-done | bytes 2080 | tf_op jit(solution)/shard_map/ppermute | solution.py:20
  22.0 0.2 fusion.46
  22.2 0.1 broadcast_compare_fusion.1
  22.3 0.6 collective-permute-done
  22.9 158.5 %all-gather.5.cloned.1.call-done = bf16[16,2,96,2304]{3,2,1,0:T(8,128)(2,1)} async-done(((bf16[1,2,96,2304]{3,2,1,0:T(8,128)(2,1)}), bf16[16,2,96,2304]{3,2,1,0:T(8,128)(2,1)}) %all-gather.5.cloned.1.call-update) | async-done | bytes 14155792 | tf_op jit(solution)/shard_map/all_gather | solution.py:72
  181.4 19.8 %fusion.1 = f32[1024,2304]{1,0:T(8,128)S(1)} fusion(bf16[3072,2304]{1,0:T(8,128)(2,1)} %bitcast.47, bf16[512,3072]{0,1:T(8,128)(2,1)} %collective-permute-done, bf16[512,3072]{0,1:T(8,128)(2,1)S(1)} %bitcast.39), kind=kOutput, calls=%fused_computation.2 | convolution fusion | flops 14508097536 | bytes 29884416 | tf_op jit(solution)/shard_map/dot_general | solution.py:73
  201.2 3.6 %multiply_convert_fusion.4 = (bf16[1024,768]{1,0:T(8,128)(2,1)S(1)}, bf16[1024,768]{1,0:T(8,128)(2,1)S(1)}, bf16[1024,768]{1,0:T(8,128)(2,1)}) fusion(f32[1024,2304]{1,0:T(8,128)S(1)} %fusion.1), kind=kLoop, calls=%fused_computation.18 | loop fusion | flops 11796480 | bytes 14155776 | tf_op jit(solution)/shard_map/convert_element_type | solution.py:76
  204.7 1.7 copy.41
  206.4 2.9 %reshape.286 = bf16[2,512,6,128]{1,0,3,2:T(2,128)(2,1)S(1)} reshape(bf16[1024,768]{0,1:T(8,128)(2,1)} %copy.41) | data formatting | bytes 3145728 | tf_op jit(solution)/shard_map/reshape | solution.py:77
  209.3 2.8 %reshape.302 = bf16[2,512,6,128]{3,2,1,0:T(8,128)(2,1)} reshape(bf16[1024,768]{1,0:T(8,128)(2,1)S(1)} %get-tuple-element.9) | data formatting | bytes 3145728 | tf_op jit(solution)/shard_map/reshape | solution.py:77
  212.0 1.3 broadcast_select_fusion
  213.3 0.3 copy-done.1
  213.6 1.4 fusion.23
  215.1 0.6 dynamic-slice
  216.2 0.1 broadcast_add_fusion.1
  216.3 0.1 broadcast_add_fusion
  216.3 0.2 dynamic-update-slice
  216.5 0.1 iota_compare_fusion
  216.6 7.4 %all-reduce = s32[8]{0:T(128)S(1)} all-reduce(s32[8]{0:T(128)S(1)} %dynamic-update-slice), channel_id=2, replica_groups=mesh['sq'=4,'core'=2,'fsdp'=4] {'sq'}, use_global_device_ids=true, to_apply=%add | all-reduce | flops 8 | bytes 64
  224.0 0.1 reshape.289
  224.1 0.1 copy.45
  224.2 0.4 compare_and_fusion
  224.6 3.4 %reshape.299 = bf16[2,512,6,128]{3,2,1,0:T(8,128)(2,1)S(1)} reshape(bf16[1024,768]{1,0:T(8,128)(2,1)} %get-tuple-element.11) | data formatting | bytes 3145728 | tf_op jit(solution)/shard_map/reshape | solution.py:77
  228.0 16.4 %all-gather.7.cloned.1.call-done = bf16[8,6,128,128]{3,2,1,0:T(8,128)(2,1)} async-done(((bf16[2,6,128,128]{3,2,1,0:T(8,128)(2,1)}), bf16[8,6,128,128]{3,2,1,0:T(8,128)(2,1)}) %all-gather.7.cloned.1.call-update) | async-done | bytes 1572880 | tf_op jit(solution)/shard_map/all_gather | solution.py:89
  244.5 3.3 %fusion.20 = bf16[2,6,128,128]{3,0,2,1:T(2,128)(2,1)S(1)} fusion(bf16[4,2,6,128,128]{4,3,2,1,0:T(8,128)(2,1)} %bitcast.48, s32[4,2]{0,1:T(2,128)S(1)} %copy.45, s32[4,2]{0,1:T(2,128)S(1)} %broadcast_add_fusion, s32[2]{0:T(128)S(1)} %get-tuple-element.5, s32[2]{0:T(128)S(1)} %get-tuple-element.7), kind=kOutput, calls=%fused_computation.28 | convolution fusion | flops 3342384 | bytes 1966160 | tf_op jit(solution)/shard_map/bsk,skhef->bhef/dot_general | solution.py:93
  247.8 2.3 fusion.32
  250.1 8.7 %fusion.10 = (f32[2,512]{1,0:T(2,128)S(1)}, f32[2,6,128,512]{3,2,1,0:T(8,128)}) fusion(f32[2,6,128,512]{3,2,1,0:T(8,128)} %fusion.32, pred[2,512]{1,0:T(4,128)(4,1)S(1)} %get-tuple-element.20, pred[2,512,512]{2,1,0:T(8,128)(4,1)S(1)} %compare_and_fusion, bf16[2,512,6,128]{1,0,3,2:T(2,128)(2,1)} %copy-done, bf16[2,512,6,128]{3,2,1,0:T(8,128)(2,1)S(1)} %reshape.299, ...), kind=kOutput, calls=%fused_computation.13 | convolution fusion | flops 1620048896 | bytes 11539456 | tf_op jit(solution)/shard_map/shij,sjhe->sihe/dot_general | solution.py:34
  258.8 0.1 dynamic_slice.27
  258.8 2.4 copy.51
  261.2 0.1 rev.3
  261.4 0.3 multiply_convert_fusion.1
  261.7 0.1 fusion.51
  261.8 0.6 collective-permute-start.4
  262.4 1.9 collective-permute-done.4
  264.3 1.5 maximum_select_fusion
  (23 shorter events, 0.2 us)
Async XLA Ops:
  6.5 174.9 %all-gather.5.cloned.1.call-start = ((), (), s32[]{:S(2)}) async-start(), calls=%async_computation | async-start | bytes 15040512 | tf_op jit(solution)/shard_map/all_gather | solution.py:72
  8.8 1.9 collective-permute-start.1
  11.8 3.3 %copy-start.3 = (f32[3072]{0:T(1024)S(1)}, f32[3072]{0:T(1024)}, u32[]{:S(2)}) copy-start(f32[3072]{0:T(1024)} %param.9) | copy-start | bytes 36868
  11.8 232.7 %all-gather.7.cloned.1.call-start = ((), (), s32[]{:S(2)}) async-start(), calls=%async_computation.1 | async-start | bytes 1966080 | tf_op jit(solution)/shard_map/all_gather | solution.py:89
  16.7 0.7 copy-start.2
  17.0 5.9 %collective-permute-start = (bf16[512,3072]{0,1:T(8,128)(2,1)S(1)}, bf16[512,3072]{0,1:T(8,128)(2,1)}, u32[]{:S(2)}, u32[]{:S(2)}) collective-permute-start(bf16[512,3072]{0,1:T(8,128)(2,1)S(1)} %bitcast.38), channel_id=1, source_target_pairs={{0,4},{4,0},{1,5},{5,1},{2,6},{6,2},{3,7},{7,3},{8,12},{12,8},{9,1... | collective-permute-start | bytes 9437192 | tf_op jit(solution)/shard_map/ppermute | solution.py:20
  17.4 4.6 %collective-permute-start.2 = (s32[512]{0:T(512)S(1)}, s32[512]{0:T(512)S(1)}, u32[]{:S(2)}, u32[]{:S(2)}) collective-permute-start(s32[512]{0:T(512)S(1)} %bitcast.43), channel_id=1, source_target_pairs={{0,4},{4,0},{1,5},{5,1},{2,6},{6,2},{3,7},{7,3},{8,12},{12,8},{9,1... | collective-permute-start | bytes 6152 | tf_op jit(solution)/shard_map/ppermute | solution.py:20
  209.3 4.0 %copy-start = (bf16[2,512,6,128]{1,0,3,2:T(2,128)(2,1)}, bf16[2,512,6,128]{1,0,3,2:T(2,128)(2,1)S(1)}, u32[]{:S(2)}) copy-start(bf16[2,512,6,128]{1,0,3,2:T(2,128)(2,1)S(1)} %reshape.286) | copy-start | bytes 4718596
  212.0 1.6 copy-start.1
  213.6 1.5 copy-start.5
  250.1 8.7 %copy-start.4 = (f32[1536]{0:T(1024)S(1)}, f32[1536]{0:T(1024)}, u32[]{:S(2)}) copy-start(f32[1536]{0:T(1024)} %param.13) | copy-start | bytes 18436
  258.8 2.5 collective-permute-start.3
  261.8 2.5 collective-permute-start.4
Sparse Core Ops, SparseCore 0:
  11.9 169.4 all-gather.4
  215.2 29.2 all-gather.6

commit v3 on v2

--- a/solution.py
+++ b/solution.py
@@ -86,10 +86,22 @@
 
         tail_keys = jnp.where((docs == last[:, None])[:, :, None, None], key_rows, jnp.zeros_like(key_rows))
         tail = jnp.einsum("bjhe,bjhf->bhef", tail_keys, value_rows, preferred_element_type=jnp.float32)
-        all_tail = lax.all_gather(tail.astype(jnp.bfloat16), "sq")
-        all_last = lax.all_gather(last, "sq")
-        all_block = 2 * jnp.arange(n_sq, dtype=jnp.int32)[:, None] + slot_core[None, :]
-        counted = (all_block[None] < block[:, None, None]) & (all_last[None] == first[:, None, None])
+        tag = jnp.broadcast_to(last.astype(jnp.bfloat16)[:, None, None], (2, 16, HEAD_DIM))
+        message = jnp.concatenate([tail.astype(jnp.bfloat16).reshape(2, heads * HEAD_DIM, HEAD_DIM), tag], axis=1)
+        received = [message] + [
+            lax.ppermute(message, "sq", [(i, i + shift) for i in range(n_sq - shift)])
+            for shift in range(1, n_sq)
+        ]
+        received = jnp.stack(received)
+        all_tail = received[:, :, : heads * HEAD_DIM].reshape(n_sq, 2, heads, HEAD_DIM, HEAD_DIM)
+        all_last = received[:, :, heads * HEAD_DIM, 0].astype(jnp.int32)
+        shifts = jnp.arange(n_sq, dtype=jnp.int32)[:, None]
+        all_block = 2 * (sq - shifts) + slot_core[None, :]
+        counted = (
+            (shifts <= sq)[None]
+            & (all_block[None] < block[:, None, None])
+            & (all_last[None] == first[:, None, None])
+        )
         carried = jnp.einsum(
             "bsk,skhef->bhef",
             counted.astype(jnp.bfloat16),

time: 273 us -> 269 us (0.985)
  waiting for transfers between devices: 183 us -> 175 us
  starting transfers between devices: 1.91 us -> 9.79 us
  blocking collectives: 7.37 us -> 0 us
  other arithmetic: 10.3 us -> 15.6 us
    all_gather x1 -> x0, waiting for transfers between devices: 16.4 us -> none  [shards(): all_tail = lax.all_gather(tail.astype(jnp.bfloat16), 'sq')]
    ppermute x0 -> x3, waiting for transfers between devices: none -> 8.75 us  [shards(): lax.ppermute(message, 'sq', [(i, i + shift) for i in range(n_sq - shift)])]
    ppermute x0 -> x3, starting transfers between devices: none -> 7.91 us  [shards(): lax.ppermute(message, 'sq', [(i, i + shift) for i in range(n_sq - shift)])]
    unnamed x1 -> x0, blocking collectives: 7.37 us -> none
    another operation x0 -> x2, other arithmetic: none -> 3.09 us  [shards(): received = jnp.stack(received)]
  transfers between devices with their start and end apart: 7 -> 9, of which waited for: 6 -> 7; matrix products, arithmetic and copies ran while one was open for 5% -> 5% of each run, Pallas kernels for 0% -> 0%
where the time goes in v3:
time: 269 us
  waiting for transfers between devices  175 us (65%)
  matrix products  32.9 us (12%)
  local copies, waits for them, and re-layouts  22.2 us (8%)
  other arithmetic  15.6 us (6%)
  between operations  13.6 us (5%)
  starting transfers between devices  9.79 us (4%)
    all_gather x1, waiting for transfers between devices, shards(): gathered = lax.all_gather(both, ('sq', 'fsdp'), axis=0, tiled=False)  159 us
    dot_general x1, matrix products, shards(): jnp.dot(pair, gathered.reshape(width, 3 * half), preferred_element_type=j...  19.8 us
    reshape x3, local copies, waits for them, and re-layouts, shards(): query_rows, key_rows, value_rows = [jax.nn.silu(summed[:, part * half:(pa...  9.02 us
    ppermute x3, waiting for transfers between devices, shards(): lax.ppermute(message, 'sq', [(i, i + shift) for i in range(n_sq - shift)])  8.75 us
    dot_general x1, matrix products, mix_block(): jnp.einsum('shij,sjhe->sihe', weights, value_rows, preferred_element_type...  8.7 us
    ppermute x3, starting transfers between devices, shards(): lax.ppermute(message, 'sq', [(i, i + shift) for i in range(n_sq - shift)])  7.91 us
    ppermute x5, waiting for transfers between devices, swap_core(): return lax.ppermute(value, 'core', [(0, 1), (1, 0)])  7.16 us
  transfers between devices with their start and end apart: 9, of which 7 were waited for; matrix products, arithmetic and copies ran while one was open for 5% of the time, Pallas kernels for 0%

profile of v3, /device:TPU:0, one launch (start us, length us, event | category | flops | bytes accessed | tf_op | source)
XLA Modules:
  0.0 268.6 jit_solution(907509501336090205)
XLA Ops:
  6.5 1.0 constant_dynamic-slice_fusion.5
  7.5 1.2 constant_dynamic-slice_fusion.3
  8.8 0.5 collective-permute-start.1
  9.3 1.4 collective-permute-done.1
  10.7 1.0 maximum_select_fusion.1
  11.8 3.2 %copy.123 = bf16[1,512,3072]{1,2,0:T(8,128)(2,1)S(1)} copy(bf16[1,512,3072]{2,1,0:T(8,128)(2,1)} %param.7) | data formatting | bytes 6291456 | tf_op args[0]
  15.0 0.1 mul.75
  15.1 0.7 multiply_reduce_fusion
  15.8 0.9 fusion.9
  16.7 0.3 copy.124
  16.9 0.4 collective-permute-start
  17.4 0.3 collective-permute-start.2
  17.9 0.8 iota_compare_fusion
  18.7 3.3 %collective-permute-done.2 = s32[512]{0:T(512)S(1)} collective-permute-done((s32[512]{0:T(512)S(1)}, s32[512]{0:T(512)S(1)}, u32[]{:S(2)}, u32[]{:S(2)}) %collective-permute-start.2) | collective-permute-done | bytes 2080 | tf_op jit(solution)/shard_map/ppermute | solution.py:20
  21.9 0.2 fusion.41
  22.1 0.1 broadcast_compare_fusion.1
  22.2 0.6 collective-permute-done
  22.8 158.6 %all-gather.2.cloned.1.call-done = bf16[16,2,96,2304]{3,2,1,0:T(8,128)(2,1)} async-done(((bf16[1,2,96,2304]{3,2,1,0:T(8,128)(2,1)}), bf16[16,2,96,2304]{3,2,1,0:T(8,128)(2,1)}) %all-gather.2.cloned.1.call-update) | async-done | bytes 14155792 | tf_op jit(solution)/shard_map/all_gather | solution.py:72
  181.4 19.8 %fusion.1 = f32[1024,2304]{1,0:T(8,128)S(1)} fusion(bf16[3072,2304]{1,0:T(8,128)(2,1)} %bitcast.62, bf16[512,3072]{0,1:T(8,128)(2,1)} %collective-permute-done, bf16[512,3072]{0,1:T(8,128)(2,1)S(1)} %bitcast.48), kind=kOutput, calls=%fused_computation.2 | convolution fusion | flops 14508097536 | bytes 29884416 | tf_op jit(solution)/shard_map/dot_general | solution.py:73
  201.2 3.6 %multiply_convert_fusion.4 = (bf16[1024,768]{1,0:T(8,128)(2,1)S(1)}, bf16[1024,768]{1,0:T(8,128)(2,1)S(1)}, bf16[1024,768]{1,0:T(8,128)(2,1)}) fusion(f32[1024,2304]{1,0:T(8,128)S(1)} %fusion.1), kind=kLoop, calls=%fused_computation.18 | loop fusion | flops 11796480 | bytes 14155776 | tf_op jit(solution)/shard_map/convert_element_type | solution.py:76
  204.7 1.7 copy.127
  206.4 2.9 %reshape.311 = bf16[2,512,6,128]{1,0,3,2:T(2,128)(2,1)S(1)} reshape(bf16[1024,768]{0,1:T(8,128)(2,1)} %copy.127) | data formatting | bytes 3145728 | tf_op jit(solution)/shard_map/reshape | solution.py:77
  209.3 2.8 %reshape.322 = bf16[2,512,6,128]{3,2,1,0:T(8,128)(2,1)} reshape(bf16[1024,768]{1,0:T(8,128)(2,1)S(1)} %get-tuple-element.9) | data formatting | bytes 3145728 | tf_op jit(solution)/shard_map/reshape | solution.py:77
  212.0 1.3 broadcast_select_fusion
  213.3 0.3 copy-done.1
  213.6 0.7 fusion.16
  214.4 0.9 fusion.46
  215.2 3.4 %collective-permute-start.3 = (bf16[2,784,128]{2,1,0:T(8,128)(2,1)}, bf16[2,784,128]{2,1,0:T(8,128)(2,1)S(1)}, u32[]{:S(2)}, u32[]{:S(2)}) collective-permute-start(bf16[2,784,128]{2,1,0:T(8,128)(2,1)} %get-tuple-element.15), channel_id=1, source_target_pairs={{0,8},{8,16},{16,24},{1,9},{9,17},{17,25},{2,10},{10,18},{18,26},{... | collective-permute-start | bytes 1204232 | tf_op jit(solution)/shard_map/ppermute | solution.py:92
  218.6 2.5 collective-permute-start.4
  221.1 2.1 collective-permute-start.5
  223.2 1.2 compare_and_fusion
  224.4 3.4 %reshape.319 = bf16[2,512,6,128]{3,2,1,0:T(8,128)(2,1)S(1)} reshape(bf16[1024,768]{1,0:T(8,128)(2,1)} %get-tuple-element.11) | data formatting | bytes 3145728 | tf_op jit(solution)/shard_map/reshape | solution.py:77
  227.8 0.8 collective-permute-done.3
  228.6 7.9 %collective-permute-done.4 = bf16[2,784,128]{2,1,0:T(8,128)(2,1)S(1)} collective-permute-done((bf16[2,784,128]{2,1,0:T(8,128)(2,1)}, bf16[2,784,128]{2,1,0:T(8,128)(2,1)S(1)}, u32[]{:S(2)}, u32[]{:S(2)}) %collective-permute-start.4) | collective-permute-done | bytes 401440 | tf_op jit(solution)/shard_map/ppermute | solution.py:92
  236.6 0.7 pad_maximum_fusion.5
  237.2 2.2 pad_maximum_fusion
  239.5 0.1 copy.142
  239.6 2.6 copy.134
  242.2 1.4 fusion.15
  243.7 2.3 fusion.25
  246.0 8.7 %fusion.10 = (f32[2,512]{1,0:T(2,128)S(1)}, f32[2,6,128,512]{3,2,1,0:T(8,128)}) fusion(f32[2,6,128,512]{3,2,1,0:T(8,128)} %fusion.25, pred[2,512]{1,0:T(4,128)(4,1)S(1)} %get-tuple-element.22, pred[2,512,512]{2,1,0:T(8,128)(4,1)S(1)} %copy-done.3, bf16[2,512,6,128]{1,0,3,2:T(2,128)(2,1)} %copy-done, bf16[2,512,6,128]{3,2,1,0:T(8,128)(2,1)S(1)} %reshape.319, ...), kind=kOutput, calls=%fused_computation.13 | convolution fusion | flops 1620048896 | bytes 11539456 | tf_op jit(solution)/shard_map/shij,sjhe->sihe/dot_general | solution.py:34
  254.8 2.4 copy.137
  257.2 0.1 rev.3
  257.3 0.3 multiply_convert_fusion.1
  257.7 0.1 fusion.47
  257.8 0.6 collective-permute-start.7
  258.3 1.9 collective-permute-done.7
  260.2 1.5 maximum_select_fusion
  (31 shorter events, 0.5 us)
Async XLA Ops:
  6.5 174.9 %all-gather.2.cloned.1.call-start = ((), (), s32[]{:S(2)}) async-start(), calls=%async_computation | async-start | bytes 15040512 | tf_op jit(solution)/shard_map/all_gather | solution.py:72
  8.8 1.9 collective-permute-start.1
  11.8 3.2 %copy-start.5 = (f32[3072]{0:T(1024)S(1)}, f32[3072]{0:T(1024)}, u32[]{:S(2)}) copy-start(f32[3072]{0:T(1024)} %param.9) | copy-start | bytes 36868
  16.7 0.7 copy-start.4
  16.9 5.9 %collective-permute-start = (bf16[512,3072]{0,1:T(8,128)(2,1)S(1)}, bf16[512,3072]{0,1:T(8,128)(2,1)}, u32[]{:S(2)}, u32[]{:S(2)}) collective-permute-start(bf16[512,3072]{0,1:T(8,128)(2,1)S(1)} %bitcast.47), channel_id=1, source_target_pairs={{0,4},{4,0},{1,5},{5,1},{2,6},{6,2},{3,7},{7,3},{8,12},{12,8},{9,1... | collective-permute-start | bytes 9437192 | tf_op jit(solution)/shard_map/ppermute | solution.py:20
  17.4 4.6 %collective-permute-start.2 = (s32[512]{0:T(512)S(1)}, s32[512]{0:T(512)S(1)}, u32[]{:S(2)}, u32[]{:S(2)}) collective-permute-start(s32[512]{0:T(512)S(1)} %bitcast.58), channel_id=1, source_target_pairs={{0,4},{4,0},{1,5},{5,1},{2,6},{6,2},{3,7},{7,3},{8,12},{12,8},{9,1... | collective-permute-start | bytes 6152 | tf_op jit(solution)/shard_map/ppermute | solution.py:20
  209.3 4.0 %copy-start = (bf16[2,512,6,128]{1,0,3,2:T(2,128)(2,1)}, bf16[2,512,6,128]{1,0,3,2:T(2,128)(2,1)S(1)}, u32[]{:S(2)}) copy-start(bf16[2,512,6,128]{1,0,3,2:T(2,128)(2,1)S(1)} %reshape.311) | copy-start | bytes 4718596
  212.0 1.6 copy-start.1
  213.6 9.5 %copy-start.2 = (pred[512,512]{1,0:T(8,128)(4,1)S(1)}, pred[512,512]{1,0:T(8,128)(4,1)}, u32[]{:S(2)}) copy-start(pred[512,512]{1,0:T(8,128)(4,1)} %iota_compare_fusion) | copy-start | bytes 786436
  215.2 13.4 %collective-permute-start.3 = (bf16[2,784,128]{2,1,0:T(8,128)(2,1)}, bf16[2,784,128]{2,1,0:T(8,128)(2,1)S(1)}, u32[]{:S(2)}, u32[]{:S(2)}) collective-permute-start(bf16[2,784,128]{2,1,0:T(8,128)(2,1)} %get-tuple-element.15), channel_id=1, source_target_pairs={{0,8},{8,16},{16,24},{1,9},{9,17},{17,25},{2,10},{10,18},{18,26},{... | collective-permute-start | bytes 1204232 | tf_op jit(solution)/shard_map/ppermute | solution.py:92
  218.6 17.9 %collective-permute-start.4 = (bf16[2,784,128]{2,1,0:T(8,128)(2,1)}, bf16[2,784,128]{2,1,0:T(8,128)(2,1)S(1)}, u32[]{:S(2)}, u32[]{:S(2)}) collective-permute-start(bf16[2,784,128]{2,1,0:T(8,128)(2,1)} %get-tuple-element.15), channel_id=1, source_target_pairs={{0,16},{8,24},{1,17},{9,25},{2,18},{10,26},{3,19},{11,27},{4,20},{... | collective-permute-start | bytes 1204232 | tf_op jit(solution)/shard_map/ppermute | solution.py:92
  221.1 15.5 %collective-permute-start.5 = (bf16[2,784,128]{2,1,0:T(8,128)(2,1)}, bf16[2,784,128]{2,1,0:T(8,128)(2,1)}, u32[]{:S(2)}, u32[]{:S(2)}) collective-permute-start(bf16[2,784,128]{2,1,0:T(8,128)(2,1)} %get-tuple-element.15), channel_id=1, source_target_pairs={{0,24},{1,25},{2,26},{3,27},{4,28},{5,29},{6,30},{7,31}} | collective-permute-start | bytes 1204232 | tf_op jit(solution)/shard_map/ppermute | solution.py:92
  243.7 2.3 copy-start.3
  246.0 8.7 %copy-start.6 = (f32[1536]{0:T(1024)S(1)}, f32[1536]{0:T(1024)}, u32[]{:S(2)}) copy-start(f32[1536]{0:T(1024)} %param.13) | copy-start | bytes 18436
  254.7 2.5 collective-permute-start.6
  257.8 2.5 collective-permute-start.7
Sparse Core Ops, SparseCore 0:
  11.9 169.4 all-gather.1

commit v4 on v3

--- a/solution.py
+++ b/solution.py
@@ -24,16 +24,17 @@
     return jnp.where(core == 0, jnp.stack([mine, theirs]), jnp.stack([theirs, mine]))
 
 
-def mix_block(query_rows, key_rows, value_rows, doc_rows, past_state, past_doc):
+def local_mix(query_rows, key_rows, value_rows, doc_rows):
     count = doc_rows.shape[1]
     scores = jnp.einsum("sihe,sjhe->shij", query_rows, key_rows, preferred_element_type=jnp.float32)
     row_pos = lax.broadcasted_iota(jnp.int32, (count, count), 0)
     col_pos = lax.broadcasted_iota(jnp.int32, (count, count), 1)
     visible = (row_pos >= col_pos)[None] & (doc_rows[:, :, None] == doc_rows[:, None, :])
     weights = jnp.where(visible[:, None], scores, 0.0).astype(jnp.bfloat16)
-    local_part = jnp.einsum(
-        "shij,sjhe->sihe", weights, value_rows, preferred_element_type=jnp.float32
-    )
+    return jnp.einsum("shij,sjhe->sihe", weights, value_rows, preferred_element_type=jnp.float32)
+
+
+def past_mix(local_part, query_rows, doc_rows, past_state, past_doc):
     from_past = jnp.einsum(
         "sihe,shef->sihf",
         query_rows,
@@ -86,6 +87,8 @@
 
         tail_keys = jnp.where((docs == last[:, None])[:, :, None, None], key_rows, jnp.zeros_like(key_rows))
         tail = jnp.einsum("bjhe,bjhf->bhef", tail_keys, value_rows, preferred_element_type=jnp.float32)
+        local_part = lax.optimization_barrier(local_mix(query_rows, key_rows, value_rows, docs))
+
         tag = jnp.broadcast_to(last.astype(jnp.bfloat16)[:, None, None], (2, 16, HEAD_DIM))
         message = jnp.concatenate([tail.astype(jnp.bfloat16).reshape(2, heads * HEAD_DIM, HEAD_DIM), tag], axis=1)
         received = [message] + [
@@ -109,7 +112,7 @@
             preferred_element_type=jnp.float32,
         )
 
-        mixed = mix_block(query_rows, key_rows, value_rows, docs, carried, first)
+        mixed = past_mix(local_part, query_rows, docs, carried, first)
         mixed = mixed.reshape(2, count, half)
         squares = jnp.sum(mixed * mixed, axis=-1)
         total = squares + swap_core(squares)[::-1]

time: 269 us -> 259 us (0.963)
  waiting for transfers between devices: 175 us -> 167 us
    ppermute x3, waiting for transfers between devices: 8.75 us -> 1.58 us  [shards(): lax.ppermute(message, 'sq', [(i, i + shift) for i in range(n_sq - shift)])]
  transfers between devices with their start and end apart: 9 -> 9, of which waited for: 7 -> 5; matrix products, arithmetic and copies ran while one was open for 5% -> 8% of each run, Pallas kernels for 0% -> 0%
where the time goes in v4:
time: 259 us; the launch traced here: 258 us
  waiting for transfers between devices  167 us (64%)
  matrix products  31.2 us (12%)
  local copies, waits for them, and re-layouts  20.8 us (8%)
  other arithmetic  15.7 us (6%)
  between operations  13.6 us (5%)
  starting transfers between devices  9.83 us (4%)
    all_gather x1, waiting for transfers between devices, shards(): gathered = lax.all_gather(both, ('sq', 'fsdp'), axis=0, tiled=False)  158 us
    dot_general x1, matrix products, shards(): jnp.dot(pair, gathered.reshape(width, 3 * half), preferred_element_type=j...  19.8 us
    reshape x3, local copies, waits for them, and re-layouts, shards(): query_rows, key_rows, value_rows = [jax.nn.silu(summed[:, part * half:(pa...  9.03 us
    dot_general x1, matrix products, local_mix(): jnp.einsum('shij,sjhe->sihe', weights, value_rows, preferred_element_type...  8.43 us
    ppermute x3, starting transfers between devices, shards(): lax.ppermute(message, 'sq', [(i, i + shift) for i in range(n_sq - shift)])  7.9 us
    ppermute x5, waiting for transfers between devices, swap_core(): return lax.ppermute(value, 'core', [(0, 1), (1, 0)])  7.27 us
  transfers between devices with their start and end apart: 9, of which 5 were waited for; matrix products, arithmetic and copies ran while one was open for 8% of the time, Pallas kernels for 0%

profile of v4, /device:TPU:0, one launch (start us, length us, event | category | flops | bytes accessed | tf_op | source)
XLA Modules:
  0.0 257.9 jit_solution(12724733243392806523)
XLA Ops:
  6.5 1.0 constant_dynamic-slice_fusion.5
  7.5 1.2 constant_dynamic-slice_fusion.3
  8.8 0.5 collective-permute-start.1
  9.3 1.4 collective-permute-done.1
  10.7 1.0 maximum_select_fusion.1
  11.8 3.2 %copy.123 = bf16[1,512,3072]{1,2,0:T(8,128)(2,1)S(1)} copy(bf16[1,512,3072]{2,1,0:T(8,128)(2,1)} %param.7) | data formatting | bytes 6291456 | tf_op args[0]
  15.0 0.1 mul.75
  15.1 0.7 multiply_reduce_fusion
  15.8 0.9 fusion.9
  16.7 0.3 copy.124
  16.9 0.4 collective-permute-start
  17.4 0.3 collective-permute-start.2
  17.8 0.1 iota_compare_fusion
  18.0 4.0 %collective-permute-done.2 = s32[512]{0:T(512)S(1)} collective-permute-done((s32[512]{0:T(512)S(1)}, s32[512]{0:T(512)S(1)}, u32[]{:S(2)}, u32[]{:S(2)}) %collective-permute-start.2) | collective-permute-done | bytes 2080 | tf_op jit(solution)/shard_map/ppermute | solution.py:20
  21.9 0.2 fusion.38
  22.2 0.1 broadcast_compare_fusion
  22.3 1.2 compare_and_fusion
  23.5 157.9 %all-gather.2.cloned.1.call-done = bf16[16,2,96,2304]{3,2,1,0:T(8,128)(2,1)} async-done(((bf16[1,2,96,2304]{3,2,1,0:T(8,128)(2,1)}), bf16[16,2,96,2304]{3,2,1,0:T(8,128)(2,1)}) %all-gather.2.cloned.1.call-update) | async-done | bytes 14155792 | tf_op jit(solution)/shard_map/all_gather | solution.py:73
  181.4 19.8 %fusion.1 = f32[1024,2304]{1,0:T(8,128)S(1)} fusion(bf16[3072,2304]{1,0:T(8,128)(2,1)} %bitcast.61, bf16[512,3072]{0,1:T(8,128)(2,1)} %collective-permute-done, bf16[512,3072]{0,1:T(8,128)(2,1)S(1)} %bitcast.48), kind=kOutput, calls=%fused_computation.2 | convolution fusion | flops 14508097536 | bytes 29884416 | tf_op jit(solution)/shard_map/dot_general | solution.py:74
  201.2 3.6 %multiply_convert_fusion.3 = (bf16[1024,768]{1,0:T(8,128)(2,1)}, bf16[1024,768]{1,0:T(8,128)(2,1)S(1)}, bf16[1024,768]{1,0:T(8,128)(2,1)S(1)}) fusion(f32[1024,2304]{1,0:T(8,128)S(1)} %fusion.1), kind=kLoop, calls=%fused_computation.16 | loop fusion | flops 11796480 | bytes 14155776 | tf_op jit(solution)/shard_map/convert_element_type | solution.py:77
  204.7 1.7 copy.127
  206.4 2.9 %reshape.311 = bf16[2,512,6,128]{1,0,3,2:T(2,128)(2,1)S(1)} reshape(bf16[1024,768]{0,1:T(8,128)(2,1)} %copy.127) | data formatting | bytes 3145728 | tf_op jit(solution)/shard_map/reshape | solution.py:78
  209.3 2.8 %reshape.322 = bf16[2,512,6,128]{3,2,1,0:T(8,128)(2,1)} reshape(bf16[1024,768]{1,0:T(8,128)(2,1)S(1)} %get-tuple-element.11) | data formatting | bytes 3145728 | tf_op jit(solution)/shard_map/reshape | solution.py:78
  212.0 1.3 broadcast_select_fusion
  213.3 0.3 copy-done.4
  213.6 0.7 fusion.16
  214.4 0.9 fusion.44
  215.3 3.4 %collective-permute-start.3 = (bf16[2,784,128]{2,1,0:T(8,128)(2,1)}, bf16[2,784,128]{2,1,0:T(8,128)(2,1)S(1)}, u32[]{:S(2)}, u32[]{:S(2)}) collective-permute-start(bf16[2,784,128]{2,1,0:T(8,128)(2,1)} %get-tuple-element.15), channel_id=1, source_target_pairs={{0,8},{8,16},{16,24},{1,9},{9,17},{17,25},{2,10},{10,18},{18,26},{... | collective-permute-start | bytes 1204232 | tf_op jit(solution)/shard_map/ppermute | solution.py:95
  218.6 2.5 collective-permute-start.4
  221.1 2.0 collective-permute-start.5
  223.2 3.4 %reshape.319 = bf16[2,512,6,128]{3,2,1,0:T(8,128)(2,1)S(1)} reshape(bf16[1024,768]{1,0:T(8,128)(2,1)} %get-tuple-element.9) | data formatting | bytes 3145728 | tf_op jit(solution)/shard_map/reshape | solution.py:78
  226.6 8.4 %fusion.10 = f32[2,512,6,128]{1,3,2,0:T(8,128)} fusion(pred[2,512,512]{2,1,0:T(8,128)(4,1)} %compare_and_fusion, bf16[2,512,6,128]{1,0,3,2:T(2,128)(2,1)} %copy-done.2, bf16[2,512,6,128]{3,2,1,0:T(8,128)(2,1)} %reshape.322, bf16[2,512,6,128]{3,2,1,0:T(8,128)(2,1)S(1)} %reshape.319), kind=kOutput, calls=%fused_computation.20 | convolution fusion | flops 1616904192 | bytes 8388608 | tf_op jit(solution)/shard_map/shij,sjhe->sihe/dot_general | solution.py:34
  235.0 1.6 collective-permute-done.4
  236.6 0.7 pad_maximum_fusion.5
  237.3 1.1 pad_maximum_fusion
  238.4 0.1 copy.142
  238.5 1.2 copy.134
  239.7 1.4 fusion.15
  241.2 0.9 multiply_reduce_fusion.1
  242.1 0.1 collective-permute-start.6
  242.2 0.1 dynamic_slice.27
  242.3 2.3 copy.137
  244.6 0.1 rev.3
  244.7 2.2 multiply_convert_fusion.1
  247.0 0.1 fusion.45
  247.1 0.5 collective-permute-start.7
  247.6 1.9 collective-permute-done.7
  249.6 1.5 maximum_select_fusion
  (33 shorter events, 0.4 us)
Async XLA Ops:
  6.5 174.9 %all-gather.2.cloned.1.call-start = ((), (), s32[]{:S(2)}) async-start(), calls=%async_computation | async-start | bytes 15040512 | tf_op jit(solution)/shard_map/all_gather | solution.py:73
  8.8 1.9 collective-permute-start.1
  11.8 3.2 %copy-start.6 = (f32[3072]{0:T(1024)S(1)}, f32[3072]{0:T(1024)}, u32[]{:S(2)}) copy-start(f32[3072]{0:T(1024)} %param.9) | copy-start | bytes 36868
  16.7 0.7 copy-start.5
  16.9 6.6 %collective-permute-start = (bf16[512,3072]{0,1:T(8,128)(2,1)S(1)}, bf16[512,3072]{0,1:T(8,128)(2,1)}, u32[]{:S(2)}, u32[]{:S(2)}) collective-permute-start(bf16[512,3072]{0,1:T(8,128)(2,1)S(1)} %bitcast.47), channel_id=1, source_target_pairs={{0,4},{4,0},{1,5},{5,1},{2,6},{6,2},{3,7},{7,3},{8,12},{12,8},{9,1... | collective-permute-start | bytes 9437192 | tf_op jit(solution)/shard_map/ppermute | solution.py:20
  17.4 4.6 %collective-permute-start.2 = (s32[512]{0:T(512)S(1)}, s32[512]{0:T(512)S(1)}, u32[]{:S(2)}, u32[]{:S(2)}) collective-permute-start(s32[512]{0:T(512)S(1)} %bitcast.57), channel_id=1, source_target_pairs={{0,4},{4,0},{1,5},{5,1},{2,6},{6,2},{3,7},{7,3},{8,12},{12,8},{9,1... | collective-permute-start | bytes 6152 | tf_op jit(solution)/shard_map/ppermute | solution.py:20
  209.3 4.1 %copy-start.2 = (bf16[2,512,6,128]{1,0,3,2:T(2,128)(2,1)}, bf16[2,512,6,128]{1,0,3,2:T(2,128)(2,1)S(1)}, u32[]{:S(2)}) copy-start(bf16[2,512,6,128]{1,0,3,2:T(2,128)(2,1)S(1)} %reshape.311) | copy-start | bytes 4718596
  212.0 1.6 copy-start.4
  215.3 19.7 %collective-permute-start.3 = (bf16[2,784,128]{2,1,0:T(8,128)(2,1)}, bf16[2,784,128]{2,1,0:T(8,128)(2,1)S(1)}, u32[]{:S(2)}, u32[]{:S(2)}) collective-permute-start(bf16[2,784,128]{2,1,0:T(8,128)(2,1)} %get-tuple-element.15), channel_id=1, source_target_pairs={{0,8},{8,16},{16,24},{1,9},{9,17},{17,25},{2,10},{10,18},{18,26},{... | collective-permute-start | bytes 1204232 | tf_op jit(solution)/shard_map/ppermute | solution.py:95
  218.6 18.0 %collective-permute-start.4 = (bf16[2,784,128]{2,1,0:T(8,128)(2,1)}, bf16[2,784,128]{2,1,0:T(8,128)(2,1)S(1)}, u32[]{:S(2)}, u32[]{:S(2)}) collective-permute-start(bf16[2,784,128]{2,1,0:T(8,128)(2,1)} %get-tuple-element.15), channel_id=1, source_target_pairs={{0,16},{8,24},{1,17},{9,25},{2,18},{10,26},{3,19},{11,27},{4,20},{... | collective-permute-start | bytes 1204232 | tf_op jit(solution)/shard_map/ppermute | solution.py:95
  221.1 15.5 %collective-permute-start.5 = (bf16[2,784,128]{2,1,0:T(8,128)(2,1)}, bf16[2,784,128]{2,1,0:T(8,128)(2,1)}, u32[]{:S(2)}, u32[]{:S(2)}) collective-permute-start(bf16[2,784,128]{2,1,0:T(8,128)(2,1)} %get-tuple-element.15), channel_id=1, source_target_pairs={{0,24},{1,25},{2,26},{3,27},{4,28},{5,29},{6,30},{7,31}} | collective-permute-start | bytes 1204232 | tf_op jit(solution)/shard_map/ppermute | solution.py:95
  226.6 8.4 %copy-start = (bf16[2,512,6,128]{3,2,1,0:T(8,128)(2,1)}, bf16[2,512,6,128]{3,2,1,0:T(8,128)(2,1)S(1)}, u32[]{:S(2)}) copy-start(bf16[2,512,6,128]{3,2,1,0:T(8,128)(2,1)S(1)} %reshape.319) | copy-start | bytes 4718596
  238.5 2.7 %copy-start.1 = (bf16[2,512,6,128]{3,2,1,0:T(8,128)(2,1)S(1)}, bf16[2,512,6,128]{3,2,1,0:T(8,128)(2,1)}, u32[]{:S(2)}) copy-start(bf16[2,512,6,128]{3,2,1,0:T(8,128)(2,1)} %copy-done) | copy-start | bytes 4718596
  238.5 2.7 %copy-start.3 = (f32[2,512,6,128]{1,3,2,0:T(8,128)S(1)}, f32[2,512,6,128]{1,3,2,0:T(8,128)}, u32[]{:S(2)}) copy-start(f32[2,512,6,128]{1,3,2,0:T(8,128)} %fusion.10) | copy-start | bytes 9437188
  241.2 1.0 copy-start.7
  242.1 2.5 collective-permute-start.6
  247.1 2.5 collective-permute-start.7
Sparse Core Ops, SparseCore 0:
  11.9 169.4 all-gather.1

commit v5 on v4

--- a/solution.py
+++ b/solution.py
@@ -2,6 +2,83 @@
 import jax.numpy as jnp
 from jax import lax
 from jax.sharding import Mesh, PartitionSpec as P
+from jax.experimental import pallas as pl
+
+
+def _local_kernel(q_ref, k_ref, v_ref, dcol_ref, drow_ref, local_ref):
+    q, k = q_ref[...], k_ref[...]
+    count = q.shape[0]
+    scores = lax.dot_general(q, k, (((1,), (1,)), ((), ())), preferred_element_type=jnp.float32)
+    row_pos = lax.broadcasted_iota(jnp.int32, (count, count), 0)
+    col_pos = lax.broadcasted_iota(jnp.int32, (count, count), 1)
+    visible = (row_pos >= col_pos) & (dcol_ref[...] == drow_ref[...])
+    weights = jnp.where(visible, scores, 0.0).astype(jnp.bfloat16)
+    local_ref[...] = jnp.dot(weights, v_ref[...], preferred_element_type=jnp.float32)
+
+
+def _tail_kernel(k_ref, v_ref, dcol_ref, drow_ref, tail_ref):
+    k, drow = k_ref[...], drow_ref[...]
+    last = drow[:, k.shape[0] - 1:k.shape[0]]
+    tail_keys = jnp.where(dcol_ref[...] == last, k, jnp.zeros_like(k))
+    tail_ref[...] = lax.dot_general(
+        tail_keys, v_ref[...], (((0,), (0,)), ((), ())), preferred_element_type=jnp.float32
+    )
+
+
+def _past_kernel(local_ref, q_ref, state_ref, dcol_ref, drow_ref, out_ref):
+    first = drow_ref[...][:, 0:1]
+    from_past = jnp.dot(q_ref[...], state_ref[...], preferred_element_type=jnp.float32)
+    out_ref[...] = local_ref[...] + jnp.where(dcol_ref[...] == first, from_past, 0.0)
+
+
+def head_specs(count, heads, parts):
+    return [pl.BlockSpec((count, HEAD_DIM), lambda b, h, p=p: (b, p * heads + h)) for p in parts]
+
+
+def doc_specs(count):
+    return [
+        pl.BlockSpec((None, count, 1), lambda b, h: (b, 0, 0)),
+        pl.BlockSpec((None, 1, count), lambda b, h: (b, 0, 0)),
+    ]
+
+
+def state_spec():
+    return pl.BlockSpec((None, None, HEAD_DIM, HEAD_DIM), lambda b, h: (b, h, 0, 0))
+
+
+def local_attention(qkv, docs, heads):
+    blocks, count = docs.shape
+    return pl.pallas_call(
+        _local_kernel,
+        grid=(blocks, heads),
+        in_specs=head_specs(count, heads, (0, 1, 2)) + doc_specs(count),
+        out_specs=head_specs(count, heads, (0,))[0],
+        out_shape=jax.ShapeDtypeStruct((blocks * count, heads * HEAD_DIM), jnp.float32),
+    )(qkv, qkv, qkv, docs.reshape(blocks, count, 1), docs.reshape(blocks, 1, count))
+
+
+def tail_states(qkv, docs, heads):
+    blocks, count = docs.shape
+    return pl.pallas_call(
+        _tail_kernel,
+        grid=(blocks, heads),
+        in_specs=head_specs(count, heads, (1, 2)) + doc_specs(count),
+        out_specs=state_spec(),
+        out_shape=jax.ShapeDtypeStruct((blocks, heads, HEAD_DIM, HEAD_DIM), jnp.float32),
+    )(qkv, qkv, docs.reshape(blocks, count, 1), docs.reshape(blocks, 1, count))
+
+
+def add_past(local, qkv, state, docs, heads):
+    blocks, count = docs.shape
+    tile = head_specs(count, heads, (0,))[0]
+    return pl.pallas_call(
+        _past_kernel,
+        grid=(blocks, heads),
+        in_specs=[tile, tile, state_spec()] + doc_specs(count),
+        out_specs=tile,
+        out_shape=jax.ShapeDtypeStruct(local.shape, jnp.float32),
+        input_output_aliases={0: 0},
+    )(local, qkv, state, docs.reshape(blocks, count, 1), docs.reshape(blocks, 1, count))
 
 HEADS = 12
 HEAD_DIM = 128
@@ -22,27 +99,6 @@
 
 def in_core_order(core, mine, theirs):
     return jnp.where(core == 0, jnp.stack([mine, theirs]), jnp.stack([theirs, mine]))
-
-
-def local_mix(query_rows, key_rows, value_rows, doc_rows):
-    count = doc_rows.shape[1]
-    scores = jnp.einsum("sihe,sjhe->shij", query_rows, key_rows, preferred_element_type=jnp.float32)
-    row_pos = lax.broadcasted_iota(jnp.int32, (count, count), 0)
-    col_pos = lax.broadcasted_iota(jnp.int32, (count, count), 1)
-    visible = (row_pos >= col_pos)[None] & (doc_rows[:, :, None] == doc_rows[:, None, :])
-    weights = jnp.where(visible[:, None], scores, 0.0).astype(jnp.bfloat16)
-    return jnp.einsum("shij,sjhe->sihe", weights, value_rows, preferred_element_type=jnp.float32)
-
-
-def past_mix(local_part, query_rows, doc_rows, past_state, past_doc):
-    from_past = jnp.einsum(
-        "sihe,shef->sihf",
-        query_rows,
-        past_state.astype(jnp.bfloat16),
-        preferred_element_type=jnp.float32,
-    )
-    joined = (doc_rows == past_doc[:, None])[:, :, None, None]
-    return local_part + jnp.where(joined, from_past, 0.0)
 
 
 def make_shards(n_sq, n_fsdp):
@@ -72,12 +128,7 @@
         both = in_core_order(core, mine, swap_core(other))
         gathered = lax.all_gather(both, ("sq", "fsdp"), axis=0, tiled=False)
         summed = jnp.dot(pair, gathered.reshape(width, 3 * half), preferred_element_type=jnp.float32)
-        query_rows, key_rows, value_rows = [
-            jax.nn.silu(summed[:, part * half:(part + 1) * half])
-            .astype(jnp.bfloat16)
-            .reshape(2, count, heads, HEAD_DIM)
-            for part in range(3)
-        ]
+        qkv = jax.nn.silu(summed).astype(jnp.bfloat16)
 
         own_docs = doc_ids[0]
         docs = jnp.stack([own_docs, swap_core(own_docs)])
@@ -85,9 +136,8 @@
         slot_core = jnp.stack([core, 1 - core])
         block = 2 * sq + slot_core
 
-        tail_keys = jnp.where((docs == last[:, None])[:, :, None, None], key_rows, jnp.zeros_like(key_rows))
-        tail = jnp.einsum("bjhe,bjhf->bhef", tail_keys, value_rows, preferred_element_type=jnp.float32)
-        local_part = lax.optimization_barrier(local_mix(query_rows, key_rows, value_rows, docs))
+        tail = tail_states(qkv, docs, heads)
+        local_part = local_attention(qkv, docs, heads)
 
         tag = jnp.broadcast_to(last.astype(jnp.bfloat16)[:, None, None], (2, 16, HEAD_DIM))
         message = jnp.concatenate([tail.astype(jnp.bfloat16).reshape(2, heads * HEAD_DIM, HEAD_DIM), tag], axis=1)
@@ -112,7 +162,7 @@
             preferred_element_type=jnp.float32,
         )
 
-        mixed = past_mix(local_part, query_rows, docs, carried, first)
+        mixed = add_past(local_part, qkv, carried.astype(jnp.bfloat16), docs, heads)
         mixed = mixed.reshape(2, count, half)
         squares = jnp.sum(mixed * mixed, axis=-1)
         total = squares + swap_core(squares)[::-1]

time: 259 us -> 264 us (1.019)
  Pallas kernels: 0 us -> 31.2 us
  local copies, waits for them, and re-layouts: 20.8 us -> 9.84 us
  matrix products: 31.2 us -> 22.6 us
  other arithmetic: 15.7 us -> 8.78 us
    pallas_call x0 -> x3, Pallas kernels: none -> 31.2 us  [the longest x1 11.6 us: local_attention(): pl.pallas_call(_local_kernel, grid=(blocks, heads), in_specs=head_specs(c...]
    dot_general x3 -> x0, matrix products: 10 us -> none  [the longest x1 8.43 us: local_mix(): jnp.einsum('shij,sjhe->sihe', weights, value_rows, preferred_element_type...]
    reshape x4 -> x2, local copies, waits for them, and re-layouts: 11.4 us -> 1.65 us  [the longest x1 1.05 us: local_attention(): docs.reshape(blocks, count, 1)]
  transfers between devices with their start and end apart: 9 -> 9, of which waited for: 5 -> 6; matrix products, arithmetic and copies ran while one was open for 8% -> 3% of each run, Pallas kernels for 0% -> 4%
where the time goes in v5:
time: 264 us; the launch traced here: 263 us
  waiting for transfers between devices  168 us (64%)
  Pallas kernels  31.2 us (12%)
  matrix products  22.6 us (9%)
  between operations  13.6 us (5%)
  local copies, waits for them, and re-layouts  9.84 us (4%)
  starting transfers between devices  9.02 us (3%)
  other arithmetic  8.78 us (3%)
    all_gather x1, waiting for transfers between devices, shards(): gathered = lax.all_gather(both, ('sq', 'fsdp'), axis=0, tiled=False)  157 us
    dot_general x1, matrix products, shards(): jnp.dot(pair, gathered.reshape(width, 3 * half), preferred_element_type=j...  21.2 us
    pallas_call x1, Pallas kernels, local_attention(): pl.pallas_call(_local_kernel, grid=(blocks, heads), in_specs=head_specs(c...  11.6 us
    pallas_call x1, Pallas kernels, tail_states(): pl.pallas_call(_tail_kernel, grid=(blocks, heads), in_specs=head_specs(co...  10.1 us
    pallas_call x1, Pallas kernels, add_past(): pl.pallas_call(_past_kernel, grid=(blocks, heads), in_specs=[tile, tile,...  9.48 us
    ppermute x5, waiting for transfers between devices, swap_core(): return lax.ppermute(value, 'core', [(0, 1), (1, 0)])  8.92 us
    ppermute x3, starting transfers between devices, shards(): lax.ppermute(message, 'sq', [(i, i + shift) for i in range(n_sq - shift)])  7.37 us
  transfers between devices with their start and end apart: 9, of which 6 were waited for; matrix products, arithmetic and copies ran while one was open for 3% of the time, Pallas kernels for 4%

profile of v5, /device:TPU:0, one launch (start us, length us, event | category | flops | bytes accessed | tf_op | source)
XLA Modules:
  0.0 263.1 jit_solution(2924324093923606074)
XLA Ops:
  6.5 1.0 constant_dynamic-slice_fusion.5
  7.5 1.2 constant_dynamic-slice_fusion.3
  8.8 0.5 collective-permute-start.1
  9.3 1.4 collective-permute-done.1
  10.7 1.0 maximum_select_fusion.1
  11.7 0.0 all-gather.2.cloned.1.call-update
  11.8 3.2 %copy.84 = bf16[1,512,3072]{1,2,0:T(8,128)(2,1)S(1)} copy(bf16[1,512,3072]{2,1,0:T(8,128)(2,1)} %param.7) | data formatting | bytes 6291456 | tf_op args[0]
  15.0 0.1 mul.69
  15.1 0.7 multiply_reduce_fusion
  15.8 0.9 fusion.6
  16.7 0.2 copy.85
  16.9 0.4 collective-permute-start
  17.3 0.0 copy-done.1
  17.4 0.4 collective-permute-start.2
  17.7 4.4 %collective-permute-done.2 = s32[512]{0:T(512)S(1)} collective-permute-done((s32[512]{0:T(512)S(1)}, s32[512]{0:T(512)S(1)}, u32[]{:S(2)}, u32[]{:S(2)}) %collective-permute-start.2) | collective-permute-done | bytes 2080 | tf_op jit(solution)/shard_map/ppermute | solution.py:97
  22.1 1.1 copy.86.dcol_ref
  23.2 0.6 reshape.238.drow_ref
  23.8 0.2 fusion.21
  23.9 157.4 %all-gather.2.cloned.1.call-done = bf16[16,2,96,2304]{3,2,1,0:T(8,128)(2,1)} async-done(((bf16[1,2,96,2304]{3,2,1,0:T(8,128)(2,1)}), bf16[16,2,96,2304]{3,2,1,0:T(8,128)(2,1)}) %all-gather.2.cloned.1.call-update) | async-done | bytes 14155792 | tf_op jit(solution)/shard_map/all_gather | solution.py:129
  181.4 21.2 %multiply_convert_fusion.q_ref.k_ref.v_ref = bf16[1024,2304]{1,0:T(8,128)(2,1)} fusion(bf16[3072,2304]{1,0:T(8,128)(2,1)} %bitcast.57, bf16[512,3072]{0,1:T(8,128)(2,1)} %collective-permute-done, bf16[512,3072]{0,1:T(8,128)(2,1)S(1)} %bitcast.42), kind=kOutput, calls=%fused_computation | convolution fusion | flops 14519894016 | bytes 25165824 | tf_op jit(solution)/shard_map/dot_general | solution.py:130
  202.6 10.1 %shard_map.74 = f32[2,6,128,128]{3,2,1,0:T(8,128)} custom-call(bf16[1024,2304]{1,0:T(8,128)(2,1)} %multiply_convert_fusion.q_ref.k_ref.v_ref, bf16[1024,2304]{1,0:T(8,128)(2,1)} %multiply_convert_fusion.q_ref.k_ref.v_ref, s32[2,512,1]{2,1,0:T(8,128)} %copy.86.dcol_ref, s32[2,1,512]{2,1,0:T(1,128)} %reshape.238.drow_ref), custom_call_target="tpu_custom_call" | custom-call | tf_op jit(solution)/shard_map/pallas_call | solution.py:62
  212.7 1.2 convert_element_type.50
  213.9 0.1 broadcast_in_dim.2
  213.9 0.1 fusion.24
  214.1 3.4 %collective-permute-start.3 = (bf16[2,784,128]{2,1,0:T(8,128)(2,1)S(1)}, bf16[2,784,128]{2,1,0:T(8,128)(2,1)S(1)}, u32[]{:S(2)}, u32[]{:S(2)}) collective-permute-start(bf16[2,784,128]{2,1,0:T(8,128)(2,1)S(1)} %get-tuple-element.10), channel_id=1, source_target_pairs={{0,8},{8,16},{16,24},{1,9},{9,17},{17,25},{2,10},{10,18},{18,26},{... | collective-permute-start | bytes 1204232 | tf_op jit(solution)/shard_map/ppermute | solution.py:145
  217.4 2.5 collective-permute-start.4
  219.9 1.5 collective-permute-start.5
  221.5 0.1 broadcast_add_fusion.1
  221.5 0.1 broadcast_add_fusion
  221.6 0.1 fusion.17
  221.7 11.6 %shard_map.73.local_ref = f32[1024,768]{1,0:T(8,128)} custom-call(bf16[1024,2304]{1,0:T(8,128)(2,1)} %multiply_convert_fusion.q_ref.k_ref.v_ref, bf16[1024,2304]{1,0:T(8,128)(2,1)} %multiply_convert_fusion.q_ref.k_ref.v_ref, bf16[1024,2304]{1,0:T(8,128)(2,1)} %multiply_convert_fusion.q_ref.k_ref.v_ref, s32[2,512,1]{2,1,0:T(8,128)} %copy.86.dcol_ref, ...), custom_call_target="tpu_custom_call" | custom-call | tf_op jit(solution)/shard_map/pallas_call | solution.py:51
  233.4 1.7 collective-permute-done.4
  235.1 0.1 pad_maximum_fusion
  235.2 0.1 copy.94
  235.3 1.2 copy.89
  236.5 1.4 convolution_bitcast_fusion
  238.0 0.8 copy.96.state_ref
  238.8 9.5 %shard_map.75 = f32[1024,768]{1,0:T(8,128)} custom-call(f32[1024,768]{1,0:T(8,128)} %shard_map.73.local_ref, bf16[1024,2304]{1,0:T(8,128)(2,1)} %multiply_convert_fusion.q_ref.k_ref.v_ref, bf16[2,6,128,128]{3,2,1,0:T(8,128)(2,1)} %copy.96.state_ref, s32[2,512,1]{2,1,0:T(8,128)} %copy.86.dcol_ref, ...), custom_call_target="tpu_custom_call", output_to_operand_aliasing={{}: (0, {})} | custom-call | tf_op jit(solution)/shard_map/pallas_call | solution.py:74
  248.3 2.3 multiply_reduce_fusion.1
  250.6 0.1 collective-permute-start.6
  250.7 0.1 dynamic_slice.27
  250.8 1.1 collective-permute-done.6
  251.8 0.1 rev.3
  252.0 0.3 multiply_convert_fusion.2
  252.3 0.1 fusion.25
  252.4 0.2 collective-permute-start.7
  252.7 2.1 collective-permute-done.7
  254.8 1.5 maximum_select_fusion
  (21 shorter events, 0.2 us)
Async XLA Ops:
  6.5 174.9 %all-gather.2.cloned.1.call-start = ((), (), s32[]{:S(2)}) async-start(), calls=%async_computation | async-start | bytes 15040512 | tf_op jit(solution)/shard_map/all_gather | solution.py:129
  8.8 1.9 collective-permute-start.1
  11.8 3.2 %copy-start.2 = (f32[3072]{0:T(1024)S(1)}, f32[3072]{0:T(1024)}, u32[]{:S(2)}) copy-start(f32[3072]{0:T(1024)} %param.9) | copy-start | bytes 36868
  16.7 0.7 copy-start.1
  16.9 7.0 %collective-permute-start = (bf16[512,3072]{0,1:T(8,128)(2,1)S(1)}, bf16[512,3072]{0,1:T(8,128)(2,1)}, u32[]{:S(2)}, u32[]{:S(2)}) collective-permute-start(bf16[512,3072]{0,1:T(8,128)(2,1)S(1)} %bitcast.41), channel_id=1, source_target_pairs={{0,4},{4,0},{1,5},{5,1},{2,6},{6,2},{3,7},{7,3},{8,12},{12,8},{9,1... | collective-permute-start | bytes 9437192 | tf_op jit(solution)/shard_map/ppermute | solution.py:97
  17.4 4.7 %collective-permute-start.2 = (s32[512]{0:T(512)S(1)}, s32[512]{0:T(512)S(1)}, u32[]{:S(2)}, u32[]{:S(2)}) collective-permute-start(s32[512]{0:T(512)S(1)} %bitcast.53), channel_id=1, source_target_pairs={{0,4},{4,0},{1,5},{5,1},{2,6},{6,2},{3,7},{7,3},{8,12},{12,8},{9,1... | collective-permute-start | bytes 6152 | tf_op jit(solution)/shard_map/ppermute | solution.py:97
  214.1 19.3 %collective-permute-start.3 = (bf16[2,784,128]{2,1,0:T(8,128)(2,1)S(1)}, bf16[2,784,128]{2,1,0:T(8,128)(2,1)S(1)}, u32[]{:S(2)}, u32[]{:S(2)}) collective-permute-start(bf16[2,784,128]{2,1,0:T(8,128)(2,1)S(1)} %get-tuple-element.10), channel_id=1, source_target_pairs={{0,8},{8,16},{16,24},{1,9},{9,17},{17,25},{2,10},{10,18},{18,26},{... | collective-permute-start | bytes 1204232 | tf_op jit(solution)/shard_map/ppermute | solution.py:145
  217.4 17.6 %collective-permute-start.4 = (bf16[2,784,128]{2,1,0:T(8,128)(2,1)S(1)}, bf16[2,784,128]{2,1,0:T(8,128)(2,1)S(1)}, u32[]{:S(2)}, u32[]{:S(2)}) collective-permute-start(bf16[2,784,128]{2,1,0:T(8,128)(2,1)S(1)} %get-tuple-element.10), channel_id=1, source_target_pairs={{0,16},{8,24},{1,17},{9,25},{2,18},{10,26},{3,19},{11,27},{4,20},{... | collective-permute-start | bytes 1204232 | tf_op jit(solution)/shard_map/ppermute | solution.py:145
  219.9 15.1 %collective-permute-start.5 = (bf16[2,784,128]{2,1,0:T(8,128)(2,1)S(1)}, bf16[2,784,128]{2,1,0:T(8,128)(2,1)S(1)}, u32[]{:S(2)}, u32[]{:S(2)}) collective-permute-start(bf16[2,784,128]{2,1,0:T(8,128)(2,1)S(1)} %get-tuple-element.10), channel_id=1, source_target_pairs={{0,24},{1,25},{2,26},{3,27},{4,28},{5,29},{6,30},{7,31}} | collective-permute-start | bytes 1204232 | tf_op jit(solution)/shard_map/ppermute | solution.py:145
  248.3 2.4 copy-start.3
  248.3 3.7 %copy-start = (f32[1024,768]{1,0:T(8,128)S(1)}, f32[1024,768]{1,0:T(8,128)}, u32[]{:S(2)}) copy-start(f32[1024,768]{1,0:T(8,128)} %shard_map.75) | copy-start | bytes 9437188
  250.6 1.2 collective-permute-start.6
  252.4 2.4 collective-permute-start.7
Sparse Core Ops, SparseCore 0:
  11.9 169.4 all-gather.1

commit v6 on v4

--- a/solution.py
+++ b/solution.py
@@ -2,6 +2,7 @@
 import jax.numpy as jnp
 from jax import lax
 from jax.sharding import Mesh, PartitionSpec as P
+from jax.experimental import pallas as pl
 
 HEADS = 12
 HEAD_DIM = 128
@@ -24,25 +25,88 @@
     return jnp.where(core == 0, jnp.stack([mine, theirs]), jnp.stack([theirs, mine]))
 
 
-def local_mix(query_rows, key_rows, value_rows, doc_rows):
-    count = doc_rows.shape[1]
-    scores = jnp.einsum("sihe,sjhe->shij", query_rows, key_rows, preferred_element_type=jnp.float32)
+def head_columns(ref):
+    return [slice(h * HEAD_DIM, (h + 1) * HEAD_DIM) for h in range(ref.shape[1] // HEAD_DIM)]
+
+
+def _local_kernel(q_ref, k_ref, v_ref, dcol_ref, drow_ref, local_ref):
+    count = q_ref.shape[0]
     row_pos = lax.broadcasted_iota(jnp.int32, (count, count), 0)
     col_pos = lax.broadcasted_iota(jnp.int32, (count, count), 1)
-    visible = (row_pos >= col_pos)[None] & (doc_rows[:, :, None] == doc_rows[:, None, :])
-    weights = jnp.where(visible[:, None], scores, 0.0).astype(jnp.bfloat16)
-    return jnp.einsum("shij,sjhe->sihe", weights, value_rows, preferred_element_type=jnp.float32)
-
-
-def past_mix(local_part, query_rows, doc_rows, past_state, past_doc):
-    from_past = jnp.einsum(
-        "sihe,shef->sihf",
-        query_rows,
-        past_state.astype(jnp.bfloat16),
-        preferred_element_type=jnp.float32,
-    )
-    joined = (doc_rows == past_doc[:, None])[:, :, None, None]
-    return local_part + jnp.where(joined, from_past, 0.0)
+    visible = (row_pos >= col_pos) & (dcol_ref[...] == drow_ref[...])
+    for cols in head_columns(q_ref):
+        scores = lax.dot_general(
+            q_ref[:, cols], k_ref[:, cols], (((1,), (1,)), ((), ())), preferred_element_type=jnp.float32
+        )
+        weights = jnp.where(visible, scores, 0.0).astype(jnp.bfloat16)
+        local_ref[:, cols] = jnp.dot(weights, v_ref[:, cols], preferred_element_type=jnp.float32)
+
+
+def _tail_kernel(k_ref, v_ref, dcol_ref, drow_ref, tail_ref):
+    count = k_ref.shape[0]
+    ending = dcol_ref[...] == drow_ref[...][:, count - 1:count]
+    for h, cols in enumerate(head_columns(k_ref)):
+        tail_keys = jnp.where(ending, k_ref[:, cols], jnp.zeros((count, HEAD_DIM), k_ref.dtype))
+        tail_ref[h] = lax.dot_general(
+            tail_keys, v_ref[:, cols], (((0,), (0,)), ((), ())), preferred_element_type=jnp.float32
+        )
+
+
+def _past_kernel(local_ref, q_ref, state_ref, dcol_ref, drow_ref, out_ref):
+    joined = dcol_ref[...] == drow_ref[...][:, 0:1]
+    for h, cols in enumerate(head_columns(q_ref)):
+        from_past = jnp.dot(q_ref[:, cols], state_ref[h], preferred_element_type=jnp.float32)
+        out_ref[:, cols] = local_ref[:, cols] + jnp.where(joined, from_past, 0.0)
+
+
+def head_specs(count, heads, parts):
+    return [pl.BlockSpec((count, heads * HEAD_DIM), lambda b, p=p: (b, p)) for p in parts]
+
+
+def doc_specs(count):
+    return [
+        pl.BlockSpec((None, count, 1), lambda b: (b, 0, 0)),
+        pl.BlockSpec((None, 1, count), lambda b: (b, 0, 0)),
+    ]
+
+
+def state_spec(heads):
+    return pl.BlockSpec((None, heads, HEAD_DIM, HEAD_DIM), lambda b: (b, 0, 0, 0))
+
+
+def local_attention(qkv, docs, heads):
+    blocks, count = docs.shape
+    return pl.pallas_call(
+        _local_kernel,
+        grid=(blocks,),
+        in_specs=head_specs(count, heads, (0, 1, 2)) + doc_specs(count),
+        out_specs=head_specs(count, heads, (0,))[0],
+        out_shape=jax.ShapeDtypeStruct((blocks * count, heads * HEAD_DIM), jnp.float32),
+    )(qkv, qkv, qkv, docs.reshape(blocks, count, 1), docs.reshape(blocks, 1, count))
+
+
+def tail_states(qkv, docs, heads):
+    blocks, count = docs.shape
+    return pl.pallas_call(
+        _tail_kernel,
+        grid=(blocks,),
+        in_specs=head_specs(count, heads, (1, 2)) + doc_specs(count),
+        out_specs=state_spec(heads),
+        out_shape=jax.ShapeDtypeStruct((blocks, heads, HEAD_DIM, HEAD_DIM), jnp.float32),
+    )(qkv, qkv, docs.reshape(blocks, count, 1), docs.reshape(blocks, 1, count))
+
+
+def add_past(local, qkv, state, docs, heads):
+    blocks, count = docs.shape
+    tile = head_specs(count, heads, (0,))[0]
+    return pl.pallas_call(
+        _past_kernel,
+        grid=(blocks,),
+        in_specs=[tile, tile, state_spec(heads)] + doc_specs(count),
+        out_specs=tile,
+        out_shape=jax.ShapeDtypeStruct(local.shape, jnp.float32),
+        input_output_aliases={0: 0},
+    )(local, qkv, state, docs.reshape(blocks, count, 1), docs.reshape(blocks, 1, count))
 
 
 def make_shards(n_sq, n_fsdp):
@@ -72,12 +136,7 @@
         both = in_core_order(core, mine, swap_core(other))
         gathered = lax.all_gather(both, ("sq", "fsdp"), axis=0, tiled=False)
         summed = jnp.dot(pair, gathered.reshape(width, 3 * half), preferred_element_type=jnp.float32)
-        query_rows, key_rows, value_rows = [
-            jax.nn.silu(summed[:, part * half:(part + 1) * half])
-            .astype(jnp.bfloat16)
-            .reshape(2, count, heads, HEAD_DIM)
-            for part in range(3)
-        ]
+        qkv = jax.nn.silu(summed).astype(jnp.bfloat16)
 
         own_docs = doc_ids[0]
         docs = jnp.stack([own_docs, swap_core(own_docs)])
@@ -85,9 +144,8 @@
         slot_core = jnp.stack([core, 1 - core])
         block = 2 * sq + slot_core
 
-        tail_keys = jnp.where((docs == last[:, None])[:, :, None, None], key_rows, jnp.zeros_like(key_rows))
-        tail = jnp.einsum("bjhe,bjhf->bhef", tail_keys, value_rows, preferred_element_type=jnp.float32)
-        local_part = lax.optimization_barrier(local_mix(query_rows, key_rows, value_rows, docs))
+        tail = tail_states(qkv, docs, heads)
+        local_part = local_attention(qkv, docs, heads)
 
         tag = jnp.broadcast_to(last.astype(jnp.bfloat16)[:, None, None], (2, 16, HEAD_DIM))
         message = jnp.concatenate([tail.astype(jnp.bfloat16).reshape(2, heads * HEAD_DIM, HEAD_DIM), tag], axis=1)
@@ -112,7 +170,7 @@
             preferred_element_type=jnp.float32,
         )
 
-        mixed = past_mix(local_part, query_rows, docs, carried, first)
+        mixed = add_past(local_part, qkv, carried.astype(jnp.bfloat16), docs, heads)
         mixed = mixed.reshape(2, count, half)
         squares = jnp.sum(mixed * mixed, axis=-1)
         total = squares + swap_core(squares)[::-1]

time: 259 us -> 252 us (0.973)
  Pallas kernels: 0 us -> 14.2 us
  local copies, waits for them, and re-layouts: 20.8 us -> 9.84 us
  matrix products: 31.2 us -> 22.6 us
  other arithmetic: 15.7 us -> 8.78 us
  waiting for transfers between devices: 167 us -> 173 us
    pallas_call x0 -> x3, Pallas kernels: none -> 14.2 us  [the longest x1 6.7 us: local_attention(): pl.pallas_call(_local_kernel, grid=(blocks,), in_specs=head_specs(count,...]
    dot_general x3 -> x0, matrix products: 10 us -> none  [the longest x1 8.43 us: local_mix(): jnp.einsum('shij,sjhe->sihe', weights, value_rows, preferred_element_type...]
    reshape x4 -> x2, local copies, waits for them, and re-layouts: 11.4 us -> 1.65 us  [the longest x1 1.05 us: local_attention(): docs.reshape(blocks, count, 1)]
    ppermute x3, waiting for transfers between devices: 1.58 us -> 6.64 us  [shards(): lax.ppermute(message, 'sq', [(i, i + shift) for i in range(n_sq - shift)])]
  transfers between devices with their start and end apart: 9 -> 9, of which waited for: 5 -> 6; matrix products, arithmetic and copies ran while one was open for 8% -> 3% of each run, Pallas kernels for 0% -> 3%
where the time goes in v6:
time: 252 us; the launch traced here: 251 us
  waiting for transfers between devices  173 us (69%)
  matrix products  22.6 us (9%)
  Pallas kernels  14.2 us (6%)
  between operations  13.6 us (5%)
  local copies, waits for them, and re-layouts  9.84 us (4%)
  starting transfers between devices  9.02 us (4%)
  other arithmetic  8.78 us (3%)
    all_gather x1, waiting for transfers between devices, shards(): gathered = lax.all_gather(both, ('sq', 'fsdp'), axis=0, tiled=False)  157 us
    dot_general x1, matrix products, shards(): jnp.dot(pair, gathered.reshape(width, 3 * half), preferred_element_type=j...  21.2 us
    ppermute x5, waiting for transfers between devices, swap_core(): return lax.ppermute(value, 'core', [(0, 1), (1, 0)])  8.92 us
    ppermute x3, starting transfers between devices, shards(): lax.ppermute(message, 'sq', [(i, i + shift) for i in range(n_sq - shift)])  7.37 us
    pallas_call x1, Pallas kernels, local_attention(): pl.pallas_call(_local_kernel, grid=(blocks,), in_specs=head_specs(count,...  6.7 us
    ppermute x3, waiting for transfers between devices, shards(): lax.ppermute(message, 'sq', [(i, i + shift) for i in range(n_sq - shift)])  6.64 us
  transfers between devices with their start and end apart: 9, of which 6 were waited for; matrix products, arithmetic and copies ran while one was open for 3% of the time, Pallas kernels for 3%

profile of v6, /device:TPU:0, one launch (start us, length us, event | category | flops | bytes accessed | tf_op | source)
XLA Modules:
  0.0 251.1 jit_solution(5916072630308587447)
XLA Ops:
  6.5 1.0 constant_dynamic-slice_fusion.5
  7.5 1.2 constant_dynamic-slice_fusion.3
  8.8 0.5 collective-permute-start.1
  9.3 1.4 collective-permute-done.1
  10.7 1.0 maximum_select_fusion.1
  11.7 0.0 all-gather.2.cloned.1.call-update
  11.8 3.2 %copy.84 = bf16[1,512,3072]{1,2,0:T(8,128)(2,1)S(1)} copy(bf16[1,512,3072]{2,1,0:T(8,128)(2,1)} %param.7) | data formatting | bytes 6291456 | tf_op args[0]
  15.0 0.1 mul.69
  15.1 0.7 multiply_reduce_fusion
  15.8 0.9 fusion.6
  16.7 0.2 copy.85
  16.9 0.4 collective-permute-start
  17.3 0.0 copy-done.1
  17.4 0.4 collective-permute-start.2
  17.7 4.4 %collective-permute-done.2 = s32[512]{0:T(512)S(1)} collective-permute-done((s32[512]{0:T(512)S(1)}, s32[512]{0:T(512)S(1)}, u32[]{:S(2)}, u32[]{:S(2)}) %collective-permute-start.2) | collective-permute-done | bytes 2080 | tf_op jit(solution)/shard_map/ppermute | solution.py:21
  22.1 1.1 copy.86.dcol_ref
  23.2 0.6 reshape.238.drow_ref
  23.8 0.2 fusion.21
  23.9 157.4 %all-gather.2.cloned.1.call-done = bf16[16,2,96,2304]{3,2,1,0:T(8,128)(2,1)} async-done(((bf16[1,2,96,2304]{3,2,1,0:T(8,128)(2,1)}), bf16[16,2,96,2304]{3,2,1,0:T(8,128)(2,1)}) %all-gather.2.cloned.1.call-update) | async-done | bytes 14155792 | tf_op jit(solution)/shard_map/all_gather | solution.py:137
  181.4 21.2 %multiply_convert_fusion.q_ref.k_ref.v_ref = bf16[1024,2304]{1,0:T(8,128)(2,1)} fusion(bf16[3072,2304]{1,0:T(8,128)(2,1)} %bitcast.57, bf16[512,3072]{0,1:T(8,128)(2,1)} %collective-permute-done, bf16[512,3072]{0,1:T(8,128)(2,1)S(1)} %bitcast.42), kind=kOutput, calls=%fused_computation | convolution fusion | flops 14519894016 | bytes 25165824 | tf_op jit(solution)/shard_map/dot_general | solution.py:138
  202.6 3.4 %shard_map.74 = f32[2,6,128,128]{3,2,1,0:T(8,128)} custom-call(bf16[1024,2304]{1,0:T(8,128)(2,1)} %multiply_convert_fusion.q_ref.k_ref.v_ref, bf16[1024,2304]{1,0:T(8,128)(2,1)} %multiply_convert_fusion.q_ref.k_ref.v_ref, s32[2,512,1]{2,1,0:T(8,128)} %copy.86.dcol_ref, s32[2,1,512]{2,1,0:T(1,128)} %reshape.238.drow_ref), custom_call_target="tpu_custom_call" | custom-call | tf_op jit(solution)/shard_map/pallas_call | solution.py:90
  206.0 1.2 convert_element_type.50
  207.2 0.1 broadcast_in_dim.2
  207.3 0.1 fusion.24
  207.4 3.4 %collective-permute-start.3 = (bf16[2,784,128]{2,1,0:T(8,128)(2,1)S(1)}, bf16[2,784,128]{2,1,0:T(8,128)(2,1)S(1)}, u32[]{:S(2)}, u32[]{:S(2)}) collective-permute-start(bf16[2,784,128]{2,1,0:T(8,128)(2,1)S(1)} %get-tuple-element.10), channel_id=1, source_target_pairs={{0,8},{8,16},{16,24},{1,9},{9,17},{17,25},{2,10},{10,18},{18,26},{... | collective-permute-start | bytes 1204232 | tf_op jit(solution)/shard_map/ppermute | solution.py:153
  210.8 2.5 collective-permute-start.4
  213.3 1.5 collective-permute-start.5
  214.8 0.1 broadcast_add_fusion.1
  214.9 0.1 broadcast_add_fusion
  214.9 0.1 fusion.17
  215.1 6.7 %shard_map.73.local_ref = f32[1024,768]{1,0:T(8,128)} custom-call(bf16[1024,2304]{1,0:T(8,128)(2,1)} %multiply_convert_fusion.q_ref.k_ref.v_ref, bf16[1024,2304]{1,0:T(8,128)(2,1)} %multiply_convert_fusion.q_ref.k_ref.v_ref, bf16[1024,2304]{1,0:T(8,128)(2,1)} %multiply_convert_fusion.q_ref.k_ref.v_ref, s32[2,512,1]{2,1,0:T(8,128)} %copy.86.dcol_ref, ...), custom_call_target="tpu_custom_call" | custom-call | tf_op jit(solution)/shard_map/pallas_call | solution.py:79
  221.8 6.6 %collective-permute-done.4 = bf16[2,784,128]{2,1,0:T(8,128)(2,1)S(1)} collective-permute-done((bf16[2,784,128]{2,1,0:T(8,128)(2,1)S(1)}, bf16[2,784,128]{2,1,0:T(8,128)(2,1)S(1)}, u32[]{:S(2)}, u32[]{:S(2)}) %collective-permute-start.4) | collective-permute-done | bytes 401440 | tf_op jit(solution)/shard_map/ppermute | solution.py:153
  228.4 0.1 pad_maximum_fusion
  228.5 0.1 copy.94
  228.7 1.2 copy.89
  229.9 1.4 convolution_bitcast_fusion
  231.3 0.8 copy.96.state_ref
  232.1 4.1 %shard_map.75 = f32[1024,768]{1,0:T(8,128)} custom-call(f32[1024,768]{1,0:T(8,128)} %shard_map.73.local_ref, bf16[1024,2304]{1,0:T(8,128)(2,1)} %multiply_convert_fusion.q_ref.k_ref.v_ref, bf16[2,6,128,128]{3,2,1,0:T(8,128)(2,1)} %copy.96.state_ref, s32[2,512,1]{2,1,0:T(8,128)} %copy.86.dcol_ref, ...), custom_call_target="tpu_custom_call", output_to_operand_aliasing={{}: (0, {})} | custom-call | tf_op jit(solution)/shard_map/pallas_call | solution.py:102
  236.2 2.3 multiply_reduce_fusion.1
  238.6 0.1 collective-permute-start.6
  238.7 0.1 dynamic_slice.27
  238.7 1.1 collective-permute-done.6
  239.8 0.1 rev.3
  239.9 0.3 multiply_convert_fusion.2
  240.3 0.1 fusion.25
  240.4 0.2 collective-permute-start.7
  240.6 2.1 collective-permute-done.7
  242.7 1.5 maximum_select_fusion
  (21 shorter events, 0.2 us)
Async XLA Ops:
  6.5 174.9 %all-gather.2.cloned.1.call-start = ((), (), s32[]{:S(2)}) async-start(), calls=%async_computation | async-start | bytes 15040512 | tf_op jit(solution)/shard_map/all_gather | solution.py:137
  8.8 1.9 collective-permute-start.1
  11.8 3.2 %copy-start.2 = (f32[3072]{0:T(1024)S(1)}, f32[3072]{0:T(1024)}, u32[]{:S(2)}) copy-start(f32[3072]{0:T(1024)} %param.9) | copy-start | bytes 36868
  16.7 0.7 copy-start.1
  16.9 7.0 %collective-permute-start = (bf16[512,3072]{0,1:T(8,128)(2,1)S(1)}, bf16[512,3072]{0,1:T(8,128)(2,1)}, u32[]{:S(2)}, u32[]{:S(2)}) collective-permute-start(bf16[512,3072]{0,1:T(8,128)(2,1)S(1)} %bitcast.41), channel_id=1, source_target_pairs={{0,4},{4,0},{1,5},{5,1},{2,6},{6,2},{3,7},{7,3},{8,12},{12,8},{9,1... | collective-permute-start | bytes 9437192 | tf_op jit(solution)/shard_map/ppermute | solution.py:21
  17.4 4.7 %collective-permute-start.2 = (s32[512]{0:T(512)S(1)}, s32[512]{0:T(512)S(1)}, u32[]{:S(2)}, u32[]{:S(2)}) collective-permute-start(s32[512]{0:T(512)S(1)} %bitcast.53), channel_id=1, source_target_pairs={{0,4},{4,0},{1,5},{5,1},{2,6},{6,2},{3,7},{7,3},{8,12},{12,8},{9,1... | collective-permute-start | bytes 6152 | tf_op jit(solution)/shard_map/ppermute | solution.py:21
  207.4 14.4 %collective-permute-start.3 = (bf16[2,784,128]{2,1,0:T(8,128)(2,1)S(1)}, bf16[2,784,128]{2,1,0:T(8,128)(2,1)S(1)}, u32[]{:S(2)}, u32[]{:S(2)}) collective-permute-start(bf16[2,784,128]{2,1,0:T(8,128)(2,1)S(1)} %get-tuple-element.10), channel_id=1, source_target_pairs={{0,8},{8,16},{16,24},{1,9},{9,17},{17,25},{2,10},{10,18},{18,26},{... | collective-permute-start | bytes 1204232 | tf_op jit(solution)/shard_map/ppermute | solution.py:153
  210.8 17.6 %collective-permute-start.4 = (bf16[2,784,128]{2,1,0:T(8,128)(2,1)S(1)}, bf16[2,784,128]{2,1,0:T(8,128)(2,1)S(1)}, u32[]{:S(2)}, u32[]{:S(2)}) collective-permute-start(bf16[2,784,128]{2,1,0:T(8,128)(2,1)S(1)} %get-tuple-element.10), channel_id=1, source_target_pairs={{0,16},{8,24},{1,17},{9,25},{2,18},{10,26},{3,19},{11,27},{4,20},{... | collective-permute-start | bytes 1204232 | tf_op jit(solution)/shard_map/ppermute | solution.py:153
  213.3 15.1 %collective-permute-start.5 = (bf16[2,784,128]{2,1,0:T(8,128)(2,1)S(1)}, bf16[2,784,128]{2,1,0:T(8,128)(2,1)S(1)}, u32[]{:S(2)}, u32[]{:S(2)}) collective-permute-start(bf16[2,784,128]{2,1,0:T(8,128)(2,1)S(1)} %get-tuple-element.10), channel_id=1, source_target_pairs={{0,24},{1,25},{2,26},{3,27},{4,28},{5,29},{6,30},{7,31}} | collective-permute-start | bytes 1204232 | tf_op jit(solution)/shard_map/ppermute | solution.py:153
  236.2 2.4 copy-start.3
  236.2 3.7 %copy-start = (f32[1024,768]{1,0:T(8,128)S(1)}, f32[1024,768]{1,0:T(8,128)}, u32[]{:S(2)}) copy-start(f32[1024,768]{1,0:T(8,128)} %shard_map.75) | copy-start | bytes 9437188
  238.6 1.2 collective-permute-start.6
  240.4 2.4 collective-permute-start.7
Sparse Core Ops, SparseCore 0:
  11.9 169.4 all-gather.1

commit v7 on v6

--- a/solution.py
+++ b/solution.py
@@ -74,29 +74,29 @@
     return pl.BlockSpec((None, heads, HEAD_DIM, HEAD_DIM), lambda b: (b, 0, 0, 0))
 
 
-def local_attention(qkv, docs, heads):
+def local_attention(query, key_value, docs, heads):
     blocks, count = docs.shape
     return pl.pallas_call(
         _local_kernel,
         grid=(blocks,),
-        in_specs=head_specs(count, heads, (0, 1, 2)) + doc_specs(count),
+        in_specs=head_specs(count, heads, (0, 0, 1)) + doc_specs(count),
         out_specs=head_specs(count, heads, (0,))[0],
         out_shape=jax.ShapeDtypeStruct((blocks * count, heads * HEAD_DIM), jnp.float32),
-    )(qkv, qkv, qkv, docs.reshape(blocks, count, 1), docs.reshape(blocks, 1, count))
-
-
-def tail_states(qkv, docs, heads):
+    )(query, key_value, key_value, docs.reshape(blocks, count, 1), docs.reshape(blocks, 1, count))
+
+
+def tail_states(key_value, docs, heads):
     blocks, count = docs.shape
     return pl.pallas_call(
         _tail_kernel,
         grid=(blocks,),
-        in_specs=head_specs(count, heads, (1, 2)) + doc_specs(count),
+        in_specs=head_specs(count, heads, (0, 1)) + doc_specs(count),
         out_specs=state_spec(heads),
         out_shape=jax.ShapeDtypeStruct((blocks, heads, HEAD_DIM, HEAD_DIM), jnp.float32),
-    )(qkv, qkv, docs.reshape(blocks, count, 1), docs.reshape(blocks, 1, count))
-
-
-def add_past(local, qkv, state, docs, heads):
+    )(key_value, key_value, docs.reshape(blocks, count, 1), docs.reshape(blocks, 1, count))
+
+
+def add_past(local, query, state, docs, heads):
     blocks, count = docs.shape
     tile = head_specs(count, heads, (0,))[0]
     return pl.pallas_call(
@@ -106,7 +106,7 @@
         out_specs=tile,
         out_shape=jax.ShapeDtypeStruct(local.shape, jnp.float32),
         input_output_aliases={0: 0},
-    )(local, qkv, state, docs.reshape(blocks, count, 1), docs.reshape(blocks, 1, count))
+    )(local, query, state, docs.reshape(blocks, count, 1), docs.reshape(blocks, 1, count))
 
 
 def make_shards(n_sq, n_fsdp):
@@ -135,8 +135,13 @@
         mine, other = halves(core * half), halves((1 - core) * half)
         both = in_core_order(core, mine, swap_core(other))
         gathered = lax.all_gather(both, ("sq", "fsdp"), axis=0, tiled=False)
-        summed = jnp.dot(pair, gathered.reshape(width, 3 * half), preferred_element_type=jnp.float32)
-        qkv = jax.nn.silu(summed).astype(jnp.bfloat16)
+        weights = gathered.reshape(width, 3 * half)
+
+        def project(columns):
+            summed = jnp.dot(pair, columns, preferred_element_type=jnp.float32)
+            return jax.nn.silu(summed).astype(jnp.bfloat16)
+
+        key_value = project(weights[:, half:])
 
         own_docs = doc_ids[0]
         docs = jnp.stack([own_docs, swap_core(own_docs)])
@@ -144,8 +149,9 @@
         slot_core = jnp.stack([core, 1 - core])
         block = 2 * sq + slot_core
 
-        tail = tail_states(qkv, docs, heads)
-        local_part = local_attention(qkv, docs, heads)
+        tail = tail_states(key_value, docs, heads)
+        query = project(weights[:, :half])
+        local_part = local_attention(query, key_value, docs, heads)
 
         tag = jnp.broadcast_to(last.astype(jnp.bfloat16)[:, None, None], (2, 16, HEAD_DIM))
         message = jnp.concatenate([tail.astype(jnp.bfloat16).reshape(2, heads * HEAD_DIM, HEAD_DIM), tag], axis=1)
@@ -170,7 +176,7 @@
             preferred_element_type=jnp.float32,
         )
 
-        mixed = add_past(local_part, qkv, carried.astype(jnp.bfloat16), docs, heads)
+        mixed = add_past(local_part, query, carried.astype(jnp.bfloat16), docs, heads)
         mixed = mixed.reshape(2, count, half)
         squares = jnp.sum(mixed * mixed, axis=-1)
         total = squares + swap_core(squares)[::-1]

time: 252 us -> 252 us (level)
  waiting for transfers between devices: 173 us -> 165 us
  other arithmetic: 8.78 us -> 12.6 us
  matrix products: 22.6 us -> 26 us
    ppermute x3, waiting for transfers between devices: 6.64 us -> 0.01 us  [shards(): lax.ppermute(message, 'sq', [(i, i + shift) for i in range(n_sq - shift)])]
    dot_general x1 -> x2, matrix products: 21.2 us -> 24.6 us  [project(): summed = jnp.dot(pair, columns, preferred_element_type=jnp.float32)]
  transfers between devices with their start and end apart: 9 -> 9, of which waited for: 6 -> 5; matrix products, arithmetic and copies ran while one was open for 3% -> 7% of each run, Pallas kernels for 3% -> 3%
where the time goes in v7:
time: 252 us
  waiting for transfers between devices  165 us (65%)
  matrix products  26 us (10%)
  Pallas kernels  14.2 us (6%)
  between operations  13.6 us (5%)
  other arithmetic  12.6 us (5%)
  starting transfers between devices  10.2 us (4%)
  local copies, waits for them, and re-layouts  9.94 us (4%)
    all_gather x1, waiting for transfers between devices, shards(): gathered = lax.all_gather(both, ('sq', 'fsdp'), axis=0, tiled=False)  157 us
    dot_general x2, matrix products, project(): summed = jnp.dot(pair, columns, preferred_element_type=jnp.float32)  24.6 us
    ppermute x3, starting transfers between devices, shards(): lax.ppermute(message, 'sq', [(i, i + shift) for i in range(n_sq - shift)])  8.64 us
    ppermute x5, waiting for transfers between devices, swap_core(): return lax.ppermute(value, 'core', [(0, 1), (1, 0)])  8.18 us
    pallas_call x1, Pallas kernels, local_attention(): pl.pallas_call(_local_kernel, grid=(blocks,), in_specs=head_specs(count,...  6.69 us
  transfers between devices with their start and end apart: 9, of which 5 were waited for; matrix products, arithmetic and copies ran while one was open for 7% of the time, Pallas kernels for 3%

profile of v7, /device:TPU:0, one launch (start us, length us, event | category | flops | bytes accessed | tf_op | source)
XLA Modules:
  0.0 251.6 jit_solution(1316263665953531635)
XLA Ops:
  6.5 1.0 constant_dynamic-slice_fusion.5
  7.6 1.2 constant_dynamic-slice_fusion.3
  8.8 0.5 collective-permute-start.1
  9.3 1.4 collective-permute-done.1
  10.7 1.0 maximum_select_fusion.1
  11.8 0.1 mul.73
  11.9 3.2 %copy.84 = bf16[1,512,3072]{1,2,0:T(8,128)(2,1)S(1)} copy(bf16[1,512,3072]{2,1,0:T(8,128)(2,1)} %param.7) | data formatting | bytes 6291456 | tf_op args[0]
  15.1 0.7 multiply_reduce_fusion
  15.8 0.9 fusion.6
  16.7 0.3 copy.85
  17.0 0.4 collective-permute-start
  17.5 0.3 collective-permute-start.2
  17.7 0.1 broadcast_add_fusion.1
  17.8 0.1 broadcast_add_fusion
  17.9 0.5 iota_compare_fusion
  18.4 3.6 %collective-permute-done.2 = s32[512]{0:T(512)S(1)} collective-permute-done((s32[512]{0:T(512)S(1)}, s32[512]{0:T(512)S(1)}, u32[]{:S(2)}, u32[]{:S(2)}) %collective-permute-start.2) | collective-permute-done | bytes 2080 | tf_op jit(solution)/shard_map/ppermute | solution.py:21
  22.0 1.0 copy.86.dcol_ref
  23.1 0.6 reshape.238.drow_ref
  23.7 0.2 fusion.23
  23.9 0.7 fusion.19
  24.6 156.8 %all-gather.2.cloned.1.call-done = bf16[16,2,96,2304]{3,2,1,0:T(8,128)(2,1)} async-done(((bf16[1,2,96,2304]{3,2,1,0:T(8,128)(2,1)}), bf16[16,2,96,2304]{3,2,1,0:T(8,128)(2,1)}) %all-gather.2.cloned.1.call-update) | async-done | bytes 14155792 | tf_op jit(solution)/shard_map/all_gather | solution.py:137
  181.4 15.4 %multiply_convert_fusion.k_ref.v_ref = bf16[1024,1536]{1,0:T(8,128)(2,1)} fusion(bf16[3072,2304]{1,0:T(8,128)(2,1)} %bitcast.51, bf16[512,3072]{0,1:T(8,128)(2,1)} %collective-permute-done, bf16[512,3072]{0,1:T(8,128)(2,1)S(1)} %bitcast.41), kind=kOutput, calls=%fused_computation.3 | convolution fusion | flops 9684123648 | bytes 18874368 | tf_op jit(solution)/shard_map/dot_general | solution.py:141
  196.8 3.4 %shard_map.74 = f32[2,6,128,128]{3,2,1,0:T(8,128)} custom-call(bf16[1024,1536]{1,0:T(8,128)(2,1)} %multiply_convert_fusion.k_ref.v_ref, bf16[1024,1536]{1,0:T(8,128)(2,1)} %multiply_convert_fusion.k_ref.v_ref, s32[2,512,1]{2,1,0:T(8,128)} %copy.86.dcol_ref, s32[2,1,512]{2,1,0:T(1,128)} %reshape.238.drow_ref), custom_call_target="tpu_custom_call" | custom-call | tf_op jit(solution)/shard_map/pallas_call | solution.py:90
  200.3 1.2 convert_element_type.54
  201.5 0.1 broadcast_in_dim.2
  201.5 0.9 fusion.27
  202.4 4.2 %collective-permute-start.5 = (bf16[2,784,128]{2,1,0:T(8,128)(2,1)}, bf16[2,784,128]{2,1,0:T(8,128)(2,1)}, u32[]{:S(2)}, u32[]{:S(2)}) collective-permute-start(bf16[2,784,128]{2,1,0:T(8,128)(2,1)} %get-tuple-element.10), channel_id=1, source_target_pairs={{0,24},{1,25},{2,26},{3,27},{4,28},{5,29},{6,30},{7,31}} | collective-permute-start | bytes 1204232 | tf_op jit(solution)/shard_map/ppermute | solution.py:159
  206.5 2.0 collective-permute-start.4
  208.6 2.5 collective-permute-start.3
  211.0 9.2 %multiply_convert_fusion.3.q_ref = bf16[1024,768]{1,0:T(8,128)(2,1)} fusion(bf16[3072,2304]{1,0:T(8,128)(2,1)} %bitcast.52, bf16[512,3072]{0,1:T(8,128)(2,1)} %collective-permute-done, bf16[512,3072]{0,1:T(8,128)(2,1)S(1)} %bitcast.42), kind=kOutput, calls=%fused_computation.11 | convolution fusion | flops 4848353280 | bytes 12582912 | tf_op jit(solution)/shard_map/dot_general | solution.py:141
  220.2 6.7 %shard_map.73.local_ref = f32[1024,768]{1,0:T(8,128)} custom-call(bf16[1024,768]{1,0:T(8,128)(2,1)} %multiply_convert_fusion.3.q_ref, bf16[1024,1536]{1,0:T(8,128)(2,1)} %multiply_convert_fusion.k_ref.v_ref, bf16[1024,1536]{1,0:T(8,128)(2,1)} %multiply_convert_fusion.k_ref.v_ref, s32[2,512,1]{2,1,0:T(8,128)} %copy.86.dcol_ref, s32[2,1,512]{2,1,0:T(1,128)} %reshape.238.drow_ref), custom_call_target="tpu_custom_call" | custom-call | tf_op jit(solution)/shard_map/pallas_call | solution.py:79
  226.9 1.4 pad_maximum_fusion.3
  228.3 0.7 pad_maximum_fusion.10
  229.0 1.2 copy.89
  230.2 0.1 copy.94
  230.3 1.5 convolution_bitcast_fusion
  231.8 0.8 copy.96.state_ref
  232.6 4.1 %shard_map.75 = f32[1024,768]{1,0:T(8,128)} custom-call(f32[1024,768]{1,0:T(8,128)} %shard_map.73.local_ref, bf16[1024,768]{1,0:T(8,128)(2,1)} %multiply_convert_fusion.3.q_ref, bf16[2,6,128,128]{3,2,1,0:T(8,128)(2,1)} %copy.96.state_ref, s32[2,512,1]{2,1,0:T(8,128)} %copy.86.dcol_ref, s32[2,1,512]{2,1,0:T(1,128)} %reshape.238.drow_ref), custom_call_target="tpu_custom_call", output_to_operand_aliasing={{}: (0, {})} | custom-call | tf_op jit(solution)/shard_map/pallas_call | solution.py:102
  236.7 2.3 multiply_reduce_fusion.1
  239.1 0.1 collective-permute-start.6
  239.1 0.1 dynamic_slice.27
  239.2 1.1 collective-permute-done.6
  240.3 0.1 rev.3
  240.4 0.3 multiply_convert_fusion.2
  240.8 0.1 fusion.28
  240.9 0.2 collective-permute-start.7
  241.1 2.1 collective-permute-done.7
  243.2 1.5 maximum_select_fusion
  (26 shorter events, 0.2 us)
Async XLA Ops:
  6.5 5.2 %copy-start.2 = (f32[3072]{0:T(1024)S(1)}, f32[3072]{0:T(1024)}, u32[]{:S(2)}) copy-start(f32[3072]{0:T(1024)} %param.9) | copy-start | bytes 36868
  6.5 174.9 %all-gather.2.cloned.1.call-start = ((), (), s32[]{:S(2)}) async-start(), calls=%async_computation | async-start | bytes 15040512 | tf_op jit(solution)/shard_map/all_gather | solution.py:137
  8.8 1.9 collective-permute-start.1
  16.7 0.8 copy-start.1
  17.0 7.5 %collective-permute-start = (bf16[512,3072]{0,1:T(8,128)(2,1)S(1)}, bf16[512,3072]{0,1:T(8,128)(2,1)}, u32[]{:S(2)}, u32[]{:S(2)}) collective-permute-start(bf16[512,3072]{0,1:T(8,128)(2,1)S(1)} %bitcast.40), channel_id=1, source_target_pairs={{0,4},{4,0},{1,5},{5,1},{2,6},{6,2},{3,7},{7,3},{8,12},{12,8},{9,1... | collective-permute-start | bytes 9437192 | tf_op jit(solution)/shard_map/ppermute | solution.py:21
  17.5 4.6 %collective-permute-start.2 = (s32[512]{0:T(512)S(1)}, s32[512]{0:T(512)S(1)}, u32[]{:S(2)}, u32[]{:S(2)}) collective-permute-start(s32[512]{0:T(512)S(1)} %bitcast.47), channel_id=1, source_target_pairs={{0,4},{4,0},{1,5},{5,1},{2,6},{6,2},{3,7},{7,3},{8,12},{12,8},{9,1... | collective-permute-start | bytes 6152 | tf_op jit(solution)/shard_map/ppermute | solution.py:21
  202.4 24.5 %collective-permute-start.5 = (bf16[2,784,128]{2,1,0:T(8,128)(2,1)}, bf16[2,784,128]{2,1,0:T(8,128)(2,1)}, u32[]{:S(2)}, u32[]{:S(2)}) collective-permute-start(bf16[2,784,128]{2,1,0:T(8,128)(2,1)} %get-tuple-element.10), channel_id=1, source_target_pairs={{0,24},{1,25},{2,26},{3,27},{4,28},{5,29},{6,30},{7,31}} | collective-permute-start | bytes 1204232 | tf_op jit(solution)/shard_map/ppermute | solution.py:159
  206.5 20.3 %collective-permute-start.4 = (bf16[2,784,128]{2,1,0:T(8,128)(2,1)}, bf16[2,784,128]{2,1,0:T(8,128)(2,1)}, u32[]{:S(2)}, u32[]{:S(2)}) collective-permute-start(bf16[2,784,128]{2,1,0:T(8,128)(2,1)} %get-tuple-element.10), channel_id=1, source_target_pairs={{0,16},{8,24},{1,17},{9,25},{2,18},{10,26},{3,19},{11,27},{4,20},{... | collective-permute-start | bytes 1204232 | tf_op jit(solution)/shard_map/ppermute | solution.py:159
  208.6 18.3 %collective-permute-start.3 = (bf16[2,784,128]{2,1,0:T(8,128)(2,1)}, bf16[2,784,128]{2,1,0:T(8,128)(2,1)}, u32[]{:S(2)}, u32[]{:S(2)}) collective-permute-start(bf16[2,784,128]{2,1,0:T(8,128)(2,1)} %get-tuple-element.10), channel_id=1, source_target_pairs={{0,8},{8,16},{16,24},{1,9},{9,17},{17,25},{2,10},{10,18},{18,26},{... | collective-permute-start | bytes 1204232 | tf_op jit(solution)/shard_map/ppermute | solution.py:159
  228.3 2.1 copy-start.4
  228.3 2.1 copy-start.5
  236.7 2.4 copy-start.3
  236.7 3.7 %copy-start = (f32[1024,768]{1,0:T(8,128)S(1)}, f32[1024,768]{1,0:T(8,128)}, u32[]{:S(2)}) copy-start(f32[1024,768]{1,0:T(8,128)} %shard_map.75) | copy-start | bytes 9437188
  239.1 1.2 collective-permute-start.6
  240.9 2.4 collective-permute-start.7
Sparse Core Ops, SparseCore 0:
  11.9 169.4 all-gather.1

commit v8 on v6

--- a/solution.py
+++ b/solution.py
@@ -52,11 +52,15 @@
         )
 
 
-def _past_kernel(local_ref, q_ref, state_ref, dcol_ref, drow_ref, out_ref):
+def _past_kernel(local_ref, q_ref, state_ref, dcol_ref, drow_ref, out_ref, squares_ref):
     joined = dcol_ref[...] == drow_ref[...][:, 0:1]
+    squares = jnp.zeros((q_ref.shape[0], 1), jnp.float32)
     for h, cols in enumerate(head_columns(q_ref)):
         from_past = jnp.dot(q_ref[:, cols], state_ref[h], preferred_element_type=jnp.float32)
-        out_ref[:, cols] = local_ref[:, cols] + jnp.where(joined, from_past, 0.0)
+        mixed = local_ref[:, cols] + jnp.where(joined, from_past, 0.0)
+        out_ref[:, cols] = mixed
+        squares = squares + jnp.sum(mixed * mixed, axis=1, keepdims=True)
+    squares_ref[...] = squares
 
 
 def head_specs(count, heads, parts):
@@ -103,8 +107,11 @@
         _past_kernel,
         grid=(blocks,),
         in_specs=[tile, tile, state_spec(heads)] + doc_specs(count),
-        out_specs=tile,
-        out_shape=jax.ShapeDtypeStruct(local.shape, jnp.float32),
+        out_specs=[tile, pl.BlockSpec((count, 1), lambda b: (b, 0))],
+        out_shape=[
+            jax.ShapeDtypeStruct(local.shape, jnp.float32),
+            jax.ShapeDtypeStruct((blocks * count, 1), jnp.float32),
+        ],
         input_output_aliases={0: 0},
     )(local, qkv, state, docs.reshape(blocks, count, 1), docs.reshape(blocks, 1, count))
 
@@ -170,9 +177,9 @@
             preferred_element_type=jnp.float32,
         )
 
-        mixed = add_past(local_part, qkv, carried.astype(jnp.bfloat16), docs, heads)
+        mixed, squares = add_past(local_part, qkv, carried.astype(jnp.bfloat16), docs, heads)
         mixed = mixed.reshape(2, count, half)
-        squares = jnp.sum(mixed * mixed, axis=-1)
+        squares = squares.reshape(2, count)
         total = squares + swap_core(squares)[::-1]
         scale = lax.rsqrt(total / ATTN_WIDTH + EPS)
         gain = lax.dynamic_slice_in_dim(out_gain, core * half, half)

time: 252 us -> 253 us (level)
  no operation moved by 1% of the time
where the time goes in v8:
time: 253 us; the launch traced here: 252 us
  waiting for transfers between devices  173 us (68%)
  matrix products  22.6 us (9%)
  Pallas kernels  14.3 us (6%)
  between operations  13.6 us (5%)
  local copies, waits for them, and re-layouts  9.84 us (4%)
  other arithmetic  9.6 us (4%)
  starting transfers between devices  9.02 us (4%)
    all_gather x1, waiting for transfers between devices, shards(): gathered = lax.all_gather(both, ('sq', 'fsdp'), axis=0, tiled=False)  157 us
    dot_general x1, matrix products, shards(): jnp.dot(pair, gathered.reshape(width, 3 * half), preferred_element_type=j...  21.2 us
    ppermute x5, waiting for transfers between devices, swap_core(): return lax.ppermute(value, 'core', [(0, 1), (1, 0)])  8.92 us
    ppermute x3, starting transfers between devices, shards(): lax.ppermute(message, 'sq', [(i, i + shift) for i in range(n_sq - shift)])  7.37 us
    pallas_call x1, Pallas kernels, local_attention(): pl.pallas_call(_local_kernel, grid=(blocks,), in_specs=head_specs(count,...  6.7 us
    ppermute x3, waiting for transfers between devices, shards(): lax.ppermute(message, 'sq', [(i, i + shift) for i in range(n_sq - shift)])  6.64 us
  transfers between devices with their start and end apart: 9, of which 6 were waited for; matrix products, arithmetic and copies ran while one was open for 3% of the time, Pallas kernels for 3%

profile of v8, /device:TPU:0, one launch (start us, length us, event | category | flops | bytes accessed | tf_op | source)
XLA Modules:
  0.0 252.0 jit_solution(15348388656396389137)
XLA Ops:
  6.5 1.0 constant_dynamic-slice_fusion.5
  7.5 1.2 constant_dynamic-slice_fusion.3
  8.8 0.5 collective-permute-start.1
  9.3 1.4 collective-permute-done.1
  10.7 1.0 maximum_select_fusion.1
  11.7 0.0 all-gather.2.cloned.1.call-update
  11.8 3.2 %copy.84 = bf16[1,512,3072]{1,2,0:T(8,128)(2,1)S(1)} copy(bf16[1,512,3072]{2,1,0:T(8,128)(2,1)} %param.7) | data formatting | bytes 6291456 | tf_op args[0]
  15.0 0.1 mul.65
  15.1 0.7 multiply_reduce_fusion
  15.8 0.9 fusion.6
  16.7 0.2 copy.85
  16.9 0.4 collective-permute-start
  17.3 0.0 copy-done
  17.4 0.4 collective-permute-start.2
  17.7 4.4 %collective-permute-done.2 = s32[512]{0:T(512)S(1)} collective-permute-done((s32[512]{0:T(512)S(1)}, s32[512]{0:T(512)S(1)}, u32[]{:S(2)}, u32[]{:S(2)}) %collective-permute-start.2) | collective-permute-done | bytes 2080 | tf_op jit(solution)/shard_map/ppermute | solution.py:21
  22.1 1.1 copy.86.dcol_ref
  23.2 0.6 reshape.240.drow_ref
  23.8 0.2 fusion.21
  23.9 157.4 %all-gather.2.cloned.1.call-done = bf16[16,2,96,2304]{3,2,1,0:T(8,128)(2,1)} async-done(((bf16[1,2,96,2304]{3,2,1,0:T(8,128)(2,1)}), bf16[16,2,96,2304]{3,2,1,0:T(8,128)(2,1)}) %all-gather.2.cloned.1.call-update) | async-done | bytes 14155792 | tf_op jit(solution)/shard_map/all_gather | solution.py:144
  181.4 21.2 %multiply_convert_fusion.q_ref.k_ref.v_ref = bf16[1024,2304]{1,0:T(8,128)(2,1)} fusion(bf16[3072,2304]{1,0:T(8,128)(2,1)} %bitcast.57, bf16[512,3072]{0,1:T(8,128)(2,1)} %collective-permute-done, bf16[512,3072]{0,1:T(8,128)(2,1)S(1)} %bitcast.42), kind=kOutput, calls=%fused_computation | convolution fusion | flops 14519894016 | bytes 25165824 | tf_op jit(solution)/shard_map/dot_general | solution.py:145
  202.6 3.4 %shard_map.74 = f32[2,6,128,128]{3,2,1,0:T(8,128)} custom-call(bf16[1024,2304]{1,0:T(8,128)(2,1)} %multiply_convert_fusion.q_ref.k_ref.v_ref, bf16[1024,2304]{1,0:T(8,128)(2,1)} %multiply_convert_fusion.q_ref.k_ref.v_ref, s32[2,512,1]{2,1,0:T(8,128)} %copy.86.dcol_ref, s32[2,1,512]{2,1,0:T(1,128)} %reshape.240.drow_ref), custom_call_target="tpu_custom_call" | custom-call | tf_op jit(solution)/shard_map/pallas_call | solution.py:94
  206.0 1.2 convert_element_type.50
  207.2 0.1 broadcast_in_dim.2
  207.3 0.1 fusion.24
  207.4 3.4 %collective-permute-start.3 = (bf16[2,784,128]{2,1,0:T(8,128)(2,1)S(1)}, bf16[2,784,128]{2,1,0:T(8,128)(2,1)S(1)}, u32[]{:S(2)}, u32[]{:S(2)}) collective-permute-start(bf16[2,784,128]{2,1,0:T(8,128)(2,1)S(1)} %get-tuple-element.14), channel_id=1, source_target_pairs={{0,8},{8,16},{16,24},{1,9},{9,17},{17,25},{2,10},{10,18},{18,26},{... | collective-permute-start | bytes 1204232 | tf_op jit(solution)/shard_map/ppermute | solution.py:160
  210.8 2.5 collective-permute-start.4
  213.3 1.5 collective-permute-start.5
  214.8 0.1 broadcast_add_fusion.1
  214.9 0.1 broadcast_add_fusion
  214.9 0.1 fusion.17
  215.1 6.7 %shard_map.73.local_ref = f32[1024,768]{1,0:T(8,128)} custom-call(bf16[1024,2304]{1,0:T(8,128)(2,1)} %multiply_convert_fusion.q_ref.k_ref.v_ref, bf16[1024,2304]{1,0:T(8,128)(2,1)} %multiply_convert_fusion.q_ref.k_ref.v_ref, bf16[1024,2304]{1,0:T(8,128)(2,1)} %multiply_convert_fusion.q_ref.k_ref.v_ref, s32[2,512,1]{2,1,0:T(8,128)} %copy.86.dcol_ref, ...), custom_call_target="tpu_custom_call" | custom-call | tf_op jit(solution)/shard_map/pallas_call | solution.py:83
  221.8 6.6 %collective-permute-done.4 = bf16[2,784,128]{2,1,0:T(8,128)(2,1)S(1)} collective-permute-done((bf16[2,784,128]{2,1,0:T(8,128)(2,1)S(1)}, bf16[2,784,128]{2,1,0:T(8,128)(2,1)S(1)}, u32[]{:S(2)}, u32[]{:S(2)}) %collective-permute-start.4) | collective-permute-done | bytes 401440 | tf_op jit(solution)/shard_map/ppermute | solution.py:160
  228.4 0.1 pad_maximum_fusion
  228.5 0.1 copy.94
  228.7 1.2 copy.89
  229.9 1.4 convolution_bitcast_fusion
  231.3 0.8 copy.96.state_ref
  232.1 4.2 %shard_map.75 = (f32[1024,768]{1,0:T(8,128)}, f32[1024,1]{1,0:T(8,128)}) custom-call(f32[1024,768]{1,0:T(8,128)} %shard_map.73.local_ref, bf16[1024,2304]{1,0:T(8,128)(2,1)} %multiply_convert_fusion.q_ref.k_ref.v_ref, bf16[2,6,128,128]{3,2,1,0:T(8,128)(2,1)} %copy.96.state_ref, s32[2,512,1]{2,1,0:T(8,128)} %copy.86.dcol_ref, ...), custom_call_target="tpu_custom_call", output_to_operand_aliasing={{0}: (0, {})} | custom-call | tf_op jit(solution)/shard_map/pallas_call | solution.py:106
  236.3 1.2 reduce.3
  237.6 0.1 collective-permute-start.6
  237.7 0.1 dynamic_slice.27
  237.8 1.1 collective-permute-done.6
  238.8 0.1 rev.3
  239.0 2.2 multiply_convert_fusion.2
  241.2 0.1 fusion.25
  241.3 0.2 collective-permute-start.7
  241.5 2.1 collective-permute-done.7
  243.6 1.5 maximum_select_fusion
  (19 shorter events, 0.1 us)
Async XLA Ops:
  6.5 174.9 %all-gather.2.cloned.1.call-start = ((), (), s32[]{:S(2)}) async-start(), calls=%async_computation | async-start | bytes 15040512 | tf_op jit(solution)/shard_map/all_gather | solution.py:144
  8.8 1.9 collective-permute-start.1
  11.8 3.2 %copy-start.1 = (f32[3072]{0:T(1024)S(1)}, f32[3072]{0:T(1024)}, u32[]{:S(2)}) copy-start(f32[3072]{0:T(1024)} %param.9) | copy-start | bytes 36868
  16.7 0.7 copy-start
  16.9 7.0 %collective-permute-start = (bf16[512,3072]{0,1:T(8,128)(2,1)S(1)}, bf16[512,3072]{0,1:T(8,128)(2,1)}, u32[]{:S(2)}, u32[]{:S(2)}) collective-permute-start(bf16[512,3072]{0,1:T(8,128)(2,1)S(1)} %bitcast.41), channel_id=1, source_target_pairs={{0,4},{4,0},{1,5},{5,1},{2,6},{6,2},{3,7},{7,3},{8,12},{12,8},{9,1... | collective-permute-start | bytes 9437192 | tf_op jit(solution)/shard_map/ppermute | solution.py:21
  17.4 4.7 %collective-permute-start.2 = (s32[512]{0:T(512)S(1)}, s32[512]{0:T(512)S(1)}, u32[]{:S(2)}, u32[]{:S(2)}) collective-permute-start(s32[512]{0:T(512)S(1)} %bitcast.53), channel_id=1, source_target_pairs={{0,4},{4,0},{1,5},{5,1},{2,6},{6,2},{3,7},{7,3},{8,12},{12,8},{9,1... | collective-permute-start | bytes 6152 | tf_op jit(solution)/shard_map/ppermute | solution.py:21
  207.4 14.4 %collective-permute-start.3 = (bf16[2,784,128]{2,1,0:T(8,128)(2,1)S(1)}, bf16[2,784,128]{2,1,0:T(8,128)(2,1)S(1)}, u32[]{:S(2)}, u32[]{:S(2)}) collective-permute-start(bf16[2,784,128]{2,1,0:T(8,128)(2,1)S(1)} %get-tuple-element.14), channel_id=1, source_target_pairs={{0,8},{8,16},{16,24},{1,9},{9,17},{17,25},{2,10},{10,18},{18,26},{... | collective-permute-start | bytes 1204232 | tf_op jit(solution)/shard_map/ppermute | solution.py:160
  210.8 17.6 %collective-permute-start.4 = (bf16[2,784,128]{2,1,0:T(8,128)(2,1)S(1)}, bf16[2,784,128]{2,1,0:T(8,128)(2,1)S(1)}, u32[]{:S(2)}, u32[]{:S(2)}) collective-permute-start(bf16[2,784,128]{2,1,0:T(8,128)(2,1)S(1)} %get-tuple-element.14), channel_id=1, source_target_pairs={{0,16},{8,24},{1,17},{9,25},{2,18},{10,26},{3,19},{11,27},{4,20},{... | collective-permute-start | bytes 1204232 | tf_op jit(solution)/shard_map/ppermute | solution.py:160
  213.3 15.1 %collective-permute-start.5 = (bf16[2,784,128]{2,1,0:T(8,128)(2,1)S(1)}, bf16[2,784,128]{2,1,0:T(8,128)(2,1)S(1)}, u32[]{:S(2)}, u32[]{:S(2)}) collective-permute-start(bf16[2,784,128]{2,1,0:T(8,128)(2,1)S(1)} %get-tuple-element.14), channel_id=1, source_target_pairs={{0,24},{1,25},{2,26},{3,27},{4,28},{5,29},{6,30},{7,31}} | collective-permute-start | bytes 1204232 | tf_op jit(solution)/shard_map/ppermute | solution.py:160
  232.1 5.5 %copy-start.2 = (f32[1536]{0:T(1024)S(1)}, f32[1536]{0:T(1024)}, u32[]{:S(2)}) copy-start(f32[1536]{0:T(1024)} %param.13) | copy-start | bytes 18436
  237.6 1.2 collective-permute-start.6
  241.3 2.4 collective-permute-start.7
Sparse Core Ops, SparseCore 0:
  11.9 169.4 all-gather.1

commit v9 on v6

--- a/solution.py
+++ b/solution.py
@@ -118,11 +118,6 @@
         half = ATTN_WIDTH // 2
         heads = HEADS // 2
 
-        normed = norm_rows(tokens[0].astype(jnp.float32), norm_gain).astype(jnp.bfloat16)
-        normed = normed.reshape(count, n_sq, 2, n_fsdp, rows).transpose(0, 1, 3, 2, 4)
-        normed = normed.reshape(count, width)
-        pair = jnp.concatenate([normed, swap_core(normed)], axis=0)
-
         def halves(start):
             return jnp.concatenate(
                 [
@@ -132,10 +127,18 @@
                 axis=1,
             )
 
-        mine, other = halves(core * half), halves((1 - core) * half)
-        both = in_core_order(core, mine, swap_core(other))
+        both = jnp.stack([halves(core * half), halves((1 - core) * half)])
         gathered = lax.all_gather(both, ("sq", "fsdp"), axis=0, tiled=False)
-        summed = jnp.dot(pair, gathered.reshape(width, 3 * half), preferred_element_type=jnp.float32)
+        own_rows = gathered[:, 0].reshape(n_sq * n_fsdp * rows, 3 * half)
+        sibling_rows = swap_core(gathered[:, 1]).reshape(n_sq * n_fsdp * rows, 3 * half)
+
+        normed = norm_rows(tokens[0].astype(jnp.float32), norm_gain).astype(jnp.bfloat16)
+        pair = jnp.concatenate([normed, swap_core(normed)], axis=0).reshape(2 * count, n_sq, 2, n_fsdp, rows)
+        by_core = [pair[:, :, slot].reshape(2 * count, n_sq * n_fsdp * rows) for slot in range(2)]
+        own_features = jnp.where(core == 0, by_core[0], by_core[1])
+        sibling_features = jnp.where(core == 0, by_core[1], by_core[0])
+        summed = jnp.dot(own_features, own_rows, preferred_element_type=jnp.float32)
+        summed = summed + jnp.dot(sibling_features, sibling_rows, preferred_element_type=jnp.float32)
         qkv = jax.nn.silu(summed).astype(jnp.bfloat16)
 
         own_docs = doc_ids[0]

time: 252 us -> 283 us (1.12)
  waiting for transfers between devices: 173 us -> 188 us
  local copies, waits for them, and re-layouts: 9.84 us -> 19.7 us
  other arithmetic: 8.78 us -> 13.8 us
    squeeze x0 -> x1, local copies, waits for them, and re-layouts: none -> 10.2 us  [shards(): gathered[:, 1]]
    all_gather x1, waiting for transfers between devices: 157 us -> 166 us  [shards(): gathered = lax.all_gather(both, ('sq', 'fsdp'), axis=0, tiled=False)]
    ppermute x5, waiting for transfers between devices: 8.92 us -> 14.2 us  [swap_core(): return lax.ppermute(value, 'core', [(0, 1), (1, 0)])]
    concatenate x1, other arithmetic: 0.03 us -> 2.87 us  [shards(): jnp.concatenate([normed, swap_core(normed)], axis=0)]
    dot_general x1 -> x2, matrix products: 21.2 us -> 23.7 us  [the longest x1 13.7 us: shards(): jnp.dot(sibling_features, sibling_rows, preferred_element_type=jnp.float32)]
  transfers between devices with their start and end apart: 9 -> 9, of which waited for: 6 -> 6; matrix products, arithmetic and copies ran while one was open for 3% -> 8% of each run, Pallas kernels for 3% -> 2%
where the time goes in v9:
time: 283 us; the launch traced here: 282 us
  waiting for transfers between devices  188 us (66%)
  matrix products  25.2 us (9%)
  local copies, waits for them, and re-layouts  19.7 us (7%)
  Pallas kernels  14.3 us (5%)
  other arithmetic  13.8 us (5%)
  between operations  13.6 us (5%)
  starting transfers between devices  8.19 us (3%)
    all_gather x1, waiting for transfers between devices, shards(): gathered = lax.all_gather(both, ('sq', 'fsdp'), axis=0, tiled=False)  166 us
    ppermute x5, waiting for transfers between devices, swap_core(): return lax.ppermute(value, 'core', [(0, 1), (1, 0)])  14.2 us
    dot_general x1, matrix products, shards(): jnp.dot(sibling_features, sibling_rows, preferred_element_type=jnp.float32)  13.7 us
    squeeze x1, local copies, waits for them, and re-layouts, shards(): gathered[:, 1]  10.2 us
    dot_general x1, matrix products, shards(): summed = jnp.dot(own_features, own_rows, preferred_element_type=jnp.float32)  10 us
    ppermute x3, starting transfers between devices, shards(): lax.ppermute(message, 'sq', [(i, i + shift) for i in range(n_sq - shift)])  7.36 us
    ppermute x3, waiting for transfers between devices, shards(): lax.ppermute(message, 'sq', [(i, i + shift) for i in range(n_sq - shift)])  7.35 us
    pallas_call x1, Pallas kernels, local_attention(): pl.pallas_call(_local_kernel, grid=(blocks,), in_specs=head_specs(count,...  6.7 us
  transfers between devices with their start and end apart: 9, of which 6 were waited for; matrix products, arithmetic and copies ran while one was open for 8% of the time, Pallas kernels for 2%

profile of v9, /device:TPU:0, one launch (start us, length us, event | category | flops | bytes accessed | tf_op | source)
XLA Modules:
  0.0 282.2 jit_solution(9697572369916260997)
XLA Ops:
  6.5 1.0 constant_dynamic-slice_fusion.5
  7.5 1.2 constant_dynamic-slice_fusion.3
  8.8 1.0 pad_maximum_fusion.4
  9.8 0.0 all-gather.3.cloned.1.call-update
  9.8 3.2 %copy.78 = bf16[1,512,3072]{1,2,0:T(8,128)(2,1)S(1)} copy(bf16[1,512,3072]{2,1,0:T(8,128)(2,1)} %param.7) | data formatting | bytes 6291456 | tf_op args[0]
  13.0 0.7 fusion
  13.7 166.0 %all-gather.3.cloned.1.call-done = bf16[32,96,2304]{2,1,0:T(8,128)(2,1)} async-done(((bf16[2,96,2304]{2,1,0:T(8,128)(2,1)}), bf16[32,96,2304]{2,1,0:T(8,128)(2,1)}) %all-gather.3.cloned.1.call-update) | async-done | bytes 14155792 | tf_op jit(solution)/shard_map/all_gather | solution.py:131
  179.7 10.2 %slice_bitcast_fusion = (bf16[16,96,2304]{2,1,0:T(8,128)(2,1)}, bf16[16,1,96,2304]{3,2,1,0:T(8,128)(2,1)}) fusion(bf16[16,2,96,2304]{3,2,1,0:T(8,128)(2,1)} %bitcast.51), kind=kLoop, calls=%fused_computation.3 | loop fusion | bytes 28311552 | tf_op jit(solution)/shard_map/squeeze | solution.py:133
  189.9 2.6 fusion.2
  192.5 0.5 collective-permute-start
  193.0 0.0 collective-permute-start.2
  193.0 8.1 %collective-permute-done.2 = s32[512]{0:T(512)S(1)} collective-permute-done((s32[512]{0:T(512)S(1)}, s32[512]{0:T(512)S(1)}, u32[]{:S(2)}, u32[]{:S(2)}) %collective-permute-start.2) | collective-permute-done | bytes 2080 | tf_op jit(solution)/shard_map/ppermute | solution.py:21
  201.2 1.0 copy.79.dcol_ref
  202.2 0.6 reshape.167.drow_ref
  202.8 0.2 fusion.17
  203.0 2.9 %collective-permute-done = bf16[512,3072]{0,1:T(8,128)(2,1)S(1)} collective-permute-done((bf16[512,3072]{0,1:T(8,128)(2,1)}, bf16[512,3072]{0,1:T(8,128)(2,1)S(1)}, u32[]{:S(2)}, u32[]{:S(2)}) %collective-permute-start) | collective-permute-done | bytes 3145760 | tf_op jit(solution)/shard_map/ppermute | solution.py:21
  205.9 2.9 %pad_maximum_fusion = bf16[1024,3072]{0,1:T(8,128)(2,1)S(1)} fusion(bf16[512,3072]{0,1:T(8,128)(2,1)S(1)} %collective-permute-done, bf16[512,3072]{0,1:T(8,128)(2,1)} %fusion.2), kind=kLoop, calls=%fused_computation.7 | loop fusion | flops 12582912 | bytes 12582912 | tf_op jit(solution)/shard_map/concatenate | solution.py:136
  208.8 0.5 broadcast_select_fusion
  209.2 10.0 %fusion.21 = f32[1024,2304]{1,0:T(8,128)S(1)} fusion(bf16[1024,1536]{0,1:T(8,128)(2,1)S(1)} %bitcast.54, bf16[1536,2304]{1,0:T(8,128)(2,1)} %bitcast.52), kind=kOutput, calls=%fused_computation.61 | convolution fusion | flops 7247757312 | bytes 19660800 | tf_op jit(solution)/shard_map/dot_general | solution.py:140
  219.3 13.7 %multiply_convert_fusion.q_ref.k_ref.v_ref = bf16[1024,2304]{1,0:T(8,128)(2,1)} fusion(f32[1024,2304]{1,0:T(8,128)S(1)} %fusion.21, bf16[1024,1536]{0,1:T(8,128)(2,1)S(1)} %bitcast.53, bf16[1536,2304]{1,0:T(8,128)(2,1)} %bitcast.10), kind=kOutput, calls=%fused_computation | convolution fusion | flops 7261913088 | bytes 24379392 | tf_op jit(solution)/shard_map/dot_general | solution.py:141
  233.0 3.4 %shard_map.74 = f32[2,6,128,128]{3,2,1,0:T(8,128)} custom-call(bf16[1024,2304]{1,0:T(8,128)(2,1)} %multiply_convert_fusion.q_ref.k_ref.v_ref, bf16[1024,2304]{1,0:T(8,128)(2,1)} %multiply_convert_fusion.q_ref.k_ref.v_ref, s32[2,512,1]{2,1,0:T(8,128)} %copy.79.dcol_ref, s32[2,1,512]{2,1,0:T(1,128)} %reshape.167.drow_ref), custom_call_target="tpu_custom_call" | custom-call | tf_op jit(solution)/shard_map/pallas_call | solution.py:90
  236.4 1.2 convert_element_type.44
  237.6 0.1 broadcast_in_dim.2
  237.7 0.1 fusion.19
  237.8 3.4 %collective-permute-start.3 = (bf16[2,784,128]{2,1,0:T(8,128)(2,1)S(1)}, bf16[2,784,128]{2,1,0:T(8,128)(2,1)S(1)}, u32[]{:S(2)}, u32[]{:S(2)}) collective-permute-start(bf16[2,784,128]{2,1,0:T(8,128)(2,1)S(1)} %get-tuple-element.14), channel_id=1, source_target_pairs={{0,8},{8,16},{16,24},{1,9},{9,17},{17,25},{2,10},{10,18},{18,26},{... | collective-permute-start | bytes 1204232 | tf_op jit(solution)/shard_map/ppermute | solution.py:156
  241.2 2.5 collective-permute-start.4
  243.7 1.5 collective-permute-start.5
  245.2 0.1 broadcast_add_fusion.1
  245.3 0.1 broadcast_add_fusion
  245.4 0.1 fusion.13
  245.5 6.7 %shard_map.73.local_ref = f32[1024,768]{1,0:T(8,128)} custom-call(bf16[1024,2304]{1,0:T(8,128)(2,1)} %multiply_convert_fusion.q_ref.k_ref.v_ref, bf16[1024,2304]{1,0:T(8,128)(2,1)} %multiply_convert_fusion.q_ref.k_ref.v_ref, bf16[1024,2304]{1,0:T(8,128)(2,1)} %multiply_convert_fusion.q_ref.k_ref.v_ref, s32[2,512,1]{2,1,0:T(8,128)} %copy.79.dcol_ref, ...), custom_call_target="tpu_custom_call" | custom-call | tf_op jit(solution)/shard_map/pallas_call | solution.py:79
  252.2 7.3 %collective-permute-done.4 = bf16[2,784,128]{2,1,0:T(8,128)(2,1)S(1)} collective-permute-done((bf16[2,784,128]{2,1,0:T(8,128)(2,1)S(1)}, bf16[2,784,128]{2,1,0:T(8,128)(2,1)S(1)}, u32[]{:S(2)}, u32[]{:S(2)}) %collective-permute-start.4) | collective-permute-done | bytes 401440 | tf_op jit(solution)/shard_map/ppermute | solution.py:156
  259.6 0.1 pad_maximum_fusion.1
  259.7 0.1 copy.87
  259.8 1.2 copy.82
  261.0 1.4 convolution_bitcast_fusion
  262.4 0.8 copy.89.state_ref
  263.3 4.1 %shard_map.75 = f32[1024,768]{1,0:T(8,128)} custom-call(f32[1024,768]{1,0:T(8,128)} %shard_map.73.local_ref, bf16[1024,2304]{1,0:T(8,128)(2,1)} %multiply_convert_fusion.q_ref.k_ref.v_ref, bf16[2,6,128,128]{3,2,1,0:T(8,128)(2,1)} %copy.89.state_ref, s32[2,512,1]{2,1,0:T(8,128)} %copy.79.dcol_ref, ...), custom_call_target="tpu_custom_call", output_to_operand_aliasing={{}: (0, {})} | custom-call | tf_op jit(solution)/shard_map/pallas_call | solution.py:102
  267.4 2.3 multiply_reduce_fusion
  269.7 0.1 collective-permute-start.6
  269.8 0.1 dynamic_slice.27
  269.9 1.1 collective-permute-done.6
  271.0 0.1 rev.3
  271.1 0.3 multiply_convert_fusion.1
  271.4 0.1 fusion.20
  271.5 0.2 collective-permute-start.7
  271.8 2.1 collective-permute-done.7
  273.9 1.5 maximum_select_fusion
  (23 shorter events, 0.2 us)
Async XLA Ops:
  6.5 173.2 %all-gather.3.cloned.1.call-start = ((), (), s32[]{:S(2)}) async-start(), calls=%async_computation | async-start | bytes 15040512 | tf_op jit(solution)/shard_map/all_gather | solution.py:131
  179.7 10.2 %copy-start.2 = (f32[3072]{0:T(1024)S(1)}, f32[3072]{0:T(1024)}, u32[]{:S(2)}) copy-start(f32[3072]{0:T(1024)} %param.9) | copy-start | bytes 36868
  189.9 29.4 %collective-permute-start.1 = (bf16[16,96,2304]{2,1,0:T(8,128)(2,1)}, bf16[16,96,2304]{2,1,0:T(8,128)(2,1)}, u32[]{:S(2)}, u32[]{:S(2)}) collective-permute-start(bf16[16,96,2304]{2,1,0:T(8,128)(2,1)} %get-tuple-element.7), channel_id=1, source_target_pairs={{0,4},{4,0},{1,5},{5,1},{2,6},{6,2},{3,7},{7,3},{8,12},{12,8},{9,1... | collective-permute-start | bytes 21233672 | tf_op jit(solution)/shard_map/ppermute | solution.py:21
  189.9 3.1 %copy-start.1 = (s32[1,512]{1,0:T(1,128)S(1)}, s32[1,512]{1,0:T(1,128)}, u32[]{:S(2)}) copy-start(s32[1,512]{1,0:T(1,128)} %param.8) | copy-start | bytes 6148
  192.5 13.4 %collective-permute-start = (bf16[512,3072]{0,1:T(8,128)(2,1)}, bf16[512,3072]{0,1:T(8,128)(2,1)S(1)}, u32[]{:S(2)}, u32[]{:S(2)}) collective-permute-start(bf16[512,3072]{0,1:T(8,128)(2,1)} %fusion.2), channel_id=1, source_target_pairs={{0,4},{4,0},{1,5},{5,1},{2,6},{6,2},{3,7},{7,3},{8,12},{12,8},{9,1... | collective-permute-start | bytes 9437192 | tf_op jit(solution)/shard_map/ppermute | solution.py:21
  193.0 8.2 %collective-permute-start.2 = (s32[512]{0:T(512)S(1)}, s32[512]{0:T(512)S(1)}, u32[]{:S(2)}, u32[]{:S(2)}) collective-permute-start(s32[512]{0:T(512)S(1)} %bitcast.64), channel_id=1, source_target_pairs={{0,4},{4,0},{1,5},{5,1},{2,6},{6,2},{3,7},{7,3},{8,12},{12,8},{9,1... | collective-permute-start | bytes 6152 | tf_op jit(solution)/shard_map/ppermute | solution.py:21
  237.8 14.4 %collective-permute-start.3 = (bf16[2,784,128]{2,1,0:T(8,128)(2,1)S(1)}, bf16[2,784,128]{2,1,0:T(8,128)(2,1)S(1)}, u32[]{:S(2)}, u32[]{:S(2)}) collective-permute-start(bf16[2,784,128]{2,1,0:T(8,128)(2,1)S(1)} %get-tuple-element.14), channel_id=1, source_target_pairs={{0,8},{8,16},{16,24},{1,9},{9,17},{17,25},{2,10},{10,18},{18,26},{... | collective-permute-start | bytes 1204232 | tf_op jit(solution)/shard_map/ppermute | solution.py:156
  241.2 18.3 %collective-permute-start.4 = (bf16[2,784,128]{2,1,0:T(8,128)(2,1)S(1)}, bf16[2,784,128]{2,1,0:T(8,128)(2,1)S(1)}, u32[]{:S(2)}, u32[]{:S(2)}) collective-permute-start(bf16[2,784,128]{2,1,0:T(8,128)(2,1)S(1)} %get-tuple-element.14), channel_id=1, source_target_pairs={{0,16},{8,24},{1,17},{9,25},{2,18},{10,26},{3,19},{11,27},{4,20},{... | collective-permute-start | bytes 1204232 | tf_op jit(solution)/shard_map/ppermute | solution.py:156
  243.7 15.8 %collective-permute-start.5 = (bf16[2,784,128]{2,1,0:T(8,128)(2,1)S(1)}, bf16[2,784,128]{2,1,0:T(8,128)(2,1)S(1)}, u32[]{:S(2)}, u32[]{:S(2)}) collective-permute-start(bf16[2,784,128]{2,1,0:T(8,128)(2,1)S(1)} %get-tuple-element.14), channel_id=1, source_target_pairs={{0,24},{1,25},{2,26},{3,27},{4,28},{5,29},{6,30},{7,31}} | collective-permute-start | bytes 1204232 | tf_op jit(solution)/shard_map/ppermute | solution.py:156
  267.4 2.4 copy-start.3
  267.4 3.7 %copy-start = (f32[1024,768]{1,0:T(8,128)S(1)}, f32[1024,768]{1,0:T(8,128)}, u32[]{:S(2)}) copy-start(f32[1024,768]{1,0:T(8,128)} %shard_map.75) | copy-start | bytes 9437188
  269.7 1.2 collective-permute-start.6
  271.5 2.4 collective-permute-start.7
Sparse Core Ops, SparseCore 0:
  10.1 169.5 all-gather.2

commit v10 on v6

--- a/solution.py
+++ b/solution.py
@@ -149,20 +149,11 @@
 
         tag = jnp.broadcast_to(last.astype(jnp.bfloat16)[:, None, None], (2, 16, HEAD_DIM))
         message = jnp.concatenate([tail.astype(jnp.bfloat16).reshape(2, heads * HEAD_DIM, HEAD_DIM), tag], axis=1)
-        received = [message] + [
-            lax.ppermute(message, "sq", [(i, i + shift) for i in range(n_sq - shift)])
-            for shift in range(1, n_sq)
-        ]
-        received = jnp.stack(received)
+        received = lax.all_gather(message, "sq")
         all_tail = received[:, :, : heads * HEAD_DIM].reshape(n_sq, 2, heads, HEAD_DIM, HEAD_DIM)
         all_last = received[:, :, heads * HEAD_DIM, 0].astype(jnp.int32)
-        shifts = jnp.arange(n_sq, dtype=jnp.int32)[:, None]
-        all_block = 2 * (sq - shifts) + slot_core[None, :]
-        counted = (
-            (shifts <= sq)[None]
-            & (all_block[None] < block[:, None, None])
-            & (all_last[None] == first[:, None, None])
-        )
+        all_block = 2 * jnp.arange(n_sq, dtype=jnp.int32)[:, None] + slot_core[None, :]
+        counted = (all_block[None] < block[:, None, None]) & (all_last[None] == first[:, None, None])
         carried = jnp.einsum(
             "bsk,skhef->bhef",
             counted.astype(jnp.bfloat16),

time: 252 us -> 263 us (1.044)
  waiting for transfers between devices: 173 us -> 189 us
  starting transfers between devices: 9.02 us -> 1.57 us
    all_gather x0 -> x1, waiting for transfers between devices: none -> 22.6 us  [shards(): received = lax.all_gather(message, 'sq')]
    ppermute x3 -> x0, starting transfers between devices: 7.37 us -> none  [shards(): lax.ppermute(message, 'sq', [(i, i + shift) for i in range(n_sq - shift)])]
    ppermute x3 -> x0, waiting for transfers between devices: 6.64 us -> none  [shards(): lax.ppermute(message, 'sq', [(i, i + shift) for i in range(n_sq - shift)])]
  transfers between devices with their start and end apart: 9 -> 7, of which waited for: 6 -> 6; matrix products, arithmetic and copies ran while one was open for 3% -> 3% of each run, Pallas kernels for 3% -> 3%
where the time goes in v10:
time: 263 us; the launch traced here: 262 us
  waiting for transfers between devices  189 us (72%)
  matrix products  22.4 us (9%)
  Pallas kernels  14.3 us (5%)
  between operations  13.6 us (5%)
  local copies, waits for them, and re-layouts  12.2 us (5%)
  other arithmetic  9.32 us (4%)
    all_gather x1, waiting for transfers between devices, shards(): gathered = lax.all_gather(both, ('sq', 'fsdp'), axis=0, tiled=False)  157 us
    all_gather x1, waiting for transfers between devices, shards(): received = lax.all_gather(message, 'sq')  22.6 us
    dot_general x1, matrix products, shards(): jnp.dot(pair, gathered.reshape(width, 3 * half), preferred_element_type=j...  20.9 us
    ppermute x5, waiting for transfers between devices, swap_core(): return lax.ppermute(value, 'core', [(0, 1), (1, 0)])  8.86 us
    pallas_call x1, Pallas kernels, local_attention(): pl.pallas_call(_local_kernel, grid=(blocks,), in_specs=head_specs(count,...  6.7 us
  transfers between devices with their start and end apart: 7, of which 6 were waited for; matrix products, arithmetic and copies ran while one was open for 3% of the time, Pallas kernels for 3%

profile of v10, /device:TPU:0, one launch (start us, length us, event | category | flops | bytes accessed | tf_op | source)
XLA Modules:
  0.0 262.3 jit_solution(12431849736141846811)
XLA Ops:
  6.5 1.0 constant_dynamic-slice_fusion.5
  7.5 1.2 constant_dynamic-slice_fusion.3
  8.8 0.5 collective-permute-start.1
  9.3 1.4 collective-permute-done.1
  10.7 1.0 maximum_select_fusion.1
  11.7 0.0 all-gather.4.cloned.1.call-update
  11.8 0.0 copy-start.2
  11.8 0.0 all-gather.6.cloned.1.call-start
  11.8 3.2 %copy.30 = bf16[1,512,3072]{1,2,0:T(8,128)(2,1)S(1)} copy(bf16[1,512,3072]{2,1,0:T(8,128)(2,1)} %param.7) | data formatting | bytes 6291456 | tf_op args[0]
  15.0 0.1 mul.69
  15.1 0.7 multiply_reduce_fusion
  15.9 0.9 fusion.6
  16.7 0.3 copy.31
  17.1 0.4 collective-permute-start
  17.5 0.3 collective-permute-start.2
  17.8 4.3 %collective-permute-done.2 = s32[512]{0:T(512)S(1)} collective-permute-done((s32[512]{0:T(512)S(1)}, s32[512]{0:T(512)S(1)}, u32[]{:S(2)}, u32[]{:S(2)}) %collective-permute-start.2) | collective-permute-done | bytes 2080 | tf_op jit(solution)/shard_map/ppermute | solution.py:21
  22.1 1.1 copy.32.dcol_ref
  23.1 0.6 reshape.230.drow_ref
  23.7 0.2 fusion.19
  23.9 157.5 %all-gather.4.cloned.1.call-done = bf16[16,2,96,2304]{3,2,1,0:T(8,128)(2,1)} async-done(((bf16[1,2,96,2304]{3,2,1,0:T(8,128)(2,1)}), bf16[16,2,96,2304]{3,2,1,0:T(8,128)(2,1)}) %all-gather.4.cloned.1.call-update) | async-done | bytes 14155792 | tf_op jit(solution)/shard_map/all_gather | solution.py:137
  181.4 20.9 %multiply_convert_fusion.q_ref.k_ref.v_ref = bf16[1024,2304]{1,0:T(8,128)(2,1)} fusion(bf16[3072,2304]{1,0:T(8,128)(2,1)} %bitcast.49, bf16[512,3072]{0,1:T(8,128)(2,1)} %collective-permute-done, bf16[512,3072]{0,1:T(8,128)(2,1)S(1)} %bitcast.38), kind=kOutput, calls=%fused_computation | convolution fusion | flops 14519894016 | bytes 25165824 | tf_op jit(solution)/shard_map/dot_general | solution.py:138
  202.3 3.4 %shard_map.74 = f32[2,6,128,128]{3,2,1,0:T(8,128)} custom-call(bf16[1024,2304]{1,0:T(8,128)(2,1)} %multiply_convert_fusion.q_ref.k_ref.v_ref, bf16[1024,2304]{1,0:T(8,128)(2,1)} %multiply_convert_fusion.q_ref.k_ref.v_ref, s32[2,512,1]{2,1,0:T(8,128)} %copy.32.dcol_ref, s32[2,1,512]{2,1,0:T(1,128)} %reshape.230.drow_ref), custom_call_target="tpu_custom_call" | custom-call | tf_op jit(solution)/shard_map/pallas_call | solution.py:90
  205.8 1.2 convert_element_type.50
  207.0 0.1 broadcast_in_dim.2
  207.1 0.8 pad_maximum_fusion.1
  207.8 0.0 all-gather.6.cloned.1.call-update
  207.9 0.1 broadcast_add_fusion.1
  208.0 0.1 broadcast_add_fusion
  208.0 0.1 fusion.15
  208.2 6.7 %shard_map.73.local_ref = f32[1024,768]{1,0:T(8,128)} custom-call(bf16[1024,2304]{1,0:T(8,128)(2,1)} %multiply_convert_fusion.q_ref.k_ref.v_ref, bf16[1024,2304]{1,0:T(8,128)(2,1)} %multiply_convert_fusion.q_ref.k_ref.v_ref, bf16[1024,2304]{1,0:T(8,128)(2,1)} %multiply_convert_fusion.q_ref.k_ref.v_ref, s32[2,512,1]{2,1,0:T(8,128)} %copy.32.dcol_ref, ...), custom_call_target="tpu_custom_call" | custom-call | tf_op jit(solution)/shard_map/pallas_call | solution.py:79
  214.9 22.6 %all-gather.6.cloned.1.call-done = bf16[8,784,128]{2,1,0:T(8,128)(2,1)} async-done(((bf16[2,784,128]{2,1,0:T(8,128)(2,1)}), bf16[8,784,128]{2,1,0:T(8,128)(2,1)}) %all-gather.6.cloned.1.call-update) | async-done | bytes 1605648 | tf_op jit(solution)/shard_map/all_gather | solution.py:152
  237.5 1.5 slice.31
  239.0 0.7 slice.28
  239.7 1.2 copy.35
  240.9 0.1 copy.40
  241.0 1.5 convolution_bitcast_fusion
  242.5 0.8 copy.42.state_ref
  243.3 4.1 %shard_map.75 = f32[1024,768]{1,0:T(8,128)} custom-call(f32[1024,768]{1,0:T(8,128)} %shard_map.73.local_ref, bf16[1024,2304]{1,0:T(8,128)(2,1)} %multiply_convert_fusion.q_ref.k_ref.v_ref, bf16[2,6,128,128]{3,2,1,0:T(8,128)(2,1)} %copy.42.state_ref, s32[2,512,1]{2,1,0:T(8,128)} %copy.32.dcol_ref, ...), custom_call_target="tpu_custom_call", output_to_operand_aliasing={{}: (0, {})} | custom-call | tf_op jit(solution)/shard_map/pallas_call | solution.py:102
  247.5 2.3 multiply_reduce_fusion.1
  249.8 0.1 collective-permute-start.3
  249.9 0.1 dynamic_slice.27
  250.0 1.1 collective-permute-done.3
  251.0 0.1 rev.3
  251.1 0.3 multiply_convert_fusion.2
  251.5 0.1 fusion.22
  251.6 0.2 collective-permute-start.4
  251.8 2.1 collective-permute-done.4
  253.9 1.5 maximum_select_fusion
  (17 shorter events, 0.1 us)
Async XLA Ops:
  6.5 174.9 %all-gather.4.cloned.1.call-start = ((), (), s32[]{:S(2)}) async-start(), calls=%async_computation | async-start | bytes 15040512 | tf_op jit(solution)/shard_map/all_gather | solution.py:137
  8.8 1.9 collective-permute-start.1
  11.8 3.3 %copy-start.2 = (f32[3072]{0:T(1024)S(1)}, f32[3072]{0:T(1024)}, u32[]{:S(2)}) copy-start(f32[3072]{0:T(1024)} %param.9) | copy-start | bytes 36868
  11.8 225.7 %all-gather.6.cloned.1.call-start = ((), (), s32[]{:S(2)}) async-start(), calls=%async_computation.1 | async-start | bytes 2007040 | tf_op jit(solution)/shard_map/all_gather | solution.py:152
  16.7 0.8 copy-start.1
  17.1 6.8 %collective-permute-start = (bf16[512,3072]{0,1:T(8,128)(2,1)S(1)}, bf16[512,3072]{0,1:T(8,128)(2,1)}, u32[]{:S(2)}, u32[]{:S(2)}) collective-permute-start(bf16[512,3072]{0,1:T(8,128)(2,1)S(1)} %bitcast.37), channel_id=1, source_target_pairs={{0,4},{4,0},{1,5},{5,1},{2,6},{6,2},{3,7},{7,3},{8,12},{12,8},{9,1... | collective-permute-start | bytes 9437192 | tf_op jit(solution)/shard_map/ppermute | solution.py:21
  17.5 4.6 %collective-permute-start.2 = (s32[512]{0:T(512)S(1)}, s32[512]{0:T(512)S(1)}, u32[]{:S(2)}, u32[]{:S(2)}) collective-permute-start(s32[512]{0:T(512)S(1)} %bitcast.45), channel_id=1, source_target_pairs={{0,4},{4,0},{1,5},{5,1},{2,6},{6,2},{3,7},{7,3},{8,12},{12,8},{9,1... | collective-permute-start | bytes 6152 | tf_op jit(solution)/shard_map/ppermute | solution.py:21
  247.4 2.4 copy-start.3
  247.5 3.7 %copy-start = (f32[1024,768]{1,0:T(8,128)S(1)}, f32[1024,768]{1,0:T(8,128)}, u32[]{:S(2)}) copy-start(f32[1024,768]{1,0:T(8,128)} %shard_map.75) | copy-start | bytes 9437188
  249.8 1.2 collective-permute-start.3
  251.6 2.4 collective-permute-start.4
Sparse Core Ops, SparseCore 0:
  11.9 169.4 all-gather.3
  208.0 29.4 all-gather.5

commit v11 on v6

--- a/solution.py
+++ b/solution.py
@@ -52,10 +52,17 @@
         )
 
 
-def _past_kernel(local_ref, q_ref, state_ref, dcol_ref, drow_ref, out_ref):
+def _past_kernel(local_ref, q_ref, counted_ref, dcol_ref, drow_ref, *rest):
+    message_refs, out_ref = rest[:-1], rest[-1]
     joined = dcol_ref[...] == drow_ref[...][:, 0:1]
     for h, cols in enumerate(head_columns(q_ref)):
-        from_past = jnp.dot(q_ref[:, cols], state_ref[h], preferred_element_type=jnp.float32)
+        carried = jnp.zeros((HEAD_DIM, HEAD_DIM), jnp.float32)
+        for shift, message_ref in enumerate(message_refs):
+            for slot in range(2):
+                part = message_ref[slot, cols, :].astype(jnp.float32)
+                carried = carried + counted_ref[2 * shift + slot] * part
+        state = carried.astype(jnp.bfloat16)
+        from_past = jnp.dot(q_ref[:, cols], state, preferred_element_type=jnp.float32)
         out_ref[:, cols] = local_ref[:, cols] + jnp.where(joined, from_past, 0.0)
 
 
@@ -96,17 +103,21 @@
     )(qkv, qkv, docs.reshape(blocks, count, 1), docs.reshape(blocks, 1, count))
 
 
-def add_past(local, qkv, state, docs, heads):
+def add_past(local, qkv, counted, messages, docs, heads):
     blocks, count = docs.shape
     tile = head_specs(count, heads, (0,))[0]
+    sources = counted.shape[1]
+    whole = [pl.BlockSpec(message.shape, lambda b: (0, 0, 0)) for message in messages]
     return pl.pallas_call(
         _past_kernel,
         grid=(blocks,),
-        in_specs=[tile, tile, state_spec(heads)] + doc_specs(count),
+        in_specs=[tile, tile, pl.BlockSpec((None, sources, 1, HEAD_DIM), lambda b: (b, 0, 0, 0))]
+        + doc_specs(count)
+        + whole,
         out_specs=tile,
         out_shape=jax.ShapeDtypeStruct(local.shape, jnp.float32),
         input_output_aliases={0: 0},
-    )(local, qkv, state, docs.reshape(blocks, count, 1), docs.reshape(blocks, 1, count))
+    )(local, qkv, counted, docs.reshape(blocks, count, 1), docs.reshape(blocks, 1, count), *messages)
 
 
 def make_shards(n_sq, n_fsdp):
@@ -153,9 +164,7 @@
             lax.ppermute(message, "sq", [(i, i + shift) for i in range(n_sq - shift)])
             for shift in range(1, n_sq)
         ]
-        received = jnp.stack(received)
-        all_tail = received[:, :, : heads * HEAD_DIM].reshape(n_sq, 2, heads, HEAD_DIM, HEAD_DIM)
-        all_last = received[:, :, heads * HEAD_DIM, 0].astype(jnp.int32)
+        all_last = jnp.stack([got[:, heads * HEAD_DIM, 0] for got in received]).astype(jnp.int32)
         shifts = jnp.arange(n_sq, dtype=jnp.int32)[:, None]
         all_block = 2 * (sq - shifts) + slot_core[None, :]
         counted = (
@@ -163,14 +172,11 @@
             & (all_block[None] < block[:, None, None])
             & (all_last[None] == first[:, None, None])
         )
-        carried = jnp.einsum(
-            "bsk,skhef->bhef",
-            counted.astype(jnp.bfloat16),
-            all_tail,
-            preferred_element_type=jnp.float32,
-        )
-
-        mixed = add_past(local_part, qkv, carried.astype(jnp.bfloat16), docs, heads)
+        counted = jnp.broadcast_to(
+            counted.reshape(2, 2 * n_sq, 1, 1).astype(jnp.float32), (2, 2 * n_sq, 1, HEAD_DIM)
+        )
+
+        mixed = add_past(local_part, qkv, counted, received, docs, heads)
         mixed = mixed.reshape(2, count, half)
         squares = jnp.sum(mixed * mixed, axis=-1)
         total = squares + swap_core(squares)[::-1]

time: 252 us -> 250 us (level)
  no operation moved by 1% of the time
where the time goes in v11:
time: 250 us; the launch traced here: 249 us
  waiting for transfers between devices  173 us (69%)
  matrix products  20.9 us (8%)
  Pallas kernels  15.1 us (6%)
  between operations  13.6 us (5%)
  local copies, waits for them, and re-layouts  9.22 us (4%)
  starting transfers between devices  8.97 us (4%)
  other arithmetic  8.59 us (3%)
    all_gather x1, waiting for transfers between devices, shards(): gathered = lax.all_gather(both, ('sq', 'fsdp'), axis=0, tiled=False)  158 us
    dot_general x1, matrix products, shards(): jnp.dot(pair, gathered.reshape(width, 3 * half), preferred_element_type=j...  20.9 us
    ppermute x5, waiting for transfers between devices, swap_core(): return lax.ppermute(value, 'core', [(0, 1), (1, 0)])  8.77 us
    ppermute x3, starting transfers between devices, shards(): lax.ppermute(message, 'sq', [(i, i + shift) for i in range(n_sq - shift)])  7.36 us
    pallas_call x1, Pallas kernels, local_attention(): pl.pallas_call(_local_kernel, grid=(blocks,), in_specs=head_specs(count,...  6.71 us
    ppermute x3, waiting for transfers between devices, shards(): lax.ppermute(message, 'sq', [(i, i + shift) for i in range(n_sq - shift)])  6.16 us
  transfers between devices with their start and end apart: 9, of which 6 were waited for; matrix products, arithmetic and copies ran while one was open for 3% of the time, Pallas kernels for 3%

profile of v11, /device:TPU:0, one launch (start us, length us, event | category | flops | bytes accessed | tf_op | source)
XLA Modules:
  0.0 249.0 jit_solution(1483442263641436895)
XLA Ops:
  6.5 1.0 constant_dynamic-slice_fusion.5
  7.5 1.2 constant_dynamic-slice_fusion.3
  8.8 0.5 collective-permute-start.1
  9.3 1.4 collective-permute-done.1
  10.7 1.0 maximum_select_fusion.1
  11.8 3.2 %copy.17 = bf16[1,512,3072]{1,2,0:T(8,128)(2,1)S(1)} copy(bf16[1,512,3072]{2,1,0:T(8,128)(2,1)} %param.7) | data formatting | bytes 6291456 | tf_op args[0]
  15.0 0.1 mul.69
  15.1 0.7 multiply_reduce_fusion
  15.8 0.9 fusion.6
  16.7 0.3 copy.18
  16.9 0.4 collective-permute-start
  17.4 0.3 collective-permute-start.2
  17.7 4.2 %collective-permute-done.2 = s32[512]{0:T(512)S(1)} collective-permute-done((s32[512]{0:T(512)S(1)}, s32[512]{0:T(512)S(1)}, u32[]{:S(2)}, u32[]{:S(2)}) %collective-permute-start.2) | collective-permute-done | bytes 2080 | tf_op jit(solution)/shard_map/ppermute | solution.py:21
  22.0 1.1 copy.19.dcol_ref
  23.0 0.6 reshape.343.drow_ref
  23.6 0.2 fusion.11
  23.8 157.6 %all-gather.2.cloned.1.call-done = bf16[16,2,96,2304]{3,2,1,0:T(8,128)(2,1)} async-done(((bf16[1,2,96,2304]{3,2,1,0:T(8,128)(2,1)}), bf16[16,2,96,2304]{3,2,1,0:T(8,128)(2,1)}) %all-gather.2.cloned.1.call-update) | async-done | bytes 14155792 | tf_op jit(solution)/shard_map/all_gather | solution.py:148
  181.4 20.9 %multiply_convert_fusion.q_ref.k_ref.v_ref = bf16[1024,2304]{1,0:T(8,128)(2,1)} fusion(bf16[3072,2304]{1,0:T(8,128)(2,1)} %bitcast.42, bf16[512,3072]{0,1:T(8,128)(2,1)} %collective-permute-done, bf16[512,3072]{0,1:T(8,128)(2,1)S(1)} %bitcast.30), kind=kOutput, calls=%fused_computation | convolution fusion | flops 14519894016 | bytes 25165824 | tf_op jit(solution)/shard_map/dot_general | solution.py:149
  202.3 3.4 %shard_map.74 = f32[2,6,128,128]{3,2,1,0:T(8,128)} custom-call(bf16[1024,2304]{1,0:T(8,128)(2,1)} %multiply_convert_fusion.q_ref.k_ref.v_ref, bf16[1024,2304]{1,0:T(8,128)(2,1)} %multiply_convert_fusion.q_ref.k_ref.v_ref, s32[2,512,1]{2,1,0:T(8,128)} %copy.19.dcol_ref, s32[2,1,512]{2,1,0:T(1,128)} %reshape.343.drow_ref), custom_call_target="tpu_custom_call" | custom-call | tf_op jit(solution)/shard_map/pallas_call | solution.py:97
  205.8 1.2 convert_element_type.68
  207.1 3.4 %collective-permute-start.3 = (bf16[2,784,128]{2,1,0:T(8,128)(2,1)S(1)}, bf16[2,784,128]{2,1,0:T(8,128)(2,1)S(1)}, u32[]{:S(2)}, u32[]{:S(2)}) collective-permute-start(bf16[2,784,128]{2,1,0:T(8,128)(2,1)S(1)} %pad_maximum_fusion.1.rest_0_), channel_id=1, source_target_pairs={{0,8},{8,16},{16,24},{1,9},{9,17},{17,25},{2,10},{10,18},{18,26},{... | collective-permute-start | bytes 1204232 | tf_op jit(solution)/shard_map/ppermute | solution.py:164
  210.5 2.5 collective-permute-start.4
  213.0 0.1 broadcast_add_fusion
  213.1 0.1 add.74
  213.1 1.5 collective-permute-start.5
  214.7 0.1 add.72
  214.8 0.1 and.27
  214.9 0.1 and.28
  215.0 0.1 fusion.9
  215.1 6.7 %shard_map.73.local_ref = f32[1024,768]{1,0:T(8,128)} custom-call(bf16[1024,2304]{1,0:T(8,128)(2,1)} %multiply_convert_fusion.q_ref.k_ref.v_ref, bf16[1024,2304]{1,0:T(8,128)(2,1)} %multiply_convert_fusion.q_ref.k_ref.v_ref, bf16[1024,2304]{1,0:T(8,128)(2,1)} %multiply_convert_fusion.q_ref.k_ref.v_ref, s32[2,512,1]{2,1,0:T(8,128)} %copy.19.dcol_ref, ...), custom_call_target="tpu_custom_call" | custom-call | tf_op jit(solution)/shard_map/pallas_call | solution.py:86
  221.8 0.1 slice_reduce_fusion.2
  221.9 6.2 %collective-permute-done.4.rest_2_ = bf16[2,784,128]{2,1,0:T(8,128)(2,1)S(1)} collective-permute-done((bf16[2,784,128]{2,1,0:T(8,128)(2,1)S(1)}, bf16[2,784,128]{2,1,0:T(8,128)(2,1)S(1)}, u32[]{:S(2)}, u32[]{:S(2)}) %collective-permute-start.4) | collective-permute-done | bytes 401440 | tf_op jit(solution)/shard_map/ppermute | solution.py:164
  228.1 0.1 slice_reduce_fusion.1
  228.2 0.1 slice_reduce_fusion
  228.3 0.1 reshape.347
  228.4 0.1 and_convert_fusion
  228.5 0.7 broadcast_in_dim.5.counted_ref
  229.2 5.0 %shard_map.75 = f32[1024,768]{1,0:T(8,128)} custom-call(f32[1024,768]{1,0:T(8,128)} %shard_map.73.local_ref, bf16[1024,2304]{1,0:T(8,128)(2,1)} %multiply_convert_fusion.q_ref.k_ref.v_ref, f32[2,8,1,128]{3,2,1,0:T(1,128)} %broadcast_in_dim.5.counted_ref, s32[2,512,1]{2,1,0:T(8,128)} %copy.19.dcol_ref, ...), custom_call_target="tpu_custom_call", output_to_operand_aliasing={{}: (0, {})} | custom-call | tf_op jit(solution)/shard_map/pallas_call | solution.py:111
  234.1 2.3 multiply_reduce_fusion.1
  236.5 0.1 collective-permute-start.6
  236.6 0.1 dynamic_slice.27
  236.6 1.1 collective-permute-done.6
  237.7 0.1 rev.3
  237.8 0.3 multiply_convert_fusion.2
  238.2 0.1 fusion.14
  238.3 0.2 collective-permute-start.7
  238.5 2.1 collective-permute-done.7
  240.6 1.5 maximum_select_fusion
  (35 shorter events, 0.4 us)
Async XLA Ops:
  6.5 174.9 %all-gather.2.cloned.1.call-start = ((), (), s32[]{:S(2)}) async-start(), calls=%async_computation | async-start | bytes 15040512 | tf_op jit(solution)/shard_map/all_gather | solution.py:148
  8.8 1.9 collective-permute-start.1
  11.8 3.2 %copy-start.6 = (f32[3072]{0:T(1024)S(1)}, f32[3072]{0:T(1024)}, u32[]{:S(2)}) copy-start(f32[3072]{0:T(1024)} %param.9) | copy-start | bytes 36868
  16.7 0.7 copy-start.5
  16.9 6.8 %collective-permute-start = (bf16[512,3072]{0,1:T(8,128)(2,1)S(1)}, bf16[512,3072]{0,1:T(8,128)(2,1)}, u32[]{:S(2)}, u32[]{:S(2)}) collective-permute-start(bf16[512,3072]{0,1:T(8,128)(2,1)S(1)} %bitcast.29), channel_id=1, source_target_pairs={{0,4},{4,0},{1,5},{5,1},{2,6},{6,2},{3,7},{7,3},{8,12},{12,8},{9,1... | collective-permute-start | bytes 9437192 | tf_op jit(solution)/shard_map/ppermute | solution.py:21
  17.4 4.6 %collective-permute-start.2 = (s32[512]{0:T(512)S(1)}, s32[512]{0:T(512)S(1)}, u32[]{:S(2)}, u32[]{:S(2)}) collective-permute-start(s32[512]{0:T(512)S(1)} %bitcast.34), channel_id=1, source_target_pairs={{0,4},{4,0},{1,5},{5,1},{2,6},{6,2},{3,7},{7,3},{8,12},{12,8},{9,1... | collective-permute-start | bytes 6152 | tf_op jit(solution)/shard_map/ppermute | solution.py:21
  207.1 14.7 %copy-start.1 = (bf16[2,784,128]{2,1,0:T(8,128)(2,1)}, bf16[2,784,128]{2,1,0:T(8,128)(2,1)S(1)}, u32[]{:S(2)}) copy-start(bf16[2,784,128]{2,1,0:T(8,128)(2,1)S(1)} %pad_maximum_fusion.1.rest_0_) | copy-start | bytes 1204228
  207.1 14.7 %collective-permute-start.3 = (bf16[2,784,128]{2,1,0:T(8,128)(2,1)S(1)}, bf16[2,784,128]{2,1,0:T(8,128)(2,1)S(1)}, u32[]{:S(2)}, u32[]{:S(2)}) collective-permute-start(bf16[2,784,128]{2,1,0:T(8,128)(2,1)S(1)} %pad_maximum_fusion.1.rest_0_), channel_id=1, source_target_pairs={{0,8},{8,16},{16,24},{1,9},{9,17},{17,25},{2,10},{10,18},{18,26},{... | collective-permute-start | bytes 1204232 | tf_op jit(solution)/shard_map/ppermute | solution.py:164
  210.5 17.6 %collective-permute-start.4 = (bf16[2,784,128]{2,1,0:T(8,128)(2,1)S(1)}, bf16[2,784,128]{2,1,0:T(8,128)(2,1)S(1)}, u32[]{:S(2)}, u32[]{:S(2)}) collective-permute-start(bf16[2,784,128]{2,1,0:T(8,128)(2,1)S(1)} %pad_maximum_fusion.1.rest_0_), channel_id=1, source_target_pairs={{0,16},{8,24},{1,17},{9,25},{2,18},{10,26},{3,19},{11,27},{4,20},{... | collective-permute-start | bytes 1204232 | tf_op jit(solution)/shard_map/ppermute | solution.py:164
  213.1 15.1 %collective-permute-start.5 = (bf16[2,784,128]{2,1,0:T(8,128)(2,1)S(1)}, bf16[2,784,128]{2,1,0:T(8,128)(2,1)S(1)}, u32[]{:S(2)}, u32[]{:S(2)}) collective-permute-start(bf16[2,784,128]{2,1,0:T(8,128)(2,1)S(1)} %pad_maximum_fusion.1.rest_0_), channel_id=1, source_target_pairs={{0,24},{1,25},{2,26},{3,27},{4,28},{5,29},{6,30},{7,31}} | collective-permute-start | bytes 1204232 | tf_op jit(solution)/shard_map/ppermute | solution.py:164
  221.8 7.3 %copy-start.2 = (bf16[2,784,128]{2,1,0:T(8,128)(2,1)}, bf16[2,784,128]{2,1,0:T(8,128)(2,1)S(1)}, u32[]{:S(2)}) copy-start(bf16[2,784,128]{2,1,0:T(8,128)(2,1)S(1)} %collective-permute-done.3.rest_1_) | copy-start | bytes 1204228
  228.1 1.1 copy-start.3
  228.2 1.0 copy-start.4
  234.1 2.4 copy-start.7
  234.1 3.7 %copy-start = (f32[1024,768]{1,0:T(8,128)S(1)}, f32[1024,768]{1,0:T(8,128)}, u32[]{:S(2)}) copy-start(f32[1024,768]{1,0:T(8,128)} %shard_map.75) | copy-start | bytes 9437188
  236.5 1.2 collective-permute-start.6
  238.3 2.4 collective-permute-start.7
Sparse Core Ops, SparseCore 0:
  11.9 169.4 all-gather.1

commit v12 on v11

--- a/solution.py
+++ b/solution.py
@@ -178,17 +178,13 @@
 
         mixed = add_past(local_part, qkv, counted, received, docs, heads)
         mixed = mixed.reshape(2, count, half)
-        squares = jnp.sum(mixed * mixed, axis=-1)
-        total = squares + swap_core(squares)[::-1]
-        scale = lax.rsqrt(total / ATTN_WIDTH + EPS)
-        gain = lax.dynamic_slice_in_dim(out_gain, core * half, half)
-        attended = (mixed * scale[:, :, None] * gain).astype(jnp.bfloat16)
-        theirs = swap_core(attended[1])
-        out = jnp.where(
+        theirs = swap_core(mixed[1])
+        full = jnp.where(
             core == 0,
-            jnp.concatenate([attended[0], theirs], axis=-1),
-            jnp.concatenate([theirs, attended[0]], axis=-1),
-        )
+            jnp.concatenate([mixed[0], theirs], axis=-1),
+            jnp.concatenate([theirs, mixed[0]], axis=-1),
+        )
+        out = norm_rows(full, out_gain).astype(jnp.bfloat16)
         return out[None]
 
     return shards

time: 250 us -> 249 us (level)
    ppermute x5 -> x4, waiting for transfers between devices: 8.77 us -> 9.13 us  [swap_core(): return lax.ppermute(value, 'core', [(0, 1), (1, 0)])]
  transfers between devices with their start and end apart: 9 -> 8, of which waited for: 6 -> 5; matrix products, arithmetic and copies ran while one was open for 3% -> 3% of each run, Pallas kernels for 3% -> 3%
where the time goes in v12:
time: 249 us
  waiting for transfers between devices  173 us (69%)
  matrix products  21.2 us (9%)
  Pallas kernels  15.1 us (6%)
  between operations  13.6 us (5%)
  local copies, waits for them, and re-layouts  11.1 us (4%)
  starting transfers between devices  8.77 us (4%)
  other arithmetic  6.46 us (3%)
    all_gather x1, waiting for transfers between devices, shards(): gathered = lax.all_gather(both, ('sq', 'fsdp'), axis=0, tiled=False)  157 us
    dot_general x1, matrix products, shards(): jnp.dot(pair, gathered.reshape(width, 3 * half), preferred_element_type=j...  21.2 us
    ppermute x4, waiting for transfers between devices, swap_core(): return lax.ppermute(value, 'core', [(0, 1), (1, 0)])  9.13 us
    ppermute x3, starting transfers between devices, shards(): lax.ppermute(message, 'sq', [(i, i + shift) for i in range(n_sq - shift)])  7.35 us
    pallas_call x1, Pallas kernels, local_attention(): pl.pallas_call(_local_kernel, grid=(blocks,), in_specs=head_specs(count,...  6.7 us
    ppermute x3, waiting for transfers between devices, shards(): lax.ppermute(message, 'sq', [(i, i + shift) for i in range(n_sq - shift)])  6.17 us
  transfers between devices with their start and end apart: 8, of which 5 were waited for; matrix products, arithmetic and copies ran while one was open for 3% of the time, Pallas kernels for 3%

profile of v12, /device:TPU:0, one launch (start us, length us, event | category | flops | bytes accessed | tf_op | source)
XLA Modules:
  0.0 248.9 jit_solution(5242400786047028630)
XLA Ops:
  6.5 1.0 constant_dynamic-slice_fusion.5
  7.5 1.2 constant_dynamic-slice_fusion.3
  8.8 0.5 collective-permute-start.1
  9.3 1.4 collective-permute-done.1
  10.7 1.0 maximum_select_fusion.2
  11.7 0.0 all-gather.2.cloned.1.call-update
  11.8 0.0 copy-start.5
  11.8 3.2 %copy.17 = bf16[1,512,3072]{1,2,0:T(8,128)(2,1)S(1)} copy(bf16[1,512,3072]{2,1,0:T(8,128)(2,1)} %param.7) | data formatting | bytes 6291456 | tf_op args[0]
  15.0 0.1 mul.81
  15.1 0.7 multiply_reduce_fusion
  15.8 0.9 fusion.6
  16.7 0.2 copy.18
  16.9 0.4 collective-permute-start
  17.3 0.0 copy-done.4
  17.4 0.4 collective-permute-start.2
  17.7 4.4 %collective-permute-done.2 = s32[512]{0:T(512)S(1)} collective-permute-done((s32[512]{0:T(512)S(1)}, s32[512]{0:T(512)S(1)}, u32[]{:S(2)}, u32[]{:S(2)}) %collective-permute-start.2) | collective-permute-done | bytes 2080 | tf_op jit(solution)/shard_map/ppermute | solution.py:21
  22.1 1.0 copy.19.dcol_ref
  23.2 0.6 reshape.404.drow_ref
  23.7 0.2 fusion.16
  23.9 157.5 %all-gather.2.cloned.1.call-done = bf16[16,2,96,2304]{3,2,1,0:T(8,128)(2,1)} async-done(((bf16[1,2,96,2304]{3,2,1,0:T(8,128)(2,1)}), bf16[16,2,96,2304]{3,2,1,0:T(8,128)(2,1)}) %all-gather.2.cloned.1.call-update) | async-done | bytes 14155792 | tf_op jit(solution)/shard_map/all_gather | solution.py:148
  181.4 21.2 %multiply_convert_fusion.q_ref.k_ref.v_ref = bf16[1024,2304]{1,0:T(8,128)(2,1)} fusion(bf16[3072,2304]{1,0:T(8,128)(2,1)} %bitcast.40, bf16[512,3072]{0,1:T(8,128)(2,1)} %collective-permute-done, bf16[512,3072]{0,1:T(8,128)(2,1)S(1)} %bitcast.29), kind=kOutput, calls=%fused_computation | convolution fusion | flops 14519894016 | bytes 25165824 | tf_op jit(solution)/shard_map/dot_general | solution.py:149
  202.5 3.4 %shard_map.74 = f32[2,6,128,128]{3,2,1,0:T(8,128)} custom-call(bf16[1024,2304]{1,0:T(8,128)(2,1)} %multiply_convert_fusion.q_ref.k_ref.v_ref, bf16[1024,2304]{1,0:T(8,128)(2,1)} %multiply_convert_fusion.q_ref.k_ref.v_ref, s32[2,512,1]{2,1,0:T(8,128)} %copy.19.dcol_ref, s32[2,1,512]{2,1,0:T(1,128)} %reshape.404.drow_ref), custom_call_target="tpu_custom_call" | custom-call | tf_op jit(solution)/shard_map/pallas_call | solution.py:97
  206.0 1.2 convert_element_type.75
  207.2 0.1 broadcast_in_dim.4
  207.3 3.4 %collective-permute-start.3 = (bf16[2,784,128]{2,1,0:T(8,128)(2,1)S(1)}, bf16[2,784,128]{2,1,0:T(8,128)(2,1)S(1)}, u32[]{:S(2)}, u32[]{:S(2)}) collective-permute-start(bf16[2,784,128]{2,1,0:T(8,128)(2,1)S(1)} %pad_maximum_fusion.1.rest_0_), channel_id=1, source_target_pairs={{0,8},{8,16},{16,24},{1,9},{9,17},{17,25},{2,10},{10,18},{18,26},{... | collective-permute-start | bytes 1204232 | tf_op jit(solution)/shard_map/ppermute | solution.py:164
  210.7 2.5 collective-permute-start.4
  213.2 0.1 broadcast_add_fusion
  213.3 0.1 add.68
  213.4 1.5 collective-permute-start.5
  214.9 0.1 add.65
  214.9 0.1 add.66
  215.0 0.1 and.27
  215.1 0.1 and.28
  215.2 0.1 fusion.14
  215.3 6.7 %shard_map.73.local_ref = f32[1024,768]{1,0:T(8,128)} custom-call(bf16[1024,2304]{1,0:T(8,128)(2,1)} %multiply_convert_fusion.q_ref.k_ref.v_ref, bf16[1024,2304]{1,0:T(8,128)(2,1)} %multiply_convert_fusion.q_ref.k_ref.v_ref, bf16[1024,2304]{1,0:T(8,128)(2,1)} %multiply_convert_fusion.q_ref.k_ref.v_ref, s32[2,512,1]{2,1,0:T(8,128)} %copy.19.dcol_ref, ...), custom_call_target="tpu_custom_call" | custom-call | tf_op jit(solution)/shard_map/pallas_call | solution.py:86
  222.0 0.1 slice_reduce_fusion.2
  222.2 6.2 %collective-permute-done.4.rest_2_ = bf16[2,784,128]{2,1,0:T(8,128)(2,1)S(1)} collective-permute-done((bf16[2,784,128]{2,1,0:T(8,128)(2,1)S(1)}, bf16[2,784,128]{2,1,0:T(8,128)(2,1)S(1)}, u32[]{:S(2)}, u32[]{:S(2)}) %collective-permute-start.4) | collective-permute-done | bytes 401440 | tf_op jit(solution)/shard_map/ppermute | solution.py:164
  228.3 0.1 slice_reduce_fusion.1
  228.4 0.1 slice_reduce_fusion
  228.5 0.1 reshape.407
  228.6 0.1 and_convert_fusion
  228.7 0.7 broadcast_in_dim.5.counted_ref
  229.4 4.9 %shard_map.75 = f32[1024,768]{1,0:T(8,128)} custom-call(f32[1024,768]{1,0:T(8,128)} %shard_map.73.local_ref, bf16[1024,2304]{1,0:T(8,128)(2,1)} %multiply_convert_fusion.q_ref.k_ref.v_ref, f32[2,8,1,128]{3,2,1,0:T(1,128)} %broadcast_in_dim.5.counted_ref, s32[2,512,1]{2,1,0:T(8,128)} %copy.19.dcol_ref, ...), custom_call_target="tpu_custom_call", output_to_operand_aliasing={{}: (0, {})} | custom-call | tf_op jit(solution)/shard_map/pallas_call | solution.py:111
  234.3 2.2 fusion.19
  236.6 0.1 collective-permute-start.6
  236.6 3.4 %collective-permute-done.6 = f32[512,768]{1,0:T(8,128)S(1)} collective-permute-done((f32[512,768]{1,0:T(8,128)S(1)}, f32[512,768]{1,0:T(8,128)S(1)}, u32[]{:S(2)}, u32[]{:S(2)}) %collective-permute-start.6) | collective-permute-done | bytes 1572896 | tf_op jit(solution)/shard_map/ppermute | solution.py:21
  240.0 0.4 fusion.11
  240.5 1.6 fusion.9
  (27 shorter events, 0.2 us)
Async XLA Ops:
  6.5 174.9 %all-gather.2.cloned.1.call-start = ((), (), s32[]{:S(2)}) async-start(), calls=%async_computation | async-start | bytes 15040512 | tf_op jit(solution)/shard_map/all_gather | solution.py:148
  8.8 1.9 collective-permute-start.1
  11.8 3.2 %copy-start.5 = (f32[3072]{0:T(1024)S(1)}, f32[3072]{0:T(1024)}, u32[]{:S(2)}) copy-start(f32[3072]{0:T(1024)} %param.9) | copy-start | bytes 36868
  16.7 0.7 copy-start.4
  16.9 7.0 %collective-permute-start = (bf16[512,3072]{0,1:T(8,128)(2,1)S(1)}, bf16[512,3072]{0,1:T(8,128)(2,1)}, u32[]{:S(2)}, u32[]{:S(2)}) collective-permute-start(bf16[512,3072]{0,1:T(8,128)(2,1)S(1)} %bitcast.28), channel_id=1, source_target_pairs={{0,4},{4,0},{1,5},{5,1},{2,6},{6,2},{3,7},{7,3},{8,12},{12,8},{9,1... | collective-permute-start | bytes 9437192 | tf_op jit(solution)/shard_map/ppermute | solution.py:21
  17.4 4.7 %collective-permute-start.2 = (s32[512]{0:T(512)S(1)}, s32[512]{0:T(512)S(1)}, u32[]{:S(2)}, u32[]{:S(2)}) collective-permute-start(s32[512]{0:T(512)S(1)} %bitcast.32), channel_id=1, source_target_pairs={{0,4},{4,0},{1,5},{5,1},{2,6},{6,2},{3,7},{7,3},{8,12},{12,8},{9,1... | collective-permute-start | bytes 6152 | tf_op jit(solution)/shard_map/ppermute | solution.py:21
  207.3 14.7 %copy-start = (bf16[2,784,128]{2,1,0:T(8,128)(2,1)}, bf16[2,784,128]{2,1,0:T(8,128)(2,1)S(1)}, u32[]{:S(2)}) copy-start(bf16[2,784,128]{2,1,0:T(8,128)(2,1)S(1)} %pad_maximum_fusion.1.rest_0_) | copy-start | bytes 1204228
  207.3 14.7 %collective-permute-start.3 = (bf16[2,784,128]{2,1,0:T(8,128)(2,1)S(1)}, bf16[2,784,128]{2,1,0:T(8,128)(2,1)S(1)}, u32[]{:S(2)}, u32[]{:S(2)}) collective-permute-start(bf16[2,784,128]{2,1,0:T(8,128)(2,1)S(1)} %pad_maximum_fusion.1.rest_0_), channel_id=1, source_target_pairs={{0,8},{8,16},{16,24},{1,9},{9,17},{17,25},{2,10},{10,18},{18,26},{... | collective-permute-start | bytes 1204232 | tf_op jit(solution)/shard_map/ppermute | solution.py:164
  210.7 17.6 %collective-permute-start.4 = (bf16[2,784,128]{2,1,0:T(8,128)(2,1)S(1)}, bf16[2,784,128]{2,1,0:T(8,128)(2,1)S(1)}, u32[]{:S(2)}, u32[]{:S(2)}) collective-permute-start(bf16[2,784,128]{2,1,0:T(8,128)(2,1)S(1)} %pad_maximum_fusion.1.rest_0_), channel_id=1, source_target_pairs={{0,16},{8,24},{1,17},{9,25},{2,18},{10,26},{3,19},{11,27},{4,20},{... | collective-permute-start | bytes 1204232 | tf_op jit(solution)/shard_map/ppermute | solution.py:164
  213.4 15.1 %collective-permute-start.5 = (bf16[2,784,128]{2,1,0:T(8,128)(2,1)S(1)}, bf16[2,784,128]{2,1,0:T(8,128)(2,1)S(1)}, u32[]{:S(2)}, u32[]{:S(2)}) collective-permute-start(bf16[2,784,128]{2,1,0:T(8,128)(2,1)S(1)} %pad_maximum_fusion.1.rest_0_), channel_id=1, source_target_pairs={{0,24},{1,25},{2,26},{3,27},{4,28},{5,29},{6,30},{7,31}} | collective-permute-start | bytes 1204232 | tf_op jit(solution)/shard_map/ppermute | solution.py:164
  222.0 7.4 %copy-start.1 = (bf16[2,784,128]{2,1,0:T(8,128)(2,1)}, bf16[2,784,128]{2,1,0:T(8,128)(2,1)S(1)}, u32[]{:S(2)}) copy-start(bf16[2,784,128]{2,1,0:T(8,128)(2,1)S(1)} %collective-permute-done.3.rest_1_) | copy-start | bytes 1204228
  228.3 1.1 copy-start.2
  228.4 1.0 copy-start.3
  236.5 3.9 %copy-start.6 = (f32[1536]{0:T(1024)S(1)}, f32[1536]{0:T(1024)}, u32[]{:S(2)}) copy-start(f32[1536]{0:T(1024)} %param.13) | copy-start | bytes 18436
  236.6 3.5 %collective-permute-start.6 = (f32[512,768]{1,0:T(8,128)S(1)}, f32[512,768]{1,0:T(8,128)S(1)}, u32[]{:S(2)}, u32[]{:S(2)}) collective-permute-start(f32[512,768]{1,0:T(8,128)S(1)} %get-tuple-element.9), channel_id=1, source_target_pairs={{0,4},{4,0},{1,5},{5,1},{2,6},{6,2},{3,7},{7,3},{8,12},{12,8},{9,1... | collective-permute-start | bytes 4718600 | tf_op jit(solution)/shard_map/ppermute | solution.py:21
Sparse Core Ops, SparseCore 0:
  11.9 169.4 all-gather.1

commit v13 on v11

--- a/solution.py
+++ b/solution.py
@@ -57,10 +57,12 @@
     joined = dcol_ref[...] == drow_ref[...][:, 0:1]
     for h, cols in enumerate(head_columns(q_ref)):
         carried = jnp.zeros((HEAD_DIM, HEAD_DIM), jnp.float32)
-        for shift, message_ref in enumerate(message_refs):
-            for slot in range(2):
+        index = 0
+        for message_ref in message_refs:
+            for slot in range(message_ref.shape[0]):
                 part = message_ref[slot, cols, :].astype(jnp.float32)
-                carried = carried + counted_ref[2 * shift + slot] * part
+                carried = carried + counted_ref[index] * part
+                index += 1
         state = carried.astype(jnp.bfloat16)
         from_past = jnp.dot(q_ref[:, cols], state, preferred_element_type=jnp.float32)
         out_ref[:, cols] = local_ref[:, cols] + jnp.where(joined, from_past, 0.0)
@@ -158,25 +160,28 @@
         tail = tail_states(qkv, docs, heads)
         local_part = local_attention(qkv, docs, heads)
 
-        tag = jnp.broadcast_to(last.astype(jnp.bfloat16)[:, None, None], (2, 16, HEAD_DIM))
-        message = jnp.concatenate([tail.astype(jnp.bfloat16).reshape(2, heads * HEAD_DIM, HEAD_DIM), tag], axis=1)
-        received = [message] + [
+        own_message = tail.astype(jnp.bfloat16).reshape(2, heads * HEAD_DIM, HEAD_DIM)
+        own_counted = (block[None, :] < block[:, None]) & (last[None, :] == first[:, None])
+        first_tail, second_tail = jnp.where(core == 0, tail[0], tail[1]), jnp.where(core == 0, tail[1], tail[0])
+        first_last, second_last = jnp.where(core == 0, last[0], last[1]), jnp.where(core == 0, last[1], last[0])
+        chip_tail = second_tail + jnp.where(first_last == second_last, first_tail, 0.0)
+        tag = jnp.broadcast_to(second_last.astype(jnp.bfloat16), (1, 16, HEAD_DIM))
+        message = jnp.concatenate(
+            [chip_tail.astype(jnp.bfloat16).reshape(1, heads * HEAD_DIM, HEAD_DIM), tag], axis=1
+        )
+        received = [
             lax.ppermute(message, "sq", [(i, i + shift) for i in range(n_sq - shift)])
             for shift in range(1, n_sq)
         ]
-        all_last = jnp.stack([got[:, heads * HEAD_DIM, 0] for got in received]).astype(jnp.int32)
-        shifts = jnp.arange(n_sq, dtype=jnp.int32)[:, None]
-        all_block = 2 * (sq - shifts) + slot_core[None, :]
-        counted = (
-            (shifts <= sq)[None]
-            & (all_block[None] < block[:, None, None])
-            & (all_last[None] == first[:, None, None])
-        )
+        chip_last = jnp.stack([got[0, heads * HEAD_DIM, 0] for got in received]).astype(jnp.int32)
+        shifts = jnp.arange(1, n_sq, dtype=jnp.int32)
+        far_counted = (shifts <= sq)[None, :] & (chip_last[None, :] == first[:, None])
+        counted = jnp.concatenate([own_counted, far_counted], axis=1)
         counted = jnp.broadcast_to(
-            counted.reshape(2, 2 * n_sq, 1, 1).astype(jnp.float32), (2, 2 * n_sq, 1, HEAD_DIM)
-        )
-
-        mixed = add_past(local_part, qkv, counted, received, docs, heads)
+            counted.reshape(2, n_sq + 1, 1, 1).astype(jnp.float32), (2, n_sq + 1, 1, HEAD_DIM)
+        )
+
+        mixed = add_past(local_part, qkv, counted, [own_message] + received, docs, heads)
         mixed = mixed.reshape(2, count, half)
         squares = jnp.sum(mixed * mixed, axis=-1)
         total = squares + swap_core(squares)[::-1]

time: 250 us -> 246 us (0.984)
  waiting for transfers between devices: 173 us -> 163 us
  other arithmetic: 8.59 us -> 11.2 us
    ppermute x3, waiting for transfers between devices: 6.16 us -> 0.01 us  [shards(): lax.ppermute(message, 'sq', [(i, i + shift) for i in range(n_sq - shift)])]
    all_gather x1, waiting for transfers between devices: 158 us -> 154 us  [shards(): gathered = lax.all_gather(both, ('sq', 'fsdp'), axis=0, tiled=False)]
    convert_element_type x3, other arithmetic: 0.28 us -> 3.06 us  [the longest x1 1.8 us: shards(): jnp.stack([got[0, heads * HEAD_DIM, 0] for got in received])]
  transfers between devices with their start and end apart: 9 -> 9, of which waited for: 6 -> 5; matrix products, arithmetic and copies ran while one was open for 3% -> 4% of each run, Pallas kernels for 3% -> 3%
where the time goes in v13:
time: 246 us
  waiting for transfers between devices  163 us (66%)
  matrix products  21.1 us (9%)
  between operations  16 us (7%)
  Pallas kernels  14.7 us (6%)
  other arithmetic  11.2 us (5%)
  local copies, waits for them, and re-layouts  11.1 us (5%)
  starting transfers between devices  8.98 us (4%)
    all_gather x1, waiting for transfers between devices, shards(): gathered = lax.all_gather(both, ('sq', 'fsdp'), axis=0, tiled=False)  154 us
    dot_general x1, matrix products, shards(): jnp.dot(pair, gathered.reshape(width, 3 * half), preferred_element_type=j...  21.1 us
    ppermute x5, waiting for transfers between devices, swap_core(): return lax.ppermute(value, 'core', [(0, 1), (1, 0)])  8.24 us
    ppermute x3, starting transfers between devices, shards(): lax.ppermute(message, 'sq', [(i, i + shift) for i in range(n_sq - shift)])  7.35 us
    pallas_call x1, Pallas kernels, local_attention(): pl.pallas_call(_local_kernel, grid=(blocks,), in_specs=head_specs(count,...  6.77 us
  transfers between devices with their start and end apart: 9, of which 5 were waited for; matrix products, arithmetic and copies ran while one was open for 4% of the time, Pallas kernels for 3%

profile of v13, /device:TPU:0, one launch (start us, length us, event | category | flops | bytes accessed | tf_op | source)
XLA Modules:
  0.0 245.7 jit_solution(16872063196526584308)
XLA Ops:
  6.5 1.0 constant_dynamic-slice_fusion.5
  7.5 1.2 constant_dynamic-slice_fusion.3
  8.8 0.5 collective-permute-start.1
  9.3 1.4 collective-permute-done.1
  10.7 1.0 maximum_select_fusion.1
  11.8 3.2 %copy.17 = bf16[1,512,3072]{1,2,0:T(8,128)(2,1)S(1)} copy(bf16[1,512,3072]{2,1,0:T(8,128)(2,1)} %param.7) | data formatting | bytes 6291456 | tf_op args[0]
  15.0 0.1 mul.58
  15.1 0.7 multiply_reduce_fusion
  15.8 0.9 fusion.6
  16.7 0.2 copy.18
  16.9 0.4 collective-permute-start
  17.3 0.0 copy-done.6
  17.4 0.4 collective-permute-start.2
  17.7 0.1 add_add_fusion
  17.8 0.6 slice.51
  18.4 3.7 %collective-permute-done.2 = s32[512]{0:T(512)S(1)} collective-permute-done((s32[512]{0:T(512)S(1)}, s32[512]{0:T(512)S(1)}, u32[]{:S(2)}, u32[]{:S(2)}) %collective-permute-start.2) | collective-permute-done | bytes 2080 | tf_op jit(solution)/shard_map/ppermute | solution.py:21
  22.1 0.6 slice.64
  25.1 1.1 copy.19.dcol_ref
  26.2 0.6 reshape.347.drow_ref
  26.8 0.2 fusion.10
  27.0 154.4 %all-gather.2.cloned.1.call-done = bf16[16,2,96,2304]{3,2,1,0:T(8,128)(2,1)} async-done(((bf16[1,2,96,2304]{3,2,1,0:T(8,128)(2,1)}), bf16[16,2,96,2304]{3,2,1,0:T(8,128)(2,1)}) %all-gather.2.cloned.1.call-update) | async-done | bytes 14155792 | tf_op jit(solution)/shard_map/all_gather | solution.py:150
  181.4 21.1 %multiply_convert_fusion.q_ref.k_ref.v_ref = bf16[1024,2304]{1,0:T(8,128)(2,1)} fusion(bf16[3072,2304]{1,0:T(8,128)(2,1)} %bitcast.39, bf16[512,3072]{0,1:T(8,128)(2,1)} %collective-permute-done, bf16[512,3072]{0,1:T(8,128)(2,1)S(1)} %bitcast.30), kind=kOutput, calls=%fused_computation | convolution fusion | flops 14519894016 | bytes 25165824 | tf_op jit(solution)/shard_map/dot_general | solution.py:151
  202.5 3.4 %shard_map.74 = f32[2,6,128,128]{3,2,1,0:T(8,128)} custom-call(bf16[1024,2304]{1,0:T(8,128)(2,1)} %multiply_convert_fusion.q_ref.k_ref.v_ref, bf16[1024,2304]{1,0:T(8,128)(2,1)} %multiply_convert_fusion.q_ref.k_ref.v_ref, s32[2,512,1]{2,1,0:T(8,128)} %copy.19.dcol_ref, s32[2,1,512]{2,1,0:T(1,128)} %reshape.347.drow_ref), custom_call_target="tpu_custom_call" | custom-call | tf_op jit(solution)/shard_map/pallas_call | solution.py:99
  205.9 1.2 add_convert_fusion
  207.2 3.4 %collective-permute-start.3 = (bf16[1,784,128]{2,1,0:T(8,128)(2,1)S(1)}, bf16[1,784,128]{2,1,0:T(8,128)(2,1)S(1)}, u32[]{:S(2)}, u32[]{:S(2)}) collective-permute-start(bf16[1,784,128]{2,1,0:T(8,128)(2,1)S(1)} %concatenate.70), channel_id=1, source_target_pairs={{0,8},{8,16},{16,24},{1,9},{9,17},{17,25},{2,10},{10,18},{18,26},{... | collective-permute-start | bytes 602120 | tf_op jit(solution)/shard_map/ppermute | solution.py:173
  210.5 2.5 %collective-permute-start.4 = (bf16[1,784,128]{2,1,0:T(8,128)(2,1)S(1)}, bf16[1,784,128]{2,1,0:T(8,128)(2,1)S(1)}, u32[]{:S(2)}, u32[]{:S(2)}) collective-permute-start(bf16[1,784,128]{2,1,0:T(8,128)(2,1)S(1)} %concatenate.70), channel_id=1, source_target_pairs={{0,16},{8,24},{1,17},{9,25},{2,18},{10,26},{3,19},{11,27},{4,20},{... | collective-permute-start | bytes 602120 | tf_op jit(solution)/shard_map/ppermute | solution.py:173
  213.0 1.5 collective-permute-start.5
  214.5 0.1 compare_and_fusion.1
  214.6 6.8 %shard_map.73.local_ref = f32[1024,768]{1,0:T(8,128)} custom-call(bf16[1024,2304]{1,0:T(8,128)(2,1)} %multiply_convert_fusion.q_ref.k_ref.v_ref, bf16[1024,2304]{1,0:T(8,128)(2,1)} %multiply_convert_fusion.q_ref.k_ref.v_ref, bf16[1024,2304]{1,0:T(8,128)(2,1)} %multiply_convert_fusion.q_ref.k_ref.v_ref, s32[2,512,1]{2,1,0:T(8,128)} %copy.19.dcol_ref, ...), custom_call_target="tpu_custom_call" | custom-call | tf_op jit(solution)/shard_map/pallas_call | solution.py:88
  221.4 0.8 convert_element_type.64
  222.2 0.5 slice.65
  222.7 0.5 slice.66
  223.3 0.5 slice.67
  223.8 1.8 maximum_convert_fusion
  225.6 0.1 compare_and_fusion
  225.7 0.1 add_convert_fusion.1
  225.7 0.7 broadcast_in_dim.7.counted_ref
  226.4 4.5 %shard_map.75 = f32[1024,768]{1,0:T(8,128)} custom-call(f32[1024,768]{1,0:T(8,128)} %shard_map.73.local_ref, bf16[1024,2304]{1,0:T(8,128)(2,1)} %multiply_convert_fusion.q_ref.k_ref.v_ref, f32[2,5,1,128]{3,2,1,0:T(1,128)} %broadcast_in_dim.7.counted_ref, s32[2,512,1]{2,1,0:T(8,128)} %copy.19.dcol_ref, ...), custom_call_target="tpu_custom_call", output_to_operand_aliasing={{}: (0, {})} | custom-call | tf_op jit(solution)/shard_map/pallas_call | solution.py:113
  230.9 2.3 multiply_reduce_fusion.1
  233.2 0.1 collective-permute-start.6
  233.3 0.1 dynamic_slice.27
  233.4 1.1 collective-permute-done.6
  234.5 0.1 rev.3
  234.6 0.3 multiply_convert_fusion.2
  234.9 0.1 fusion.13
  235.0 0.2 collective-permute-start.7
  235.3 2.1 collective-permute-done.7
  237.4 1.5 maximum_select_fusion
  (29 shorter events, 0.2 us)
Async XLA Ops:
  6.5 174.9 %all-gather.2.cloned.1.call-start = ((), (), s32[]{:S(2)}) async-start(), calls=%async_computation | async-start | bytes 15040512 | tf_op jit(solution)/shard_map/all_gather | solution.py:150
  8.8 1.9 collective-permute-start.1
  11.8 3.2 %copy-start.5 = (f32[3072]{0:T(1024)S(1)}, f32[3072]{0:T(1024)}, u32[]{:S(2)}) copy-start(f32[3072]{0:T(1024)} %param.9) | copy-start | bytes 36868
  16.7 0.7 copy-start.6
  16.9 10.1 %collective-permute-start = (bf16[512,3072]{0,1:T(8,128)(2,1)S(1)}, bf16[512,3072]{0,1:T(8,128)(2,1)}, u32[]{:S(2)}, u32[]{:S(2)}) collective-permute-start(bf16[512,3072]{0,1:T(8,128)(2,1)S(1)} %bitcast.29), channel_id=1, source_target_pairs={{0,4},{4,0},{1,5},{5,1},{2,6},{6,2},{3,7},{7,3},{8,12},{12,8},{9,1... | collective-permute-start | bytes 9437192 | tf_op jit(solution)/shard_map/ppermute | solution.py:21
  17.4 4.7 %collective-permute-start.2 = (s32[512]{0:T(512)S(1)}, s32[512]{0:T(512)S(1)}, u32[]{:S(2)}, u32[]{:S(2)}) collective-permute-start(s32[512]{0:T(512)S(1)} %bitcast.35), channel_id=1, source_target_pairs={{0,4},{4,0},{1,5},{5,1},{2,6},{6,2},{3,7},{7,3},{8,12},{12,8},{9,1... | collective-permute-start | bytes 6152 | tf_op jit(solution)/shard_map/ppermute | solution.py:21
  207.2 15.0 %collective-permute-start.3 = (bf16[1,784,128]{2,1,0:T(8,128)(2,1)S(1)}, bf16[1,784,128]{2,1,0:T(8,128)(2,1)S(1)}, u32[]{:S(2)}, u32[]{:S(2)}) collective-permute-start(bf16[1,784,128]{2,1,0:T(8,128)(2,1)S(1)} %concatenate.70), channel_id=1, source_target_pairs={{0,8},{8,16},{16,24},{1,9},{9,17},{17,25},{2,10},{10,18},{18,26},{... | collective-permute-start | bytes 602120 | tf_op jit(solution)/shard_map/ppermute | solution.py:173
  210.5 12.2 %collective-permute-start.4 = (bf16[1,784,128]{2,1,0:T(8,128)(2,1)S(1)}, bf16[1,784,128]{2,1,0:T(8,128)(2,1)S(1)}, u32[]{:S(2)}, u32[]{:S(2)}) collective-permute-start(bf16[1,784,128]{2,1,0:T(8,128)(2,1)S(1)} %concatenate.70), channel_id=1, source_target_pairs={{0,16},{8,24},{1,17},{9,25},{2,18},{10,26},{3,19},{11,27},{4,20},{... | collective-permute-start | bytes 602120 | tf_op jit(solution)/shard_map/ppermute | solution.py:173
  213.0 10.2 %collective-permute-start.5 = (bf16[1,784,128]{2,1,0:T(8,128)(2,1)S(1)}, bf16[1,784,128]{2,1,0:T(8,128)(2,1)S(1)}, u32[]{:S(2)}, u32[]{:S(2)}) collective-permute-start(bf16[1,784,128]{2,1,0:T(8,128)(2,1)S(1)} %concatenate.70), channel_id=1, source_target_pairs={{0,24},{1,25},{2,26},{3,27},{4,28},{5,29},{6,30},{7,31}} | collective-permute-start | bytes 602120 | tf_op jit(solution)/shard_map/ppermute | solution.py:173
  214.6 6.8 %copy-start.1 = (f32[2,6,128,128]{3,2,1,0:T(8,128)S(1)}, f32[2,6,128,128]{3,2,1,0:T(8,128)}, u32[]{:S(2)}) copy-start(f32[2,6,128,128]{3,2,1,0:T(8,128)} %shard_map.74) | copy-start | bytes 2359300
  222.2 4.2 %copy-start.2 = (bf16[1,784,128]{2,1,0:T(8,128)(2,1)}, bf16[1,784,128]{2,1,0:T(8,128)(2,1)S(1)}, u32[]{:S(2)}) copy-start(bf16[1,784,128]{2,1,0:T(8,128)(2,1)S(1)} %collective-permute-done.3.rest_1_) | copy-start | bytes 602116
  222.7 3.7 %copy-start.3 = (bf16[1,784,128]{2,1,0:T(8,128)(2,1)}, bf16[1,784,128]{2,1,0:T(8,128)(2,1)S(1)}, u32[]{:S(2)}) copy-start(bf16[1,784,128]{2,1,0:T(8,128)(2,1)S(1)} %collective-permute-done.4.rest_2_) | copy-start | bytes 602116
  223.3 3.2 %copy-start.4 = (bf16[1,784,128]{2,1,0:T(8,128)(2,1)}, bf16[1,784,128]{2,1,0:T(8,128)(2,1)S(1)}, u32[]{:S(2)}) copy-start(bf16[1,784,128]{2,1,0:T(8,128)(2,1)S(1)} %collective-permute-done.5.rest_3_) | copy-start | bytes 602116
  230.9 2.4 copy-start.7
  230.9 3.7 %copy-start = (f32[1024,768]{1,0:T(8,128)S(1)}, f32[1024,768]{1,0:T(8,128)}, u32[]{:S(2)}) copy-start(f32[1024,768]{1,0:T(8,128)} %shard_map.75) | copy-start | bytes 9437188
  233.2 1.2 collective-permute-start.6
  235.0 2.4 collective-permute-start.7
Sparse Core Ops, SparseCore 0:
  11.9 169.4 all-gather.1

commit v14 on v13

--- a/solution.py
+++ b/solution.py
@@ -42,14 +42,24 @@
         local_ref[:, cols] = jnp.dot(weights, v_ref[:, cols], preferred_element_type=jnp.float32)
 
 
-def _tail_kernel(k_ref, v_ref, dcol_ref, drow_ref, tail_ref):
-    count = k_ref.shape[0]
-    ending = dcol_ref[...] == drow_ref[...][:, count - 1:count]
+def _tail_kernel(k_ref, v_ref, dcol_ref, drow_ref, own_ref, message_ref):
+    count = dcol_ref.shape[1]
+    lasts = [drow_ref[block][:, count - 1:count] for block in range(2)]
+    chip_last = jnp.maximum(lasts[0], lasts[1])
     for h, cols in enumerate(head_columns(k_ref)):
-        tail_keys = jnp.where(ending, k_ref[:, cols], jnp.zeros((count, HEAD_DIM), k_ref.dtype))
-        tail_ref[h] = lax.dot_general(
-            tail_keys, v_ref[:, cols], (((0,), (0,)), ((), ())), preferred_element_type=jnp.float32
-        )
+        chip = jnp.zeros((HEAD_DIM, HEAD_DIM), jnp.float32)
+        for block in range(2):
+            rows = slice(block * count, (block + 1) * count)
+            ending = dcol_ref[block] == lasts[block]
+            tail_keys = jnp.where(ending, k_ref[rows, cols], jnp.zeros((count, HEAD_DIM), k_ref.dtype))
+            tail = lax.dot_general(
+                tail_keys, v_ref[rows, cols], (((0,), (0,)), ((), ())), preferred_element_type=jnp.float32
+            )
+            own_ref[block, cols, :] = tail.astype(jnp.bfloat16)
+            chip = chip + jnp.where(lasts[block] == chip_last, tail, 0.0)
+        message_ref[0, cols, :] = chip.astype(jnp.bfloat16)
+    tag = jnp.broadcast_to(chip_last.astype(jnp.float32), (16, HEAD_DIM)).astype(jnp.bfloat16)
+    message_ref[0, pl.ds(k_ref.shape[1], 16), :] = tag
 
 
 def _past_kernel(local_ref, q_ref, counted_ref, dcol_ref, drow_ref, *rest):
@@ -96,12 +106,24 @@
 
 def tail_states(qkv, docs, heads):
     blocks, count = docs.shape
+    width = heads * HEAD_DIM
     return pl.pallas_call(
         _tail_kernel,
-        grid=(blocks,),
-        in_specs=head_specs(count, heads, (1, 2)) + doc_specs(count),
-        out_specs=state_spec(heads),
-        out_shape=jax.ShapeDtypeStruct((blocks, heads, HEAD_DIM, HEAD_DIM), jnp.float32),
+        grid=(1,),
+        in_specs=[
+            pl.BlockSpec((blocks * count, width), lambda i: (0, 1)),
+            pl.BlockSpec((blocks * count, width), lambda i: (0, 2)),
+            pl.BlockSpec((blocks, count, 1), lambda i: (0, 0, 0)),
+            pl.BlockSpec((blocks, 1, count), lambda i: (0, 0, 0)),
+        ],
+        out_specs=[
+            pl.BlockSpec((blocks, width, HEAD_DIM), lambda i: (0, 0, 0)),
+            pl.BlockSpec((1, width + 16, HEAD_DIM), lambda i: (0, 0, 0)),
+        ],
+        out_shape=[
+            jax.ShapeDtypeStruct((blocks, width, HEAD_DIM), jnp.bfloat16),
+            jax.ShapeDtypeStruct((1, width + 16, HEAD_DIM), jnp.bfloat16),
+        ],
     )(qkv, qkv, docs.reshape(blocks, count, 1), docs.reshape(blocks, 1, count))
 
 
@@ -157,18 +179,10 @@
         slot_core = jnp.stack([core, 1 - core])
         block = 2 * sq + slot_core
 
-        tail = tail_states(qkv, docs, heads)
+        own_message, message = tail_states(qkv, docs, heads)
         local_part = local_attention(qkv, docs, heads)
 
-        own_message = tail.astype(jnp.bfloat16).reshape(2, heads * HEAD_DIM, HEAD_DIM)
         own_counted = (block[None, :] < block[:, None]) & (last[None, :] == first[:, None])
-        first_tail, second_tail = jnp.where(core == 0, tail[0], tail[1]), jnp.where(core == 0, tail[1], tail[0])
-        first_last, second_last = jnp.where(core == 0, last[0], last[1]), jnp.where(core == 0, last[1], last[0])
-        chip_tail = second_tail + jnp.where(first_last == second_last, first_tail, 0.0)
-        tag = jnp.broadcast_to(second_last.astype(jnp.bfloat16), (1, 16, HEAD_DIM))
-        message = jnp.concatenate(
-            [chip_tail.astype(jnp.bfloat16).reshape(1, heads * HEAD_DIM, HEAD_DIM), tag], axis=1
-        )
         received = [
             lax.ppermute(message, "sq", [(i, i + shift) for i in range(n_sq - shift)])
             for shift in range(1, n_sq)

time: 246 us -> 245 us (level)
  waiting for transfers between devices: 163 us -> 166 us
    all_gather x1, waiting for transfers between devices: 154 us -> 158 us  [shards(): gathered = lax.all_gather(both, ('sq', 'fsdp'), axis=0, tiled=False)]
  transfers between devices with their start and end apart: 9 -> 9, of which waited for: 5 -> 5; matrix products, arithmetic and copies ran while one was open for 4% -> 3% of each run, Pallas kernels for 3% -> 3%
where the time goes in v14:
time: 245 us
  waiting for transfers between devices  166 us (68%)
  matrix products  21.1 us (9%)
  Pallas kernels  15.9 us (6%)
  between operations  13.6 us (6%)
  local copies, waits for them, and re-layouts  9.92 us (4%)
  other arithmetic  9.22 us (4%)
  starting transfers between devices  8.93 us (4%)
    all_gather x1, waiting for transfers between devices, shards(): gathered = lax.all_gather(both, ('sq', 'fsdp'), axis=0, tiled=False)  158 us
    dot_general x1, matrix products, shards(): jnp.dot(pair, gathered.reshape(width, 3 * half), preferred_element_type=j...  21.1 us
    ppermute x5, waiting for transfers between devices, swap_core(): return lax.ppermute(value, 'core', [(0, 1), (1, 0)])  8.69 us
    ppermute x3, starting transfers between devices, shards(): lax.ppermute(message, 'sq', [(i, i + shift) for i in range(n_sq - shift)])  7.32 us
    pallas_call x1, Pallas kernels, local_attention(): pl.pallas_call(_local_kernel, grid=(blocks,), in_specs=head_specs(count,...  6.69 us
  transfers between devices with their start and end apart: 9, of which 5 were waited for; matrix products, arithmetic and copies ran while one was open for 3% of the time, Pallas kernels for 3%

profile of v14, /device:TPU:0, one launch (start us, length us, event | category | flops | bytes accessed | tf_op | source)
XLA Modules:
  0.0 244.9 jit_solution(9484461834726258911)
XLA Ops:
  6.5 1.0 constant_dynamic-slice_fusion.5
  7.5 1.2 constant_dynamic-slice_fusion.3
  8.8 0.5 collective-permute-start.1
  9.3 1.4 collective-permute-done.1
  10.7 1.0 maximum_select_fusion.1
  11.7 0.0 all-gather.2.cloned.1.call-update
  11.8 0.0 copy-start.4
  11.8 3.2 %copy.17 = bf16[1,512,3072]{1,2,0:T(8,128)(2,1)S(1)} copy(bf16[1,512,3072]{2,1,0:T(8,128)(2,1)} %param.7) | data formatting | bytes 6291456 | tf_op args[0]
  15.0 0.1 mul.58
  15.1 0.7 multiply_reduce_fusion
  15.8 0.9 fusion.6
  16.7 0.0 copy-start.5
  16.7 0.3 copy.18
  17.0 0.4 collective-permute-start
  17.4 0.3 collective-permute-start.2
  17.8 0.1 add_add_fusion
  17.8 4.1 %collective-permute-done.2 = s32[512]{0:T(512)S(1)} collective-permute-done((s32[512]{0:T(512)S(1)}, s32[512]{0:T(512)S(1)}, u32[]{:S(2)}, u32[]{:S(2)}) %collective-permute-start.2) | collective-permute-done | bytes 2080 | tf_op jit(solution)/shard_map/ppermute | solution.py:21
  22.0 1.1 copy.19.dcol_ref
  23.0 0.6 reshape.289.drow_ref
  23.6 0.2 fusion.10
  23.8 0.0 collective-permute-done
  23.9 157.5 %all-gather.2.cloned.1.call-done = bf16[16,2,96,2304]{3,2,1,0:T(8,128)(2,1)} async-done(((bf16[1,2,96,2304]{3,2,1,0:T(8,128)(2,1)}), bf16[16,2,96,2304]{3,2,1,0:T(8,128)(2,1)}) %all-gather.2.cloned.1.call-update) | async-done | bytes 14155792 | tf_op jit(solution)/shard_map/all_gather | solution.py:172
  181.4 21.1 %multiply_convert_fusion.q_ref.k_ref.v_ref = bf16[1024,2304]{1,0:T(8,128)(2,1)} fusion(bf16[3072,2304]{1,0:T(8,128)(2,1)} %bitcast.32, bf16[512,3072]{0,1:T(8,128)(2,1)} %collective-permute-done, bf16[512,3072]{0,1:T(8,128)(2,1)S(1)} %bitcast.26), kind=kOutput, calls=%fused_computation | convolution fusion | flops 14519894016 | bytes 25165824 | tf_op jit(solution)/shard_map/dot_general | solution.py:173
  202.5 4.8 %shard_map.74 = (bf16[2,768,128]{2,1,0:T(8,128)(2,1)}, bf16[1,784,128]{2,1,0:T(8,128)(2,1)}) custom-call(bf16[1024,2304]{1,0:T(8,128)(2,1)} %multiply_convert_fusion.q_ref.k_ref.v_ref, bf16[1024,2304]{1,0:T(8,128)(2,1)} %multiply_convert_fusion.q_ref.k_ref.v_ref, s32[2,512,1]{2,1,0:T(8,128)} %copy.19.dcol_ref, s32[2,1,512]{2,1,0:T(1,128)} %reshape.289.drow_ref), custom_call_target="tpu_custom_call" | custom-call | tf_op jit(solution)/shard_map/pallas_call | solution.py:110
  207.2 3.4 %collective-permute-start.3 = (bf16[1,784,128]{2,1,0:T(8,128)(2,1)}, bf16[1,784,128]{2,1,0:T(8,128)(2,1)S(1)}, u32[]{:S(2)}, u32[]{:S(2)}) collective-permute-start(bf16[1,784,128]{2,1,0:T(8,128)(2,1)} %get-tuple-element.7), channel_id=1, source_target_pairs={{0,8},{8,16},{16,24},{1,9},{9,17},{17,25},{2,10},{10,18},{18,26},{... | collective-permute-start | bytes 602120 | tf_op jit(solution)/shard_map/ppermute | solution.py:187
  210.6 2.5 %collective-permute-start.4 = (bf16[1,784,128]{2,1,0:T(8,128)(2,1)}, bf16[1,784,128]{2,1,0:T(8,128)(2,1)S(1)}, u32[]{:S(2)}, u32[]{:S(2)}) collective-permute-start(bf16[1,784,128]{2,1,0:T(8,128)(2,1)} %get-tuple-element.7), channel_id=1, source_target_pairs={{0,16},{8,24},{1,17},{9,25},{2,18},{10,26},{3,19},{11,27},{4,20},{... | collective-permute-start | bytes 602120 | tf_op jit(solution)/shard_map/ppermute | solution.py:187
  213.1 1.5 collective-permute-start.5
  214.6 0.1 compare_and_fusion.1
  214.7 6.7 %shard_map.73.local_ref = f32[1024,768]{1,0:T(8,128)} custom-call(bf16[1024,2304]{1,0:T(8,128)(2,1)} %multiply_convert_fusion.q_ref.k_ref.v_ref, bf16[1024,2304]{1,0:T(8,128)(2,1)} %multiply_convert_fusion.q_ref.k_ref.v_ref, bf16[1024,2304]{1,0:T(8,128)(2,1)} %multiply_convert_fusion.q_ref.k_ref.v_ref, s32[2,512,1]{2,1,0:T(8,128)} %copy.19.dcol_ref, ...), custom_call_target="tpu_custom_call" | custom-call | tf_op jit(solution)/shard_map/pallas_call | solution.py:98
  221.4 0.0 collective-permute-done.3.rest_1_
  221.4 0.5 slice.36
  221.9 0.5 slice.37
  222.4 0.5 slice.38
  223.0 1.8 maximum_convert_fusion
  224.7 0.1 compare_and_fusion
  224.8 0.1 add_convert_fusion
  224.9 0.7 broadcast_in_dim.2.counted_ref
  225.6 4.5 %shard_map.75 = f32[1024,768]{1,0:T(8,128)} custom-call(f32[1024,768]{1,0:T(8,128)} %shard_map.73.local_ref, bf16[1024,2304]{1,0:T(8,128)(2,1)} %multiply_convert_fusion.q_ref.k_ref.v_ref, f32[2,5,1,128]{3,2,1,0:T(1,128)} %broadcast_in_dim.2.counted_ref, s32[2,512,1]{2,1,0:T(8,128)} %copy.19.dcol_ref, ...), custom_call_target="tpu_custom_call", output_to_operand_aliasing={{}: (0, {})} | custom-call | tf_op jit(solution)/shard_map/pallas_call | solution.py:135
  230.0 2.3 multiply_reduce_fusion.1
  232.4 0.1 collective-permute-start.6
  232.5 0.1 dynamic_slice.27
  232.6 1.1 collective-permute-done.6
  233.6 0.1 rev.3
  233.7 0.3 multiply_convert_fusion.2
  234.1 0.1 fusion.13
  234.2 0.2 collective-permute-start.7
  234.4 2.1 collective-permute-done.7
  236.5 1.5 maximum_select_fusion
  (22 shorter events, 0.1 us)
Async XLA Ops:
  6.5 174.9 %all-gather.2.cloned.1.call-start = ((), (), s32[]{:S(2)}) async-start(), calls=%async_computation | async-start | bytes 15040512 | tf_op jit(solution)/shard_map/all_gather | solution.py:172
  8.8 1.9 collective-permute-start.1
  11.8 3.2 %copy-start.4 = (f32[3072]{0:T(1024)S(1)}, f32[3072]{0:T(1024)}, u32[]{:S(2)}) copy-start(f32[3072]{0:T(1024)} %param.9) | copy-start | bytes 36868
  16.7 0.7 copy-start.5
  17.0 6.9 %collective-permute-start = (bf16[512,3072]{0,1:T(8,128)(2,1)S(1)}, bf16[512,3072]{0,1:T(8,128)(2,1)}, u32[]{:S(2)}, u32[]{:S(2)}) collective-permute-start(bf16[512,3072]{0,1:T(8,128)(2,1)S(1)} %bitcast.25), channel_id=1, source_target_pairs={{0,4},{4,0},{1,5},{5,1},{2,6},{6,2},{3,7},{7,3},{8,12},{12,8},{9,1... | collective-permute-start | bytes 9437192 | tf_op jit(solution)/shard_map/ppermute | solution.py:21
  17.4 4.6 %collective-permute-start.2 = (s32[512]{0:T(512)S(1)}, s32[512]{0:T(512)S(1)}, u32[]{:S(2)}, u32[]{:S(2)}) collective-permute-start(s32[512]{0:T(512)S(1)} %bitcast.29), channel_id=1, source_target_pairs={{0,4},{4,0},{1,5},{5,1},{2,6},{6,2},{3,7},{7,3},{8,12},{12,8},{9,1... | collective-permute-start | bytes 6152 | tf_op jit(solution)/shard_map/ppermute | solution.py:21
  207.2 14.1 %collective-permute-start.3 = (bf16[1,784,128]{2,1,0:T(8,128)(2,1)}, bf16[1,784,128]{2,1,0:T(8,128)(2,1)S(1)}, u32[]{:S(2)}, u32[]{:S(2)}) collective-permute-start(bf16[1,784,128]{2,1,0:T(8,128)(2,1)} %get-tuple-element.7), channel_id=1, source_target_pairs={{0,8},{8,16},{16,24},{1,9},{9,17},{17,25},{2,10},{10,18},{18,26},{... | collective-permute-start | bytes 602120 | tf_op jit(solution)/shard_map/ppermute | solution.py:187
  210.6 11.3 %collective-permute-start.4 = (bf16[1,784,128]{2,1,0:T(8,128)(2,1)}, bf16[1,784,128]{2,1,0:T(8,128)(2,1)S(1)}, u32[]{:S(2)}, u32[]{:S(2)}) collective-permute-start(bf16[1,784,128]{2,1,0:T(8,128)(2,1)} %get-tuple-element.7), channel_id=1, source_target_pairs={{0,16},{8,24},{1,17},{9,25},{2,18},{10,26},{3,19},{11,27},{4,20},{... | collective-permute-start | bytes 602120 | tf_op jit(solution)/shard_map/ppermute | solution.py:187
  213.1 9.3 %collective-permute-start.5 = (bf16[1,784,128]{2,1,0:T(8,128)(2,1)}, bf16[1,784,128]{2,1,0:T(8,128)(2,1)S(1)}, u32[]{:S(2)}, u32[]{:S(2)}) collective-permute-start(bf16[1,784,128]{2,1,0:T(8,128)(2,1)} %get-tuple-element.7), channel_id=1, source_target_pairs={{0,24},{1,25},{2,26},{3,27},{4,28},{5,29},{6,30},{7,31}} | collective-permute-start | bytes 602120 | tf_op jit(solution)/shard_map/ppermute | solution.py:187
  221.4 4.2 %copy-start.1 = (bf16[1,784,128]{2,1,0:T(8,128)(2,1)}, bf16[1,784,128]{2,1,0:T(8,128)(2,1)S(1)}, u32[]{:S(2)}) copy-start(bf16[1,784,128]{2,1,0:T(8,128)(2,1)S(1)} %collective-permute-done.3.rest_1_) | copy-start | bytes 602116
  221.9 3.7 %copy-start.2 = (bf16[1,784,128]{2,1,0:T(8,128)(2,1)}, bf16[1,784,128]{2,1,0:T(8,128)(2,1)S(1)}, u32[]{:S(2)}) copy-start(bf16[1,784,128]{2,1,0:T(8,128)(2,1)S(1)} %collective-permute-done.4.rest_2_) | copy-start | bytes 602116
  222.4 3.2 %copy-start.3 = (bf16[1,784,128]{2,1,0:T(8,128)(2,1)}, bf16[1,784,128]{2,1,0:T(8,128)(2,1)S(1)}, u32[]{:S(2)}) copy-start(bf16[1,784,128]{2,1,0:T(8,128)(2,1)S(1)} %collective-permute-done.5.rest_3_) | copy-start | bytes 602116
  230.0 2.4 copy-start.6
  230.0 3.7 %copy-start = (f32[1024,768]{1,0:T(8,128)S(1)}, f32[1024,768]{1,0:T(8,128)}, u32[]{:S(2)}) copy-start(f32[1024,768]{1,0:T(8,128)} %shard_map.75) | copy-start | bytes 9437188
  232.4 1.2 collective-permute-start.6
  234.2 2.4 collective-permute-start.7
Sparse Core Ops, SparseCore 0:
  11.9 169.4 all-gather.1

commit v15 on v14

--- a/solution.py
+++ b/solution.py
@@ -158,6 +158,17 @@
         normed = normed.reshape(count, width)
         pair = jnp.concatenate([normed, swap_core(normed)], axis=0)
 
+        own_docs = doc_ids[0]
+        docs = jnp.stack([own_docs, swap_core(own_docs)])
+        first, last = docs[:, 0], docs[:, -1]
+        chip_last = jnp.stack(
+            [
+                lax.ppermute(jnp.max(last), "sq", [(i, i + shift) for i in range(n_sq - shift)])
+                for shift in range(1, n_sq)
+            ]
+        )
+        pair, chip_last = lax.optimization_barrier((pair, chip_last))
+
         def halves(start):
             return jnp.concatenate(
                 [
@@ -173,9 +184,6 @@
         summed = jnp.dot(pair, gathered.reshape(width, 3 * half), preferred_element_type=jnp.float32)
         qkv = jax.nn.silu(summed).astype(jnp.bfloat16)
 
-        own_docs = doc_ids[0]
-        docs = jnp.stack([own_docs, swap_core(own_docs)])
-        first, last = docs[:, 0], docs[:, -1]
         slot_core = jnp.stack([core, 1 - core])
         block = 2 * sq + slot_core
 
@@ -187,7 +195,6 @@
             lax.ppermute(message, "sq", [(i, i + shift) for i in range(n_sq - shift)])
             for shift in range(1, n_sq)
         ]
-        chip_last = jnp.stack([got[0, heads * HEAD_DIM, 0] for got in received]).astype(jnp.int32)
         shifts = jnp.arange(1, n_sq, dtype=jnp.int32)
         far_counted = (shifts <= sq)[None, :] & (chip_last[None, :] == first[:, None])
         counted = jnp.concatenate([own_counted, far_counted], axis=1)

time: 245 us -> 243 us (level)
  waiting for transfers between devices: 166 us -> 148 us
  starting transfers between devices: 8.93 us -> 19.3 us
  other arithmetic: 9.22 us -> 15.4 us
    all_gather x1, waiting for transfers between devices: 158 us -> 139 us  [shards(): gathered = lax.all_gather(both, ('sq', 'fsdp'), axis=0, tiled=False)]
    ppermute x0 -> x3, starting transfers between devices: none -> 10.3 us  [shards(): lax.ppermute(jnp.max(last), 'sq', [(i, i + shift) for i in range(n_sq - s...]
    concatenate x0 -> x1, other arithmetic: none -> 5.36 us  [shards(): pair = jnp.concatenate([normed, swap_core(normed)], axis=0)]
  transfers between devices with their start and end apart: 9 -> 12, of which waited for: 5 -> 5; matrix products, arithmetic and copies ran while one was open for 3% -> 6% of each run, Pallas kernels for 3% -> 3%
where the time goes in v15:
time: 243 us; the launch traced here: 242 us
  waiting for transfers between devices  148 us (61%)
  matrix products  21.8 us (9%)
  starting transfers between devices  19.3 us (8%)
  Pallas kernels  15.9 us (7%)
  other arithmetic  15.4 us (6%)
  between operations  13.6 us (6%)
  local copies, waits for them, and re-layouts  8.43 us (3%)
    all_gather x1, waiting for transfers between devices, shards(): gathered = lax.all_gather(both, ('sq', 'fsdp'), axis=0, tiled=False)  139 us
    dot_general x1, matrix products, shards(): jnp.dot(pair, gathered.reshape(width, 3 * half), preferred_element_type=j...  21.8 us
    ppermute x3, starting transfers between devices, shards(): lax.ppermute(jnp.max(last), 'sq', [(i, i + shift) for i in range(n_sq - s...  10.3 us
    ppermute x5, waiting for transfers between devices, swap_core(): return lax.ppermute(value, 'core', [(0, 1), (1, 0)])  8.69 us
    ppermute x3, starting transfers between devices, shards(): lax.ppermute(message, 'sq', [(i, i + shift) for i in range(n_sq - shift)])  7.32 us
    pallas_call x1, Pallas kernels, local_attention(): pl.pallas_call(_local_kernel, grid=(blocks,), in_specs=head_specs(count,...  6.68 us
    concatenate x1, other arithmetic, shards(): pair = jnp.concatenate([normed, swap_core(normed)], axis=0)  5.36 us
  transfers between devices with their start and end apart: 12, of which 5 were waited for; matrix products, arithmetic and copies ran while one was open for 6% of the time, Pallas kernels for 3%

profile of v15, /device:TPU:0, one launch (start us, length us, event | category | flops | bytes accessed | tf_op | source)
XLA Modules:
  0.0 242.3 jit_solution(11046895982425983656)
XLA Ops:
  6.5 1.0 constant_dynamic-slice_fusion.5
  7.6 1.2 constant_dynamic-slice_fusion.3
  8.8 0.5 collective-permute-start.5
  9.3 1.4 collective-permute-done.5
  10.7 1.0 maximum_select_fusion.1
  11.8 0.0 all-gather.2.cloned.1.call-update
  11.8 0.1 mul.58
  11.9 3.2 %copy.17 = bf16[1,512,3072]{1,2,0:T(8,128)(2,1)S(1)} copy(bf16[1,512,3072]{2,1,0:T(8,128)(2,1)} %param.7) | data formatting | bytes 6291456 | tf_op args[0]
  15.1 0.7 multiply_reduce_fusion
  15.8 0.9 fusion
  16.7 0.0 copy-start.5
  16.7 0.3 copy.18
  17.0 0.4 collective-permute-start
  17.4 0.3 collective-permute-start.1
  17.7 0.1 add_add_fusion
  17.8 4.1 %collective-permute-done.1 = s32[512]{0:T(512)S(1)} collective-permute-done((s32[512]{0:T(512)S(1)}, s32[512]{0:T(512)S(1)}, u32[]{:S(2)}, u32[]{:S(2)}) %collective-permute-start.1) | collective-permute-done | bytes 2080 | tf_op jit(solution)/shard_map/ppermute | solution.py:21
  21.9 0.1 fusion.3
  22.1 0.8 fusion.5
  22.8 6.1 %collective-permute-start.4 = (s32[]{:T(128)}, s32[]{:T(128)}, u32[]{:S(2)}, u32[]{:S(2)}) collective-permute-start(s32[]{:T(128)} %get-tuple-element.14), channel_id=1, source_target_pairs={{0,24},{1,25},{2,26},{3,27},{4,28},{5,29},{6,30},{7,31}} | collective-permute-start | bytes 20 | tf_op jit(solution)/shard_map/ppermute | solution.py:166
  28.9 1.8 collective-permute-start.3
  30.7 2.4 %collective-permute-start.2 = (s32[]{:T(128)}, s32[]{:T(128)}, u32[]{:S(2)}, u32[]{:S(2)}) collective-permute-start(s32[]{:T(128)} %get-tuple-element.14), channel_id=1, source_target_pairs={{0,8},{8,16},{16,24},{1,9},{9,17},{17,25},{2,10},{10,18},{18,26},{... | collective-permute-start | bytes 20 | tf_op jit(solution)/shard_map/ppermute | solution.py:166
  33.2 1.1 copy.19.dcol_ref
  34.2 0.6 reshape.265.drow_ref
  34.8 0.1 compare_and_fusion.1
  34.9 1.9 pad_add_fusion.1
  36.8 5.4 %pad_maximum_fusion = bf16[1024,3072]{0,1:T(8,128)(2,1)} fusion(bf16[512,3072]{0,1:T(8,128)(2,1)} %collective-permute-done, bf16[512,3072]{0,1:T(8,128)(2,1)S(1)} %bitcast.27), kind=kLoop, calls=%fused_computation.1 | loop fusion | flops 12582912 | bytes 12582912 | tf_op jit(solution)/shard_map/concatenate | solution.py:159
  42.2 139.2 %all-gather.2.cloned.1.call-done = bf16[16,2,96,2304]{3,2,1,0:T(8,128)(2,1)} async-done(((bf16[1,2,96,2304]{3,2,1,0:T(8,128)(2,1)}), bf16[16,2,96,2304]{3,2,1,0:T(8,128)(2,1)}) %all-gather.2.cloned.1.call-update) | async-done | bytes 14155792 | tf_op jit(solution)/shard_map/all_gather | solution.py:183
  181.4 21.8 %multiply_convert_fusion.q_ref.k_ref.v_ref = bf16[1024,2304]{1,0:T(8,128)(2,1)} fusion(bf16[1024,3072]{0,1:T(8,128)(2,1)} %pad_maximum_fusion, bf16[3072,2304]{1,0:T(8,128)(2,1)} %bitcast.33), kind=kOutput, calls=%fused_computation | convolution fusion | flops 14507311104 | bytes 25165824 | tf_op jit(solution)/shard_map/dot_general | solution.py:184
  203.2 4.7 %shard_map.74 = (bf16[2,768,128]{2,1,0:T(8,128)(2,1)}, bf16[1,784,128]{2,1,0:T(8,128)(2,1)}) custom-call(bf16[1024,2304]{1,0:T(8,128)(2,1)} %multiply_convert_fusion.q_ref.k_ref.v_ref, bf16[1024,2304]{1,0:T(8,128)(2,1)} %multiply_convert_fusion.q_ref.k_ref.v_ref, s32[2,512,1]{2,1,0:T(8,128)} %copy.19.dcol_ref, s32[2,1,512]{2,1,0:T(1,128)} %reshape.265.drow_ref), custom_call_target="tpu_custom_call" | custom-call | tf_op jit(solution)/shard_map/pallas_call | solution.py:110
  208.0 3.3 %collective-permute-start.6 = (bf16[1,784,128]{2,1,0:T(8,128)(2,1)}, bf16[1,784,128]{2,1,0:T(8,128)(2,1)S(1)}, u32[]{:S(2)}, u32[]{:S(2)}) collective-permute-start(bf16[1,784,128]{2,1,0:T(8,128)(2,1)} %get-tuple-element.12), channel_id=1, source_target_pairs={{0,8},{8,16},{16,24},{1,9},{9,17},{17,25},{2,10},{10,18},{18,26},{... | collective-permute-start | bytes 602120 | tf_op jit(solution)/shard_map/ppermute | solution.py:195
  211.3 2.5 %collective-permute-start.7 = (bf16[1,784,128]{2,1,0:T(8,128)(2,1)}, bf16[1,784,128]{2,1,0:T(8,128)(2,1)S(1)}, u32[]{:S(2)}, u32[]{:S(2)}) collective-permute-start(bf16[1,784,128]{2,1,0:T(8,128)(2,1)} %get-tuple-element.12), channel_id=1, source_target_pairs={{0,16},{8,24},{1,17},{9,25},{2,18},{10,26},{3,19},{11,27},{4,20},{... | collective-permute-start | bytes 602120 | tf_op jit(solution)/shard_map/ppermute | solution.py:195
  213.8 1.5 collective-permute-start.8
  215.3 0.1 compare_and_fusion
  215.4 0.1 add_convert_fusion
  215.5 6.7 %shard_map.73.local_ref = f32[1024,768]{1,0:T(8,128)} custom-call(bf16[1024,2304]{1,0:T(8,128)(2,1)} %multiply_convert_fusion.q_ref.k_ref.v_ref, bf16[1024,2304]{1,0:T(8,128)(2,1)} %multiply_convert_fusion.q_ref.k_ref.v_ref, bf16[1024,2304]{1,0:T(8,128)(2,1)} %multiply_convert_fusion.q_ref.k_ref.v_ref, s32[2,512,1]{2,1,0:T(8,128)} %copy.19.dcol_ref, ...), custom_call_target="tpu_custom_call" | custom-call | tf_op jit(solution)/shard_map/pallas_call | solution.py:98
  222.2 0.8 broadcast_in_dim.2.counted_ref
  223.0 0.0 copy-done.3
  223.0 4.5 %shard_map.75 = f32[1024,768]{1,0:T(8,128)} custom-call(f32[1024,768]{1,0:T(8,128)} %shard_map.73.local_ref, bf16[1024,2304]{1,0:T(8,128)(2,1)} %multiply_convert_fusion.q_ref.k_ref.v_ref, f32[2,5,1,128]{3,2,1,0:T(1,128)} %broadcast_in_dim.2.counted_ref, s32[2,512,1]{2,1,0:T(8,128)} %copy.19.dcol_ref, ...), custom_call_target="tpu_custom_call", output_to_operand_aliasing={{}: (0, {})} | custom-call | tf_op jit(solution)/shard_map/pallas_call | solution.py:135
  227.5 2.3 multiply_reduce_fusion.1
  229.8 0.1 collective-permute-start.9
  229.9 0.1 dynamic_slice.27
  230.0 1.1 collective-permute-done.9
  231.0 0.1 rev.3
  231.2 0.3 multiply_convert_fusion.2
  231.5 0.1 fusion.6
  231.6 0.2 collective-permute-start.10
  231.8 2.1 collective-permute-done.10
  234.0 1.5 maximum_select_fusion
  (27 shorter events, 0.1 us)
Async XLA Ops:
  6.5 5.2 %copy-start.4 = (f32[3072]{0:T(1024)S(1)}, f32[3072]{0:T(1024)}, u32[]{:S(2)}) copy-start(f32[3072]{0:T(1024)} %param.9) | copy-start | bytes 36868
  6.5 174.9 %all-gather.2.cloned.1.call-start = ((), (), s32[]{:S(2)}) async-start(), calls=%async_computation | async-start | bytes 15040512 | tf_op jit(solution)/shard_map/all_gather | solution.py:183
  8.8 1.9 collective-permute-start.5
  16.7 0.7 copy-start.5
  17.0 19.9 %collective-permute-start = (bf16[512,3072]{0,1:T(8,128)(2,1)S(1)}, bf16[512,3072]{0,1:T(8,128)(2,1)}, u32[]{:S(2)}, u32[]{:S(2)}) collective-permute-start(bf16[512,3072]{0,1:T(8,128)(2,1)S(1)} %bitcast.26), channel_id=1, source_target_pairs={{0,4},{4,0},{1,5},{5,1},{2,6},{6,2},{3,7},{7,3},{8,12},{12,8},{9,1... | collective-permute-start | bytes 9437192 | tf_op jit(solution)/shard_map/ppermute | solution.py:21
  17.4 4.6 %collective-permute-start.1 = (s32[512]{0:T(512)S(1)}, s32[512]{0:T(512)S(1)}, u32[]{:S(2)}, u32[]{:S(2)}) collective-permute-start(s32[512]{0:T(512)S(1)} %bitcast.30), channel_id=1, source_target_pairs={{0,4},{4,0},{1,5},{5,1},{2,6},{6,2},{3,7},{7,3},{8,12},{12,8},{9,1... | collective-permute-start | bytes 6152 | tf_op jit(solution)/shard_map/ppermute | solution.py:21
  22.8 12.1 %collective-permute-start.4 = (s32[]{:T(128)}, s32[]{:T(128)}, u32[]{:S(2)}, u32[]{:S(2)}) collective-permute-start(s32[]{:T(128)} %get-tuple-element.14), channel_id=1, source_target_pairs={{0,24},{1,25},{2,26},{3,27},{4,28},{5,29},{6,30},{7,31}} | collective-permute-start | bytes 20 | tf_op jit(solution)/shard_map/ppermute | solution.py:166
  28.9 6.0 %collective-permute-start.3 = (s32[]{:T(128)}, s32[]{:T(128)}, u32[]{:S(2)}, u32[]{:S(2)}) collective-permute-start(s32[]{:T(128)} %get-tuple-element.14), channel_id=1, source_target_pairs={{0,16},{8,24},{1,17},{9,25},{2,18},{10,26},{3,19},{11,27},{4,20},{... | collective-permute-start | bytes 20 | tf_op jit(solution)/shard_map/ppermute | solution.py:166
  30.7 4.2 %collective-permute-start.2 = (s32[]{:T(128)}, s32[]{:T(128)}, u32[]{:S(2)}, u32[]{:S(2)}) collective-permute-start(s32[]{:T(128)} %get-tuple-element.14), channel_id=1, source_target_pairs={{0,8},{8,16},{16,24},{1,9},{9,17},{17,25},{2,10},{10,18},{18,26},{... | collective-permute-start | bytes 20 | tf_op jit(solution)/shard_map/ppermute | solution.py:166
  208.0 14.2 %collective-permute-start.6 = (bf16[1,784,128]{2,1,0:T(8,128)(2,1)}, bf16[1,784,128]{2,1,0:T(8,128)(2,1)S(1)}, u32[]{:S(2)}, u32[]{:S(2)}) collective-permute-start(bf16[1,784,128]{2,1,0:T(8,128)(2,1)} %get-tuple-element.12), channel_id=1, source_target_pairs={{0,8},{8,16},{16,24},{1,9},{9,17},{17,25},{2,10},{10,18},{18,26},{... | collective-permute-start | bytes 602120 | tf_op jit(solution)/shard_map/ppermute | solution.py:195
  211.3 10.8 %collective-permute-start.7 = (bf16[1,784,128]{2,1,0:T(8,128)(2,1)}, bf16[1,784,128]{2,1,0:T(8,128)(2,1)S(1)}, u32[]{:S(2)}, u32[]{:S(2)}) collective-permute-start(bf16[1,784,128]{2,1,0:T(8,128)(2,1)} %get-tuple-element.12), channel_id=1, source_target_pairs={{0,16},{8,24},{1,17},{9,25},{2,18},{10,26},{3,19},{11,27},{4,20},{... | collective-permute-start | bytes 602120 | tf_op jit(solution)/shard_map/ppermute | solution.py:195
  213.8 8.4 %collective-permute-start.8 = (bf16[1,784,128]{2,1,0:T(8,128)(2,1)}, bf16[1,784,128]{2,1,0:T(8,128)(2,1)S(1)}, u32[]{:S(2)}, u32[]{:S(2)}) collective-permute-start(bf16[1,784,128]{2,1,0:T(8,128)(2,1)} %get-tuple-element.12), channel_id=1, source_target_pairs={{0,24},{1,25},{2,26},{3,27},{4,28},{5,29},{6,30},{7,31}} | collective-permute-start | bytes 602120 | tf_op jit(solution)/shard_map/ppermute | solution.py:195
  222.2 0.8 copy-start.1
  222.2 0.8 copy-start.2
  222.2 0.8 copy-start.3
  227.5 2.4 copy-start.6
  227.5 3.7 %copy-start = (f32[1024,768]{1,0:T(8,128)S(1)}, f32[1024,768]{1,0:T(8,128)}, u32[]{:S(2)}) copy-start(f32[1024,768]{1,0:T(8,128)} %shard_map.75) | copy-start | bytes 9437188
  229.8 1.2 collective-permute-start.9
  231.6 2.4 collective-permute-start.10
Sparse Core Ops, SparseCore 0:
  11.9 169.4 all-gather.1

commit v16 on v15

--- a/solution.py
+++ b/solution.py
@@ -161,13 +161,6 @@
         own_docs = doc_ids[0]
         docs = jnp.stack([own_docs, swap_core(own_docs)])
         first, last = docs[:, 0], docs[:, -1]
-        chip_last = jnp.stack(
-            [
-                lax.ppermute(jnp.max(last), "sq", [(i, i + shift) for i in range(n_sq - shift)])
-                for shift in range(1, n_sq)
-            ]
-        )
-        pair, chip_last = lax.optimization_barrier((pair, chip_last))
 
         def halves(start):
             return jnp.concatenate(
@@ -191,18 +184,18 @@
         local_part = local_attention(qkv, docs, heads)
 
         own_counted = (block[None, :] < block[:, None]) & (last[None, :] == first[:, None])
-        received = [
-            lax.ppermute(message, "sq", [(i, i + shift) for i in range(n_sq - shift)])
-            for shift in range(1, n_sq)
-        ]
-        shifts = jnp.arange(1, n_sq, dtype=jnp.int32)
-        far_counted = (shifts <= sq)[None, :] & (chip_last[None, :] == first[:, None])
+        received = lax.all_to_all(
+            jnp.broadcast_to(message, (n_sq,) + message.shape[1:]), "sq", 0, 0, tiled=True
+        )
+        chip_last = received[:, heads * HEAD_DIM, 0].astype(jnp.int32)
+        sources = jnp.arange(n_sq, dtype=jnp.int32)
+        far_counted = (sources < sq)[None, :] & (chip_last[None, :] == first[:, None])
         counted = jnp.concatenate([own_counted, far_counted], axis=1)
         counted = jnp.broadcast_to(
-            counted.reshape(2, n_sq + 1, 1, 1).astype(jnp.float32), (2, n_sq + 1, 1, HEAD_DIM)
-        )
-
-        mixed = add_past(local_part, qkv, counted, [own_message] + received, docs, heads)
+            counted.reshape(2, n_sq + 2, 1, 1).astype(jnp.float32), (2, n_sq + 2, 1, HEAD_DIM)
+        )
+
+        mixed = add_past(local_part, qkv, counted, [own_message, received], docs, heads)
         mixed = mixed.reshape(2, count, half)
         squares = jnp.sum(mixed * mixed, axis=-1)
         total = squares + swap_core(squares)[::-1]

time: 243 us -> 244 us (level)
  waiting for transfers between devices: 148 us -> 170 us
  starting transfers between devices: 19.3 us -> 5.2 us
  other arithmetic: 15.4 us -> 7.57 us
    all_gather x1, waiting for transfers between devices: 139 us -> 158 us  [shards(): gathered = lax.all_gather(both, ('sq', 'fsdp'), axis=0, tiled=False)]
    ppermute x6 -> x0, starting transfers between devices: 17.6 us -> none  [the longest x3 10.3 us: shards(): lax.ppermute(jnp.max(last), 'sq', [(i, i + shift) for i in range(n_sq - s...]
    concatenate x1 -> x0, other arithmetic: 5.36 us -> none  [shards(): pair = jnp.concatenate([normed, swap_core(normed)], axis=0)]
    all_to_all x0 -> x1, starting transfers between devices: none -> 3.68 us  [shards(): lax.all_to_all(jnp.broadcast_to(message, (n_sq,) + message.shape[1:]), 's...]
    all_to_all x0 -> x1, waiting for transfers between devices: none -> 3.56 us  [shards(): lax.all_to_all(jnp.broadcast_to(message, (n_sq,) + message.shape[1:]), 's...]
  transfers between devices with their start and end apart: 12 -> 7, of which waited for: 5 -> 6; matrix products, arithmetic and copies ran while one was open for 6% -> 3% of each run, Pallas kernels for 3% -> 3%
where the time goes in v16:
time: 244 us
  waiting for transfers between devices  170 us (70%)
  matrix products  20.9 us (9%)
  Pallas kernels  16.1 us (7%)
  between operations  13.6 us (6%)
  local copies, waits for them, and re-layouts  10.3 us (4%)
  other arithmetic  7.57 us (3%)
  starting transfers between devices  5.2 us (2%)
    all_gather x1, waiting for transfers between devices, shards(): gathered = lax.all_gather(both, ('sq', 'fsdp'), axis=0, tiled=False)  158 us
    dot_general x1, matrix products, shards(): jnp.dot(pair, gathered.reshape(width, 3 * half), preferred_element_type=j...  20.9 us
    ppermute x5, waiting for transfers between devices, swap_core(): return lax.ppermute(value, 'core', [(0, 1), (1, 0)])  8.86 us
    pallas_call x1, Pallas kernels, local_attention(): pl.pallas_call(_local_kernel, grid=(blocks,), in_specs=head_specs(count,...  6.71 us
  transfers between devices with their start and end apart: 7, of which 6 were waited for; matrix products, arithmetic and copies ran while one was open for 3% of the time, Pallas kernels for 3%

profile of v16, /device:TPU:0, one launch (start us, length us, event | category | flops | bytes accessed | tf_op | source)
XLA Modules:
  0.0 243.9 jit_solution(16983279624002306699)
XLA Ops:
  6.5 0.0 all-gather.2.cloned.1.call-start
  6.5 1.0 constant_dynamic-slice_fusion.5
  7.5 1.2 constant_dynamic-slice_fusion.3
  8.8 0.5 collective-permute-start.1
  9.3 1.4 collective-permute-done.1
  10.7 1.0 maximum_select_fusion.1
  11.7 0.0 all-gather.2.cloned.1.call-update
  11.8 0.0 copy-start.2
  11.8 3.2 %copy.17 = bf16[1,512,3072]{1,2,0:T(8,128)(2,1)S(1)} copy(bf16[1,512,3072]{2,1,0:T(8,128)(2,1)} %param.7) | data formatting | bytes 6291456 | tf_op args[0]
  15.0 0.0 copy-done.2
  15.0 0.1 mul.58
  15.1 0.7 multiply_reduce_fusion
  15.8 0.9 fusion.6
  16.7 0.0 copy-start.3
  16.7 0.3 copy.18
  17.0 0.4 collective-permute-start
  17.5 0.0 copy-done.3
  17.5 0.3 collective-permute-start.2
  17.7 4.3 %collective-permute-done.2 = s32[512]{0:T(512)S(1)} collective-permute-done((s32[512]{0:T(512)S(1)}, s32[512]{0:T(512)S(1)}, u32[]{:S(2)}, u32[]{:S(2)}) %collective-permute-start.2) | collective-permute-done | bytes 2080 | tf_op jit(solution)/shard_map/ppermute | solution.py:21
  22.0 1.0 copy.19.dcol_ref
  23.1 0.6 reshape.270.drow_ref
  23.7 0.0 collective-permute-done
  23.7 157.7 %all-gather.2.cloned.1.call-done = bf16[16,2,96,2304]{3,2,1,0:T(8,128)(2,1)} async-done(((bf16[1,2,96,2304]{3,2,1,0:T(8,128)(2,1)}), bf16[16,2,96,2304]{3,2,1,0:T(8,128)(2,1)}) %all-gather.2.cloned.1.call-update) | async-done | bytes 14155792 | tf_op jit(solution)/shard_map/all_gather | solution.py:176
  181.4 20.9 %multiply_convert_fusion.q_ref.k_ref.v_ref = bf16[1024,2304]{1,0:T(8,128)(2,1)} fusion(bf16[3072,2304]{1,0:T(8,128)(2,1)} %bitcast.31, bf16[512,3072]{0,1:T(8,128)(2,1)} %collective-permute-done, bf16[512,3072]{0,1:T(8,128)(2,1)S(1)} %bitcast.24), kind=kOutput, calls=%fused_computation | convolution fusion | flops 14519894016 | bytes 25165824 | tf_op jit(solution)/shard_map/dot_general | solution.py:177
  202.3 4.8 %shard_map.74 = (bf16[2,768,128]{2,1,0:T(8,128)(2,1)}, bf16[1,784,128]{2,1,0:T(8,128)(2,1)}) custom-call(bf16[1024,2304]{1,0:T(8,128)(2,1)} %multiply_convert_fusion.q_ref.k_ref.v_ref, bf16[1024,2304]{1,0:T(8,128)(2,1)} %multiply_convert_fusion.q_ref.k_ref.v_ref, s32[2,512,1]{2,1,0:T(8,128)} %copy.19.dcol_ref, s32[2,1,512]{2,1,0:T(1,128)} %reshape.270.drow_ref), custom_call_target="tpu_custom_call" | custom-call | tf_op jit(solution)/shard_map/pallas_call | solution.py:110
  207.1 1.9 broadcast_in_dim.7
  209.0 3.7 %all-to-all-start = ((bf16[4,784,128]{2,1,0:T(8,128)(2,1)}), bf16[4,784,128]{2,1,0:T(8,128)(2,1)S(1)}, u32[]{:S(2)}, u32[]{:S(2)}) async-start(bf16[4,784,128]{2,1,0:T(8,128)(2,1)} %broadcast_in_dim.7), calls=%async_computation | async-start | bytes 1605632 | tf_op jit(solution)/shard_map/all_to_all | solution.py:187
  212.7 0.1 add_add_fusion
  212.8 0.2 fusion.11
  213.0 0.1 compare_and_fusion.1
  213.1 6.7 %shard_map.73.local_ref = f32[1024,768]{1,0:T(8,128)} custom-call(bf16[1024,2304]{1,0:T(8,128)(2,1)} %multiply_convert_fusion.q_ref.k_ref.v_ref, bf16[1024,2304]{1,0:T(8,128)(2,1)} %multiply_convert_fusion.q_ref.k_ref.v_ref, bf16[1024,2304]{1,0:T(8,128)(2,1)} %multiply_convert_fusion.q_ref.k_ref.v_ref, s32[2,512,1]{2,1,0:T(8,128)} %copy.19.dcol_ref, ...), custom_call_target="tpu_custom_call" | custom-call | tf_op jit(solution)/shard_map/pallas_call | solution.py:98
  219.8 3.6 %all-to-all-done.rest_1_ = bf16[4,784,128]{2,1,0:T(8,128)(2,1)S(1)} async-done(((bf16[4,784,128]{2,1,0:T(8,128)(2,1)}), bf16[4,784,128]{2,1,0:T(8,128)(2,1)S(1)}, u32[]{:S(2)}, u32[]{:S(2)}) %all-to-all-start) | async-done | bytes 802848 | tf_op jit(solution)/shard_map/all_to_all | solution.py:187
  223.4 0.2 fusion.7
  223.5 0.1 compare_and_fusion
  223.6 0.1 add_convert_fusion
  223.7 0.7 broadcast_in_dim.8.counted_ref
  224.4 4.6 %shard_map.75 = f32[1024,768]{1,0:T(8,128)} custom-call(f32[1024,768]{1,0:T(8,128)} %shard_map.73.local_ref, bf16[1024,2304]{1,0:T(8,128)(2,1)} %multiply_convert_fusion.q_ref.k_ref.v_ref, f32[2,6,1,128]{3,2,1,0:T(1,128)} %broadcast_in_dim.8.counted_ref, s32[2,512,1]{2,1,0:T(8,128)} %copy.19.dcol_ref, ...), custom_call_target="tpu_custom_call", output_to_operand_aliasing={{}: (0, {})} | custom-call | tf_op jit(solution)/shard_map/pallas_call | solution.py:135
  229.0 2.3 multiply_reduce_fusion.1
  231.3 0.1 collective-permute-start.3
  231.4 0.0 copy-done.4
  231.4 0.1 dynamic_slice.27
  231.5 1.1 collective-permute-done.3
  232.6 0.1 rev.3
  232.7 0.3 multiply_convert_fusion.2
  233.0 0.1 fusion.14
  233.2 0.2 collective-permute-start.4
  233.4 2.1 collective-permute-done.4
  235.5 1.5 maximum_select_fusion
  (12 shorter events, 0.1 us)
Async XLA Ops:
  6.5 174.9 %all-gather.2.cloned.1.call-start = ((), (), s32[]{:S(2)}) async-start(), calls=%async_computation.1 | async-start | bytes 15040512 | tf_op jit(solution)/shard_map/all_gather | solution.py:176
  8.8 1.9 collective-permute-start.1
  11.8 3.2 %copy-start.2 = (f32[3072]{0:T(1024)S(1)}, f32[3072]{0:T(1024)}, u32[]{:S(2)}) copy-start(f32[3072]{0:T(1024)} %param.9) | copy-start | bytes 36868
  16.7 0.8 copy-start.3
  17.0 6.6 %collective-permute-start = (bf16[512,3072]{0,1:T(8,128)(2,1)S(1)}, bf16[512,3072]{0,1:T(8,128)(2,1)}, u32[]{:S(2)}, u32[]{:S(2)}) collective-permute-start(bf16[512,3072]{0,1:T(8,128)(2,1)S(1)} %bitcast.23), channel_id=1, source_target_pairs={{0,4},{4,0},{1,5},{5,1},{2,6},{6,2},{3,7},{7,3},{8,12},{12,8},{9,1... | collective-permute-start | bytes 9437192 | tf_op jit(solution)/shard_map/ppermute | solution.py:21
  17.5 4.6 %collective-permute-start.2 = (s32[512]{0:T(512)S(1)}, s32[512]{0:T(512)S(1)}, u32[]{:S(2)}, u32[]{:S(2)}) collective-permute-start(s32[512]{0:T(512)S(1)} %bitcast.28), channel_id=1, source_target_pairs={{0,4},{4,0},{1,5},{5,1},{2,6},{6,2},{3,7},{7,3},{8,12},{12,8},{9,1... | collective-permute-start | bytes 6152 | tf_op jit(solution)/shard_map/ppermute | solution.py:21
  209.0 14.3 %all-to-all-start = ((bf16[4,784,128]{2,1,0:T(8,128)(2,1)}), bf16[4,784,128]{2,1,0:T(8,128)(2,1)S(1)}, u32[]{:S(2)}, u32[]{:S(2)}) async-start(bf16[4,784,128]{2,1,0:T(8,128)(2,1)} %broadcast_in_dim.7), calls=%async_computation | async-start | bytes 1605632 | tf_op jit(solution)/shard_map/all_to_all | solution.py:187
  223.4 1.0 copy-start.1
  229.0 2.4 copy-start.4
  229.0 3.7 %copy-start = (f32[1024,768]{1,0:T(8,128)S(1)}, f32[1024,768]{1,0:T(8,128)}, u32[]{:S(2)}) copy-start(f32[1024,768]{1,0:T(8,128)} %shard_map.75) | copy-start | bytes 9437188
  231.3 1.2 collective-permute-start.3
  233.2 2.4 collective-permute-start.4
Sparse Core Ops, SparseCore 0:
  11.9 169.4 all-gather.1

commit v17 on v15

--- a/solution.py
+++ b/solution.py
@@ -167,7 +167,17 @@
                 for shift in range(1, n_sq)
             ]
         )
-        pair, chip_last = lax.optimization_barrier((pair, chip_last))
+        flipped = pair.reshape(2 * count, n_sq, n_fsdp, 2, rows)[:, :, :, ::-1].reshape(2 * count, width)
+        pair = jnp.where(core == 0, pair, flipped)
+        slot_core = jnp.stack([core, 1 - core])
+        block = 2 * sq + slot_core
+        own_counted = (block[None, :] < block[:, None]) & (last[None, :] == first[:, None])
+        far_counted = (jnp.arange(1, n_sq, dtype=jnp.int32) <= sq)[None, :] & (chip_last[None, :] == first[:, None])
+        counted = jnp.concatenate([own_counted, far_counted], axis=1)
+        counted = jnp.broadcast_to(
+            counted.reshape(2, n_sq + 1, 1, 1).astype(jnp.float32), (2, n_sq + 1, 1, HEAD_DIM)
+        )
+        pair, counted = lax.optimization_barrier((pair, counted))
 
         def halves(start):
             return jnp.concatenate(
@@ -179,7 +189,7 @@
             )
 
         mine, other = halves(core * half), halves((1 - core) * half)
-        both = in_core_order(core, mine, swap_core(other))
+        both = jnp.stack([mine, swap_core(other)])
         gathered = lax.all_gather(both, ("sq", "fsdp"), axis=0, tiled=False)
         summed = jnp.dot(pair, gathered.reshape(width, 3 * half), preferred_element_type=jnp.float32)
         qkv = jax.nn.silu(summed).astype(jnp.bfloat16)
@@ -190,17 +200,10 @@
         own_message, message = tail_states(qkv, docs, heads)
         local_part = local_attention(qkv, docs, heads)
 
-        own_counted = (block[None, :] < block[:, None]) & (last[None, :] == first[:, None])
         received = [
             lax.ppermute(message, "sq", [(i, i + shift) for i in range(n_sq - shift)])
             for shift in range(1, n_sq)
         ]
-        shifts = jnp.arange(1, n_sq, dtype=jnp.int32)
-        far_counted = (shifts <= sq)[None, :] & (chip_last[None, :] == first[:, None])
-        counted = jnp.concatenate([own_counted, far_counted], axis=1)
-        counted = jnp.broadcast_to(
-            counted.reshape(2, n_sq + 1, 1, 1).astype(jnp.float32), (2, n_sq + 1, 1, HEAD_DIM)
-        )
 
         mixed = add_past(local_part, qkv, counted, [own_message] + received, docs, heads)
         mixed = mixed.reshape(2, count, half)

time: 243 us -> 243 us (level)
  waiting for transfers between devices: 148 us -> 128 us
  local copies, waits for them, and re-layouts: 8.43 us -> 20.9 us
  other arithmetic: 15.4 us -> 23 us
    all_gather x1, waiting for transfers between devices: 139 us -> 119 us  [shards(): gathered = lax.all_gather(both, ('sq', 'fsdp'), axis=0, tiled=False)]
    rev x0 -> x2, local copies, waits for them, and re-layouts: none -> 10.3 us  [shards(): pair.reshape(2 * count, n_sq, n_fsdp, 2, rows)[:, :, :, ::-1]]
    select_n x1, other arithmetic: 1.05 us -> 6.4 us  [shards(): pair = jnp.where(core == 0, pair, flipped)]
    unnamed x15 -> x17, local copies, waits for them, and re-layouts: 3.22 us -> 5.45 us
  transfers between devices with their start and end apart: 12 -> 12, of which waited for: 5 -> 5; matrix products, arithmetic and copies ran while one was open for 6% -> 14% of each run, Pallas kernels for 3% -> 3%
where the time goes in v17:
time: 243 us; the launch traced here: 242 us
  waiting for transfers between devices  128 us (53%)
  other arithmetic  23 us (9%)
  matrix products  21.9 us (9%)
  local copies, waits for them, and re-layouts  20.9 us (9%)
  starting transfers between devices  19.1 us (8%)
  Pallas kernels  15.9 us (7%)
  between operations  13.6 us (6%)
    all_gather x1, waiting for transfers between devices, shards(): gathered = lax.all_gather(both, ('sq', 'fsdp'), axis=0, tiled=False)  119 us
    dot_general x1, matrix products, shards(): jnp.dot(pair, gathered.reshape(width, 3 * half), preferred_element_type=j...  21.9 us
    ppermute x3, starting transfers between devices, shards(): lax.ppermute(jnp.max(last), 'sq', [(i, i + shift) for i in range(n_sq - s...  10.4 us
    rev x2, local copies, waits for them, and re-layouts, shards(): pair.reshape(2 * count, n_sq, n_fsdp, 2, rows)[:, :, :, ::-1]  10.3 us
    ppermute x5, waiting for transfers between devices, swap_core(): return lax.ppermute(value, 'core', [(0, 1), (1, 0)])  8.9 us
    ppermute x3, starting transfers between devices, shards(): lax.ppermute(message, 'sq', [(i, i + shift) for i in range(n_sq - shift)])  7.37 us
    pallas_call x1, Pallas kernels, local_attention(): pl.pallas_call(_local_kernel, grid=(blocks,), in_specs=head_specs(count,...  6.7 us
    concatenate x1, other arithmetic, shards(): pair = jnp.concatenate([normed, swap_core(normed)], axis=0)  6.65 us
  transfers between devices with their start and end apart: 12, of which 5 were waited for; matrix products, arithmetic and copies ran while one was open for 14% of the time, Pallas kernels for 3%

profile of v17, /device:TPU:0, one launch (start us, length us, event | category | flops | bytes accessed | tf_op | source)
XLA Modules:
  0.0 242.3 jit_solution(18146405214429842148)
XLA Ops:
  6.5 1.0 constant_dynamic-slice_fusion.5
  7.6 1.2 constant_dynamic-slice_fusion.3
  8.8 0.5 collective-permute-start.5
  9.3 1.4 collective-permute-done.5
  10.7 1.0 pad_maximum_fusion.1
  11.7 0.1 mul.58
  11.8 3.2 %copy.19 = bf16[1,512,3072]{1,2,0:T(8,128)(2,1)S(1)} copy(bf16[1,512,3072]{2,1,0:T(8,128)(2,1)} %param.7) | data formatting | bytes 6291456 | tf_op args[0]
  15.0 0.7 multiply_reduce_fusion
  15.7 0.9 fusion
  16.6 0.3 copy.20
  16.9 1.4 copy-done.1
  18.3 0.4 collective-permute-start
  18.7 0.1 collective-permute-start.1
  18.8 0.1 add_add_fusion
  18.9 4.3 %collective-permute-done.1 = s32[512]{0:T(512)S(1)} collective-permute-done((s32[512]{0:T(512)S(1)}, s32[512]{0:T(512)S(1)}, u32[]{:S(2)}, u32[]{:S(2)}) %collective-permute-start.1) | collective-permute-done | bytes 2080 | tf_op jit(solution)/shard_map/ppermute | solution.py:21
  23.2 0.1 fusion.3
  23.3 0.7 fusion.5
  24.1 6.0 %collective-permute-start.4 = (s32[]{:T(128)}, s32[]{:T(128)}, u32[]{:S(2)}, u32[]{:S(2)}) collective-permute-start(s32[]{:T(128)} %get-tuple-element.14), channel_id=1, source_target_pairs={{0,24},{1,25},{2,26},{3,27},{4,28},{5,29},{6,30},{7,31}} | collective-permute-start | bytes 20 | tf_op jit(solution)/shard_map/ppermute | solution.py:166
  30.1 1.8 collective-permute-start.3
  31.9 2.5 %collective-permute-start.2 = (s32[]{:T(128)}, s32[]{:T(128)}, u32[]{:S(2)}, u32[]{:S(2)}) collective-permute-start(s32[]{:T(128)} %get-tuple-element.14), channel_id=1, source_target_pairs={{0,8},{8,16},{16,24},{1,9},{9,17},{17,25},{2,10},{10,18},{18,26},{... | collective-permute-start | bytes 20 | tf_op jit(solution)/shard_map/ppermute | solution.py:166
  34.5 1.0 copy.23.dcol_ref
  35.5 0.6 reshape.214.drow_ref
  36.2 2.0 pad_add_fusion.1
  38.3 0.1 add_convert_fusion
  38.4 6.7 %pad_maximum_fusion = bf16[1024,4,4,2,96]{0,4,2,3,1:T(8,128)(2,1)} fusion(bf16[512,4,4,2,96]{0,4,2,3,1:T(8,128)(2,1)} %copy-done.1, bf16[512,4,4,2,96]{0,4,3,2,1:T(8,128)(2,1)} %bitcast.3), kind=kLoop, calls=%fused_computation.2 | loop fusion | flops 12582912 | bytes 12582912 | tf_op jit(solution)/shard_map/concatenate | solution.py:159
  45.0 6.6 %rev.6 = bf16[1024,4,4,2,96]{0,4,2,3,1:T(8,128)(2,1)} reverse(bf16[1024,4,4,2,96]{0,4,2,3,1:T(8,128)(2,1)} %pad_maximum_fusion), dimensions={3} | reverse | bytes 12582912 | tf_op jit(solution)/shard_map/rev | solution.py:170
  51.6 3.7 %copy.22 = bf16[1024,4,4,2,96]{0,4,3,2,1:T(8,128)(2,1)S(1)} copy(bf16[1024,4,4,2,96]{0,4,2,3,1:T(8,128)(2,1)} %rev.6) | data formatting | bytes 12582912 | tf_op jit(solution)/shard_map/rev | solution.py:170
  55.3 6.4 %maximum_select_fusion = bf16[1024,3072]{0,1:T(8,128)(2,1)} fusion(bf16[512,3072]{0,1:T(8,128)(2,1)} %collective-permute-done, bf16[512,3072]{0,1:T(8,128)(2,1)S(1)} %bitcast.30, bf16[1024,4,4,2,96]{0,4,3,2,1:T(8,128)(2,1)S(1)} %copy.22, pred[]{:T(512)S(6)} %eq.36), kind=kLoop, calls=%fused_computation.1 | loop fusion | flops 15728640 | bytes 18874368 | tf_op jit(solution)/shard_map/jit(_where)/select_n | solution.py:171
  61.7 0.7 broadcast_in_dim.2.counted_ref
  62.4 119.0 %all-gather.3.cloned.1.call-done = bf16[32,96,2304]{2,1,0:T(8,128)(2,1)} async-done(((bf16[2,96,2304]{2,1,0:T(8,128)(2,1)}), bf16[32,96,2304]{2,1,0:T(8,128)(2,1)}) %all-gather.3.cloned.1.call-update) | async-done | bytes 14155792 | tf_op jit(solution)/shard_map/all_gather | solution.py:193
  181.3 21.9 %multiply_convert_fusion.q_ref.k_ref.v_ref = bf16[1024,2304]{1,0:T(8,128)(2,1)} fusion(bf16[1024,3072]{0,1:T(8,128)(2,1)} %maximum_select_fusion, bf16[3072,2304]{1,0:T(8,128)(2,1)} %bitcast.36), kind=kOutput, calls=%fused_computation | convolution fusion | flops 14507311104 | bytes 25165824 | tf_op jit(solution)/shard_map/dot_general | solution.py:194
  203.2 4.8 %shard_map.74 = (bf16[2,768,128]{2,1,0:T(8,128)(2,1)}, bf16[1,784,128]{2,1,0:T(8,128)(2,1)}) custom-call(bf16[1024,2304]{1,0:T(8,128)(2,1)} %multiply_convert_fusion.q_ref.k_ref.v_ref, bf16[1024,2304]{1,0:T(8,128)(2,1)} %multiply_convert_fusion.q_ref.k_ref.v_ref, s32[2,512,1]{2,1,0:T(8,128)} %copy.23.dcol_ref, s32[2,1,512]{2,1,0:T(1,128)} %reshape.214.drow_ref), custom_call_target="tpu_custom_call" | custom-call | tf_op jit(solution)/shard_map/pallas_call | solution.py:110
  208.0 3.4 %collective-permute-start.6 = (bf16[1,784,128]{2,1,0:T(8,128)(2,1)}, bf16[1,784,128]{2,1,0:T(8,128)(2,1)S(1)}, u32[]{:S(2)}, u32[]{:S(2)}) collective-permute-start(bf16[1,784,128]{2,1,0:T(8,128)(2,1)} %get-tuple-element.12), channel_id=1, source_target_pairs={{0,8},{8,16},{16,24},{1,9},{9,17},{17,25},{2,10},{10,18},{18,26},{... | collective-permute-start | bytes 602120 | tf_op jit(solution)/shard_map/ppermute | solution.py:204
  211.4 2.5 %collective-permute-start.7 = (bf16[1,784,128]{2,1,0:T(8,128)(2,1)}, bf16[1,784,128]{2,1,0:T(8,128)(2,1)S(1)}, u32[]{:S(2)}, u32[]{:S(2)}) collective-permute-start(bf16[1,784,128]{2,1,0:T(8,128)(2,1)} %get-tuple-element.12), channel_id=1, source_target_pairs={{0,16},{8,24},{1,17},{9,25},{2,18},{10,26},{3,19},{11,27},{4,20},{... | collective-permute-start | bytes 602120 | tf_op jit(solution)/shard_map/ppermute | solution.py:204
  213.9 1.5 collective-permute-start.8
  215.4 6.7 %shard_map.73.local_ref = f32[1024,768]{1,0:T(8,128)} custom-call(bf16[1024,2304]{1,0:T(8,128)(2,1)} %multiply_convert_fusion.q_ref.k_ref.v_ref, bf16[1024,2304]{1,0:T(8,128)(2,1)} %multiply_convert_fusion.q_ref.k_ref.v_ref, bf16[1024,2304]{1,0:T(8,128)(2,1)} %multiply_convert_fusion.q_ref.k_ref.v_ref, s32[2,512,1]{2,1,0:T(8,128)} %copy.23.dcol_ref, ...), custom_call_target="tpu_custom_call" | custom-call | tf_op jit(solution)/shard_map/pallas_call | solution.py:98
  222.2 0.7 copy-done.2
  222.9 0.1 copy-done.4
  223.0 4.4 %shard_map.75 = f32[1024,768]{1,0:T(8,128)} custom-call(f32[1024,768]{1,0:T(8,128)} %shard_map.73.local_ref, bf16[1024,2304]{1,0:T(8,128)(2,1)} %multiply_convert_fusion.q_ref.k_ref.v_ref, f32[2,5,1,128]{3,2,1,0:T(1,128)} %broadcast_in_dim.2.counted_ref, s32[2,512,1]{2,1,0:T(8,128)} %copy.23.dcol_ref, ...), custom_call_target="tpu_custom_call", output_to_operand_aliasing={{}: (0, {})} | custom-call | tf_op jit(solution)/shard_map/pallas_call | solution.py:135
  227.5 2.3 multiply_reduce_fusion.1
  229.9 0.1 dynamic_slice.27
  230.0 1.1 collective-permute-done.9
  231.0 0.1 rev.7
  231.2 0.3 multiply_convert_fusion.2
  231.5 0.1 fusion.6
  231.6 0.2 collective-permute-start.10
  231.8 2.1 collective-permute-done.10
  234.0 1.5 maximum_select_fusion.1
  (32 shorter events, 0.5 us)
Async XLA Ops:
  6.5 5.2 %copy-start.5 = (f32[3072]{0:T(1024)S(1)}, f32[3072]{0:T(1024)}, u32[]{:S(2)}) copy-start(f32[3072]{0:T(1024)} %param.9) | copy-start | bytes 36868
  6.5 174.8 %all-gather.3.cloned.1.call-start = ((), (), s32[]{:S(2)}) async-start(), calls=%async_computation | async-start | bytes 15040512 | tf_op jit(solution)/shard_map/all_gather | solution.py:193
  8.8 1.9 collective-permute-start.5
  16.6 1.7 copy-start.1
  16.6 2.1 copy-start.6
  18.3 20.1 %collective-permute-start = (bf16[512,3072]{0,1:T(8,128)(2,1)S(1)}, bf16[512,3072]{0,1:T(8,128)(2,1)}, u32[]{:S(2)}, u32[]{:S(2)}) collective-permute-start(bf16[512,3072]{0,1:T(8,128)(2,1)S(1)} %bitcast.29), channel_id=1, source_target_pairs={{0,4},{4,0},{1,5},{5,1},{2,6},{6,2},{3,7},{7,3},{8,12},{12,8},{9,1... | collective-permute-start | bytes 9437192 | tf_op jit(solution)/shard_map/ppermute | solution.py:21
  18.7 4.6 %collective-permute-start.1 = (s32[512]{0:T(512)S(1)}, s32[512]{0:T(512)S(1)}, u32[]{:S(2)}, u32[]{:S(2)}) collective-permute-start(s32[512]{0:T(512)S(1)} %bitcast.33), channel_id=1, source_target_pairs={{0,4},{4,0},{1,5},{5,1},{2,6},{6,2},{3,7},{7,3},{8,12},{12,8},{9,1... | collective-permute-start | bytes 6152 | tf_op jit(solution)/shard_map/ppermute | solution.py:21
  24.1 12.1 %collective-permute-start.4 = (s32[]{:T(128)}, s32[]{:T(128)}, u32[]{:S(2)}, u32[]{:S(2)}) collective-permute-start(s32[]{:T(128)} %get-tuple-element.14), channel_id=1, source_target_pairs={{0,24},{1,25},{2,26},{3,27},{4,28},{5,29},{6,30},{7,31}} | collective-permute-start | bytes 20 | tf_op jit(solution)/shard_map/ppermute | solution.py:166
  30.1 6.1 %collective-permute-start.3 = (s32[]{:T(128)}, s32[]{:T(128)}, u32[]{:S(2)}, u32[]{:S(2)}) collective-permute-start(s32[]{:T(128)} %get-tuple-element.14), channel_id=1, source_target_pairs={{0,16},{8,24},{1,17},{9,25},{2,18},{10,26},{3,19},{11,27},{4,20},{... | collective-permute-start | bytes 20 | tf_op jit(solution)/shard_map/ppermute | solution.py:166
  31.9 4.3 %collective-permute-start.2 = (s32[]{:T(128)}, s32[]{:T(128)}, u32[]{:S(2)}, u32[]{:S(2)}) collective-permute-start(s32[]{:T(128)} %get-tuple-element.14), channel_id=1, source_target_pairs={{0,8},{8,16},{16,24},{1,9},{9,17},{17,25},{2,10},{10,18},{18,26},{... | collective-permute-start | bytes 20 | tf_op jit(solution)/shard_map/ppermute | solution.py:166
  208.0 14.1 %collective-permute-start.6 = (bf16[1,784,128]{2,1,0:T(8,128)(2,1)}, bf16[1,784,128]{2,1,0:T(8,128)(2,1)S(1)}, u32[]{:S(2)}, u32[]{:S(2)}) collective-permute-start(bf16[1,784,128]{2,1,0:T(8,128)(2,1)} %get-tuple-element.12), channel_id=1, source_target_pairs={{0,8},{8,16},{16,24},{1,9},{9,17},{17,25},{2,10},{10,18},{18,26},{... | collective-permute-start | bytes 602120 | tf_op jit(solution)/shard_map/ppermute | solution.py:204
  211.4 10.7 %collective-permute-start.7 = (bf16[1,784,128]{2,1,0:T(8,128)(2,1)}, bf16[1,784,128]{2,1,0:T(8,128)(2,1)S(1)}, u32[]{:S(2)}, u32[]{:S(2)}) collective-permute-start(bf16[1,784,128]{2,1,0:T(8,128)(2,1)} %get-tuple-element.12), channel_id=1, source_target_pairs={{0,16},{8,24},{1,17},{9,25},{2,18},{10,26},{3,19},{11,27},{4,20},{... | collective-permute-start | bytes 602120 | tf_op jit(solution)/shard_map/ppermute | solution.py:204
  213.9 8.3 %collective-permute-start.8 = (bf16[1,784,128]{2,1,0:T(8,128)(2,1)}, bf16[1,784,128]{2,1,0:T(8,128)(2,1)S(1)}, u32[]{:S(2)}, u32[]{:S(2)}) collective-permute-start(bf16[1,784,128]{2,1,0:T(8,128)(2,1)} %get-tuple-element.12), channel_id=1, source_target_pairs={{0,24},{1,25},{2,26},{3,27},{4,28},{5,29},{6,30},{7,31}} | collective-permute-start | bytes 602120 | tf_op jit(solution)/shard_map/ppermute | solution.py:204
  222.1 0.7 copy-start.2
  222.1 0.8 copy-start.3
  222.2 0.8 copy-start.4
  227.5 2.4 copy-start.7
  227.5 3.7 %copy-start = (f32[1024,768]{1,0:T(8,128)S(1)}, f32[1024,768]{1,0:T(8,128)}, u32[]{:S(2)}) copy-start(f32[1024,768]{1,0:T(8,128)} %shard_map.75) | copy-start | bytes 9437188
  229.8 1.2 collective-permute-start.9
  231.6 2.4 collective-permute-start.10
Sparse Core Ops, SparseCore 0:
  11.8 169.4 all-gather.2
